TPU v7x, 256 devices: a whole 4x4x8 slice. The times are simulated.
256 devices in a mesh: dp: 32 (over x, y, core), head: 8 (over z).
Axes of the slice: x: 4, y: 4, z: 8, core: 2. Of those that a mesh axis runs over, the one named last changes fastest.
Arguments:
- hidden: bfloat16 [16384, 2048], P('dp'), may hold values from -9 to 9
- parents: int32 [256, 64], P('dp'), may hold values from -1 to 62, as said below
- owner_slot: int32 [256], replicated, may hold values from 0 to 255, as said below
- slot_lengths: int32 [256], P('dp'), may hold values from 65 to 496, as said below
- accepted_path: int32 [256, 16], P('dp'), may hold values from 0 to 63, as said below
- accepted_count: int32 [256], P('dp'), may hold values from 1 to 16, as said below
- cache_keys: bfloat16 [256, 512, 2048], P('dp', None, 'head'), may hold values from -82 to 82
- cache_values: bfloat16 [256, 512, 2048], P('dp', None, 'head'), may hold values from -5 to 5
- w_query: bfloat16 [2048, 2048], P(None, 'head'), may hold values from -0.125 to 0.125
- b_query: float32 [2048], P('head'), may hold values from -3 to 3
- w_key: bfloat16 [2048, 2048], P(None, 'head'), may hold values from -0.25 to 0.25
- w_value: bfloat16 [2048, 2048], P(None, 'head'), may hold values from -0.125 to 0.125
- b_value: float32 [2048], P('head'), may hold values from -3 to 3
- w_out: bfloat16 [2048, 2048], P('head'), may hold values from -0.5 to 0.5
- b_out: float32 [2048], replicated, may hold values from -3 to 3
- first_gain: float32 [2048], replicated, may hold values from 0.48 to 2.25
- first_shift: float32 [2048], replicated, may hold values from -2 to 2
- w_up: bfloat16 [2048, 4096], P(None, 'head'), may hold values from -0.125 to 0.125
- b_up: float32 [4096], P('head'), may hold values from -3 to 3
- w_down: bfloat16 [4096, 2048], P('head'), may hold values from -0.09375 to 0.09375
- b_down: float32 [2048], replicated, may hold values from -3 to 3
- second_gain: float32 [2048], replicated, may hold values from 0.5 to 1.5
- second_shift: float32 [2048], replicated, may hold values from -2 to 2
Outputs:
- layer_out: bfloat16 [16384, 2048], P('dp', 'head')
- new_keys: bfloat16 [256, 16, 2048], P('dp', None, 'head')
- new_values: bfloat16 [256, 16, 2048], P('dp', None, 'head')
Inputs may be any that keep to these rules, and one draw needn't show every extreme that they name: owner_slot is a permutation of the 256 slots; slot s lies on dp index s // 8. Of the 8 requests of one dp index, at most 2 have their slots on one dp index, and on every dp index some 2 do. `slot_lengths`: some slot is filled to exactly 496 positions. parents[r, 0] = -1 and 0 <= parents[r, i] < i for i >= 1. For k < accepted_count[r], accepted_path[r, k] is the node at depth k on the way from the root to some node of request r's tree (so entry 0 is node 0); later entries are arbitrary node indices. `accepted_count`: some request has the full 16 entries.
All inputs are finite; a program needn't handle non-finite values.
Results may differ from a plain program's by a relative error of at most 0.018.
Values may be sent and summed in bfloat16 or wider, within the bound.
No kernel may reach another device: no remote copies, remote signals or barrier semaphores. Data moves between devices by JAX's collectives and lax.ppermute only.
A program may use at most 64 MiB of HBM per device.

v0:
```python
import math

import jax
import jax.numpy as jnp
from jax import lax
from jax.sharding import PartitionSpec as P

HD = 128
PEER_MOST = 2


EPSILON = 1e-05


def for_sending(shard):

    def short(part):
        return part.astype(jnp.bfloat16) if part.dtype == jnp.float32 else part

    return jax.tree.map(short, shard)


def ancestry(parent_row, draft):
    nodes = jnp.arange(draft, dtype=jnp.int32)
    reach = (parent_row[:, None] == nodes[None, :]).astype(jnp.float32) + jnp.eye(
        draft, dtype=jnp.float32
    )
    for turn in range(max(1, draft.bit_length())):
        reach = jnp.minimum(jnp.dot(reach, reach, precision=lax.Precision.HIGHEST), 1.0)
    return reach > 0.5


def normalize(mixed, gain, shift):
    center = jnp.mean(mixed, axis=-1, keepdims=True)
    square = jnp.mean(mixed * mixed, axis=-1, keepdims=True)
    return (mixed - center) * lax.rsqrt(square - center * center + EPSILON) * gain + shift


def normalize_shared(mixed, sums, gain, shift, model_width):
    center = (sums[0] / model_width)[:, None]
    square = (sums[1] / model_width)[:, None]
    return (mixed - center) * lax.rsqrt(square - center * center + EPSILON) * gain + shift


def score_block(query_heads, key_block):
    return jnp.einsum("qhd,khd->hqk", query_heads, key_block, preferred_element_type=jnp.float32)


def silent_scores(query_heads, key_block):
    return jnp.full(
        (query_heads.shape[1], query_heads.shape[0], key_block.shape[0]), -jnp.inf, jnp.float32
    )


def mix_block(probs_block, value_block):
    return jnp.einsum("hqk,khd->qhd", probs_block, value_block, preferred_element_type=jnp.float32)


def silent_mix(probs_block, value_block):
    return jnp.zeros(
        (probs_block.shape[1], probs_block.shape[0], value_block.shape[2]), jnp.float32
    )


def split_three(values):
    high = values.astype(jnp.bfloat16)
    rest = values - high.astype(jnp.float32)
    middle = rest.astype(jnp.bfloat16)
    low = (rest - middle.astype(jnp.float32)).astype(jnp.bfloat16)
    return jnp.stack([high, middle, low], axis=1)


def join_three(pieces):
    wide = pieces.astype(jnp.float32)
    return wide[:, 0] + (wide[:, 1] + wide[:, 2])


def local(
    hidden,
    parents,
    owner_slot,
    slot_lengths,
    accepted_path,
    accepted_count,
    cache_keys,
    cache_values,
    w_query,
    b_query,
    w_key,
    w_value,
    b_value,
    w_out,
    b_out,
    first_gain,
    first_shift,
    w_up,
    b_up,
    w_down,
    b_down,
    second_gain,
    second_shift,
):
    requests = parents.shape[0]
    draft = parents.shape[1]
    tokens = hidden.shape[0]
    model_width = hidden.shape[1]
    width = w_query.shape[1]
    local_heads = width // HD
    capacity = cache_keys.shape[1]
    block = min(capacity, 256)
    shards = lax.axis_size("dp")
    myself = lax.axis_index("dp")
    scale = 1.0 / math.sqrt(HD)
    queries = (jnp.dot(hidden, w_query, preferred_element_type=jnp.float32) + b_query).astype(
        jnp.bfloat16
    )
    key_rows = jnp.dot(hidden, w_key, preferred_element_type=jnp.float32).astype(jnp.bfloat16)
    value_rows = (jnp.dot(hidden, w_value, preferred_element_type=jnp.float32) + b_value).astype(
        jnp.bfloat16
    )
    local_ids = jnp.arange(requests, dtype=jnp.int32)
    levels = jnp.arange(accepted_path.shape[1], dtype=jnp.int32)
    chosen = local_ids[:, None] * draft + accepted_path
    usable = (levels[None, :] < accepted_count[:, None])[..., None]
    kept_keys = jnp.where(usable, key_rows[chosen], jnp.zeros((), jnp.bfloat16))
    kept_values = jnp.where(usable, value_rows[chosen], jnp.zeros((), jnp.bfloat16))
    tree_queries = queries.reshape(requests, draft, local_heads, HD)
    tree_keys = key_rows.reshape(requests, draft, local_heads, HD)
    tree_values = value_rows.reshape(requests, draft, local_heads, HD)
    lineage = jax.vmap(lambda parent_row: ancestry(parent_row, draft))(parents)
    tree_scores = (
        jnp.einsum("rqhd,rkhd->rhqk", tree_queries, tree_keys, preferred_element_type=jnp.float32)
        * scale
    )
    tree_scores = jnp.where(lineage[:, None], tree_scores, -jnp.inf)
    tree_top = jnp.max(tree_scores, axis=3, keepdims=True)
    tree_exp = jnp.exp(tree_scores - tree_top)
    tree_total = jnp.sum(tree_exp, axis=3, keepdims=True)
    tree_probs = tree_exp.astype(jnp.bfloat16)
    tree_part = jnp.einsum(
        "rhqk,rkhd->rqhd", tree_probs, tree_values, preferred_element_type=jnp.float32
    ) / jnp.transpose(tree_total, (0, 2, 1, 3))
    tree_lse = jnp.transpose((tree_top + jnp.log(tree_total))[..., 0], (0, 2, 1))[..., None]
    my_owner = lax.dynamic_slice_in_dim(owner_slot, myself * requests, requests)
    target = my_owner // requests
    earlier = local_ids[None, :] < local_ids[:, None]
    same_target = target[None, :] == target[:, None]
    rank = jnp.sum((earlier & same_target).astype(jnp.int32), axis=1)
    my_slots = myself * requests + local_ids
    every_id = jnp.arange(owner_slot.shape[0], dtype=jnp.int32)
    source_request = jnp.sum(
        jnp.where(owner_slot[None, :] == my_slots[:, None], every_id[None, :], 0), axis=1
    )
    source = source_request // requests
    source_local = source_request % requests
    source_targets = owner_slot.reshape(shards, requests)[source] // requests
    source_rank = jnp.sum(
        ((local_ids[None, :] < source_local[:, None]) & (source_targets == myself)).astype(
            jnp.int32
        ),
        axis=1,
    )

    def attend_slot(operands):
        query_slot, keys_slot, values_slot, length = operands
        query_heads = query_slot.reshape(draft, local_heads, HD)
        pieces = []
        for begin in range(0, capacity, block):
            key_block = keys_slot[begin : begin + block].reshape(block, local_heads, HD)
            pieces.append(
                lax.cond(begin < length, score_block, silent_scores, query_heads, key_block)
            )
        scores = jnp.concatenate(pieces, axis=2) * scale
        living = jnp.arange(capacity, dtype=jnp.int32) < length
        scores = jnp.where(living[None, None, :], scores, -jnp.inf)
        cache_top = jnp.max(scores, axis=2, keepdims=True)
        cache_exp = jnp.exp(scores - cache_top)
        cache_total = jnp.sum(cache_exp, axis=2, keepdims=True)
        cache_probs = cache_exp.astype(jnp.bfloat16)
        gathered = jnp.zeros((draft, local_heads, HD), jnp.float32)
        for begin in range(0, capacity, block):
            value_block = values_slot[begin : begin + block].reshape(block, local_heads, HD)
            gathered = gathered + lax.cond(
                begin < length,
                mix_block,
                silent_mix,
                cache_probs[:, :, begin : begin + block],
                value_block,
            )
        cache_part = (
            (gathered / jnp.transpose(cache_total, (1, 0, 2)))
            .astype(jnp.bfloat16)
            .reshape(draft, width)
        )
        cache_lse = (cache_top + jnp.log(cache_total))[..., 0]
        return (cache_part, cache_lse)

    shaped_queries = queries.reshape(requests, draft, width)
    slots_total = shards * PEER_MOST
    send_index = target * PEER_MOST + rank
    receive_index = source * PEER_MOST + source_rank

    def spread(values, index):
        holder = jnp.zeros((slots_total,) + values.shape[1:], values.dtype)
        return holder.at[index].set(values)

    arrived = (
        lax.all_to_all(
            spread(shaped_queries, send_index), "dp", split_axis=0, concat_axis=0, tiled=True
        ),
        lax.all_to_all(
            spread(kept_keys, send_index), "dp", split_axis=0, concat_axis=0, tiled=True
        ),
        lax.all_to_all(
            spread(kept_values, send_index), "dp", split_axis=0, concat_axis=0, tiled=True
        ),
    )
    owned_queries = arrived[0][receive_index]
    new_keys = arrived[1][receive_index]
    new_values = arrived[2][receive_index]
    owned_part, owned_lse = lax.map(
        attend_slot, (owned_queries, cache_keys, cache_values, slot_lengths)
    )
    returned = (
        lax.all_to_all(
            spread(owned_part, receive_index), "dp", split_axis=0, concat_axis=0, tiled=True
        ),
        lax.all_to_all(
            for_sending(spread(split_three(owned_lse), receive_index)),
            "dp",
            split_axis=0,
            concat_axis=0,
            tiled=True,
        ),
    )
    cache_part = returned[0][send_index]
    cache_lse = join_three(returned[1][send_index])
    cache_weight = jnp.transpose(cache_lse, (0, 2, 1))[..., None]
    larger = jnp.maximum(cache_weight, tree_lse)
    cache_share = jnp.exp(cache_weight - larger)
    tree_share = jnp.exp(tree_lse - larger)
    blended = (
        cache_share * cache_part.astype(jnp.float32).reshape(requests, draft, local_heads, HD)
        + tree_share * tree_part
    ) / (cache_share + tree_share)
    attended = blended.astype(jnp.bfloat16).reshape(tokens, width)
    attention_term = jnp.dot(attended, w_out, preferred_element_type=jnp.float32)
    feature = model_width // lax.axis_size("head")
    offset = lax.axis_index("head") * feature

    def columns(values):
        return lax.dynamic_slice_in_dim(values, offset, feature, values.ndim - 1)

    attention_sum = lax.psum(attention_term.astype(jnp.bfloat16), "head").astype(jnp.float32)
    first_normed = normalize(
        attention_sum + b_out + hidden.astype(jnp.float32), first_gain, first_shift
    ).astype(jnp.bfloat16)
    inner = jax.nn.gelu(
        jnp.dot(first_normed, w_up, preferred_element_type=jnp.float32) + b_up, approximate=True
    ).astype(jnp.bfloat16)
    down_share = lax.psum_scatter(
        jnp.dot(inner, w_down, preferred_element_type=jnp.float32).astype(jnp.bfloat16),
        "head",
        scatter_dimension=1,
        tiled=True,
    ).astype(jnp.float32)
    second_mixed = down_share + columns(b_down) + columns(first_normed).astype(jnp.float32)
    second_sums = lax.psum(
        (jnp.sum(second_mixed, axis=1), jnp.sum(second_mixed * second_mixed, axis=1)), "head"
    )
    layer_out = normalize_shared(
        second_mixed, second_sums, columns(second_gain), columns(second_shift), model_width
    ).astype(jnp.bfloat16)
    return (layer_out, new_keys, new_values)


def solution(mesh):
    placed = (
        P("dp", None),
        P("dp", None),
        P(),
        P("dp"),
        P("dp", None),
        P("dp"),
        P("dp", None, "head"),
        P("dp", None, "head"),
        P(None, "head"),
        P("head"),
        P(None, "head"),
        P(None, "head"),
        P("head"),
        P("head", None),
        P(),
        P(),
        P(),
        P(None, "head"),
        P("head"),
        P("head", None),
        P(),
        P(),
        P(),
    )
    return jax.shard_map(
        local,
        mesh=mesh,
        in_specs=placed,
        out_specs=(P("dp", "head"), P("dp", None, "head"), P("dp", None, "head")),
        check_vma=False,
    )
```

profile of v0, /device:TPU:2, one launch (start us, length us, event | category | flops | bytes accessed | tf_op | source)
XLA Modules:
  0.0 318.7 jit_solution(12774422311021160430)
XLA Ops:
  9.0 2.6 fusion.16
  13.2 2.2 scatter_fusion
  15.4 7.8 %all-to-all-start = ((bf16[64,64,256]{2,1,0:T(8,128)(2,1)}), bf16[64,64,256]{2,1,0:T(8,128)(2,1)}, u32[]{:S(2)}, u32[]{:S(2)}) async-start(bf16[64,64,256]{2,1,0:T(8,128)(2,1)} %scatter_fusion), calls=%async_computation | async-start | bytes 4194304 | tf_op jit(solution)/shard_map/all_to_all | solution.py:208
  24.9 2.6 convolution_convert_fusion.2
  27.5 21.8 %all-to-all-done = bf16[64,64,256]{2,1,0:T(8,128)(2,1)} async-done(((bf16[64,64,256]{2,1,0:T(8,128)(2,1)}), bf16[64,64,256]{2,1,0:T(8,128)(2,1)}, u32[]{:S(2)}, u32[]{:S(2)}) %all-to-all-start) | async-done | bytes 2097184 | tf_op jit(solution)/shard_map/all_to_all | solution.py:208
  49.2 2.9 gather_fusion.1
  52.1 51.4 %while.12 = (s32[]{:T(128)}, bf16[8,64,256]{2,1,0:T(8,128)(2,1)}, f32[8,2,64]{2,1,0:T(2,128)S(1)}, s32[8]{0:T(128)S(1)}, bf16[8,512,256]{2,1,0:T(8,128)(2,1)}, /...) while((s32[]{:T(128)}, bf16[8,64,256]{2,1,0:T(8,128)(2,1)}, ...), condition=%wide.region_15.16_spmd, body=%wide.region_4.15_spmd.sunk | while | flops 34259332 | bytes 5414109 | solution.py:221
  105.1 6.8 %all-to-all-start.1 = ((bf16[32,2,384]{2,1,0:T(2,128)(2,1)}), bf16[32,2,384]{2,1,0:T(2,128)(2,1)S(1)}, u32[]{:S(2)}, u32[]{:S(2)}) async-start(bf16[32,2,384]{2,1,0:T(2,128)(2,1)} %reshape.390), calls=%async_computation.1 | async-start | bytes 98304 | tf_op jit(solution)/shard_map/all_to_all | solution.py:228
  113.9 2.2 scatter_fusion.2
  116.0 2.2 all-to-all-done.1
  118.3 5.8 %all-to-all-start.2 = ((bf16[64,64,256]{2,1,0:T(8,128)(2,1)}), bf16[64,64,256]{2,1,0:T(8,128)(2,1)}, u32[]{:S(2)}, u32[]{:S(2)}) async-start(bf16[64,64,256]{2,1,0:T(8,128)(2,1)} %scatter_fusion.2), calls=%async_computation.2 | async-start | bytes 4194304 | tf_op jit(solution)/shard_map/all_to_all | solution.py:225
  127.2 2.6 fusion.17
  132.6 17.5 %all-to-all-done.2 = bf16[64,64,256]{2,1,0:T(8,128)(2,1)} async-done(((bf16[64,64,256]{2,1,0:T(8,128)(2,1)}), bf16[64,64,256]{2,1,0:T(8,128)(2,1)}, u32[]{:S(2)}, u32[]{:S(2)}) %all-to-all-start.2) | async-done | bytes 2097184 | tf_op jit(solution)/shard_map/all_to_all | solution.py:225
  150.1 2.2 gather_fusion.3
  154.3 2.0 convolution_convert_fusion
  156.6 83.2 %all-reduce.3.cloned.1.call-done = bf16[512,2048]{1,0:T(8,128)(2,1)} async-done(((bf16[512,2048]{1,0:T(8,128)(2,1)}), bf16[512,2048]{1,0:T(8,128)(2,1)}) %all-reduce.3.cloned.1.call-update) | async-done | bytes 2097168 | tf_op jit(solution)/shard_map/psum | solution.py:254
  239.9 3.5 %fusion.10 = (f32[512]{0:T(512)S(1)}, f32[512]{0:T(512)S(1)}) fusion(bf16[512,2048]{1,0:T(8,128)(2,1)} %param.33, bf16[512,2048]{1,0:T(8,128)(2,1)} %all-reduce.3.cloned.1.call-done, f32[2048]{0:T(1024)S(1)} %copy-done.7), kind=kLoop, calls=%fused_computation.37 | loop fusion | flops 7339008 | bytes 4206592 | tf_op jit(solution)/shard_map/reduce_sum | solution.py:34
  243.4 2.6 add_convert_fusion
  246.0 6.1 %convolution_convert_fusion.1 = bf16[512,2048]{1,0:T(8,128)(2,1)} fusion(bf16[512,2048]{1,0:T(8,128)(2,1)S(1)} %copy-done, bf16[512,2048]{1,0:T(8,128)(2,1)} %add_convert_fusion, bf16[2048,512]{1,0:T(8,128)(2,1)} %param.50, f32[512]{0:T(512)S(1)} %copy-done.13), kind=kOutput, calls=%fused_computation.39 | convolution fusion | flops 2151153664 | bytes 8390656 | tf_op jit(solution)/shard_map/dot_general | solution.py:262
  257.6 7.4 %all-to-all-start.3 = ((bf16[64,16,256]{2,1,0:T(8,128)(2,1)}), bf16[64,16,256]{2,1,0:T(8,128)(2,1)S(1)}, u32[]{:S(2)}, u32[]{:S(2)}) async-start(bf16[64,16,256]{2,1,0:T(8,128)(2,1)} %scatter_fusion.3), calls=%async_computation.4 | async-start | bytes 1048576 | tf_op jit(solution)/shard_map/all_to_all | solution.py:211
  267.9 6.8 %all-to-all-done.3 = bf16[64,16,256]{2,1,0:T(8,128)(2,1)S(1)} async-done(((bf16[64,16,256]{2,1,0:T(8,128)(2,1)}), bf16[64,16,256]{2,1,0:T(8,128)(2,1)S(1)}, u32[]{:S(2)}, u32[]{:S(2)}) %all-to-all-start.3) | async-done | bytes 524320 | tf_op jit(solution)/shard_map/all_to_all | solution.py:211
  274.8 5.6 %all-to-all-start.4 = ((bf16[64,16,256]{2,1,0:T(8,128)(2,1)}), bf16[64,16,256]{2,1,0:T(8,128)(2,1)S(1)}, u32[]{:S(2)}, u32[]{:S(2)}) async-start(bf16[64,16,256]{2,1,0:T(8,128)(2,1)} %scatter_fusion.4), calls=%async_computation.5 | async-start | bytes 1048576 | tf_op jit(solution)/shard_map/all_to_all | solution.py:214
  283.8 6.2 %all-to-all-done.4 = bf16[64,16,256]{2,1,0:T(8,128)(2,1)S(1)} async-done(((bf16[64,16,256]{2,1,0:T(8,128)(2,1)}), bf16[64,16,256]{2,1,0:T(8,128)(2,1)S(1)}, u32[]{:S(2)}, u32[]{:S(2)}) %all-to-all-start.4) | async-done | bytes 524320 | tf_op jit(solution)/shard_map/all_to_all | solution.py:214
  294.3 15.6 %all-reduce = (f32[512]{0:T(512)S(1)}, f32[512]{0:T(512)S(1)}) all-reduce(f32[512]{0:T(512)S(1)} %get-tuple-element.114, f32[512]{0:T(512)S(1)} %get-tuple-element.113), channel_id=1, replica_groups=mesh['dp'=32,'head'=8] {'head'}, use_global_device_ids=true, to_apply=%region_27.28 | all-reduce | flops 1024 | bytes 8192 | tf_op jit(solution)/shard_map/psum | solution.py:268
  (302 shorter events, 78.7 us)
Async XLA Ops:
  7.2 238.8 %copy-start = (bf16[512,2048]{1,0:T(8,128)(2,1)S(1)}, bf16[512,2048]{1,0:T(8,128)(2,1)}, u32[]{:S(2)}) copy-start(bf16[512,2048]{1,0:T(8,128)(2,1)} %param.52) | copy-start | bytes 6291460
  11.7 3.8 %copy-start.4 = (bf16[512,256]{1,0:T(8,128)(2,1)}, bf16[512,256]{1,0:T(8,128)(2,1)S(1)}, u32[]{:S(2)}) copy-start(bf16[512,256]{1,0:T(8,128)(2,1)S(1)} %fusion.16) | copy-start | bytes 786436
  15.4 7.8 %copy-start.10 = (s32[256]{0:T(256)S(1)}, s32[256]{0:T(256)}, u32[]{:S(2)}) copy-start(s32[256]{0:T(256)} %param.35) | copy-start | bytes 3076
  15.4 8.9 %copy-start.11 = (s32[8,64]{1,0:T(8,128)S(1)}, s32[8,64]{1,0:T(8,128)}, u32[]{:S(2)}) copy-start(s32[8,64]{1,0:T(8,128)} %param.34) | copy-start | bytes 6148
  15.4 33.8 %all-to-all-start = ((bf16[64,64,256]{2,1,0:T(8,128)(2,1)}), bf16[64,64,256]{2,1,0:T(8,128)(2,1)}, u32[]{:S(2)}, u32[]{:S(2)}) async-start(bf16[64,64,256]{2,1,0:T(8,128)(2,1)} %scatter_fusion), calls=%async_computation | async-start | bytes 4194304 | tf_op jit(solution)/shard_map/all_to_all | solution.py:208
  24.9 27.2 %copy-start.15 = (s32[8]{0:T(128)S(1)}, s32[8]{0:T(128)}, u32[]{:S(2)}) copy-start(s32[8]{0:T(128)} %param.36) | copy-start | bytes 100
  103.5 10.4 %copy-start.6 = (bf16[8,64,256]{2,1,0:T(8,128)(2,1)S(1)}, bf16[8,64,256]{2,1,0:T(8,128)(2,1)}, u32[]{:S(2)}) copy-start(bf16[8,64,256]{2,1,0:T(8,128)(2,1)} %get-tuple-element.88) | copy-start | bytes 786436
  105.1 13.1 %all-to-all-start.1 = ((bf16[32,2,384]{2,1,0:T(2,128)(2,1)}), bf16[32,2,384]{2,1,0:T(2,128)(2,1)S(1)}, u32[]{:S(2)}, u32[]{:S(2)}) async-start(bf16[32,2,384]{2,1,0:T(2,128)(2,1)} %reshape.390), calls=%async_computation.1 | async-start | bytes 98304 | tf_op jit(solution)/shard_map/all_to_all | solution.py:228
  116.0 8.5 %copy-start.5 = (bf16[512,256]{1,0:T(8,128)(2,1)S(1)}, bf16[512,256]{1,0:T(8,128)(2,1)}, u32[]{:S(2)}) copy-start(bf16[512,256]{1,0:T(8,128)(2,1)} %copy-done.4) | copy-start | bytes 786436
  118.3 31.8 %all-to-all-start.2 = ((bf16[64,64,256]{2,1,0:T(8,128)(2,1)}), bf16[64,64,256]{2,1,0:T(8,128)(2,1)}, u32[]{:S(2)}, u32[]{:S(2)}) async-start(bf16[64,64,256]{2,1,0:T(8,128)(2,1)} %scatter_fusion.2), calls=%async_computation.2 | async-start | bytes 4194304 | tf_op jit(solution)/shard_map/all_to_all | solution.py:225
  124.1 115.8 %all-reduce.3.cloned.1.call-start = ((), (), s32[]{:S(2)}) async-start(), calls=%async_computation.6 | async-start | bytes 4194304 | tf_op jit(solution)/shard_map/psum | solution.py:254
  124.5 2.6 copy-start.14
  152.2 2.1 copy-start.3
  154.3 85.6 %copy-start.7 = (f32[2048]{0:T(1024)S(1)}, f32[2048]{0:T(1024)}, u32[]{:S(2)}) copy-start(f32[2048]{0:T(1024)} %param.47) | copy-start | bytes 24580
  156.4 87.0 %copy-start.8 = (f32[2048]{0:T(1024)S(1)}, f32[2048]{0:T(1024)}, u32[]{:S(2)}) copy-start(f32[2048]{0:T(1024)} %param.49) | copy-start | bytes 24580
  156.4 87.0 %copy-start.9 = (f32[2048]{0:T(1024)S(1)}, f32[2048]{0:T(1024)}, u32[]{:S(2)}) copy-start(f32[2048]{0:T(1024)} %param.48) | copy-start | bytes 24580
  156.4 136.7 %reduce-scatter.2.cloned.1.call-start = ((), (), s32[]{:S(2)}) async-start(), calls=%async_computation.7 | async-start | bytes 2359296 | tf_op jit(solution)/shard_map/reduce_scatter | solution.py:261
  239.9 3.5 %copy-start.1 = (bf16[512,2048]{1,0:T(8,128)(2,1)S(1)}, bf16[512,2048]{1,0:T(8,128)(2,1)}, u32[]{:S(2)}) copy-start(bf16[512,2048]{1,0:T(8,128)(2,1)} %param.33) | copy-start | bytes 6291460
  239.9 3.5 %copy-start.2 = (bf16[512,2048]{1,0:T(8,128)(2,1)S(1)}, bf16[512,2048]{1,0:T(8,128)(2,1)}, u32[]{:S(2)}) copy-start(bf16[512,2048]{1,0:T(8,128)(2,1)} %all-reduce.3.cloned.1.call-done) | copy-start | bytes 6291460
  243.4 2.6 copy-start.13
  252.1 0.7 copy-start.12
  252.1 2.6 copy-start.16
  257.6 17.1 %all-to-all-start.3 = ((bf16[64,16,256]{2,1,0:T(8,128)(2,1)}), bf16[64,16,256]{2,1,0:T(8,128)(2,1)S(1)}, u32[]{:S(2)}, u32[]{:S(2)}) async-start(bf16[64,16,256]{2,1,0:T(8,128)(2,1)} %scatter_fusion.3), calls=%async_computation.4 | async-start | bytes 1048576 | tf_op jit(solution)/shard_map/all_to_all | solution.py:211
  274.8 15.3 %all-to-all-start.4 = ((bf16[64,16,256]{2,1,0:T(8,128)(2,1)}), bf16[64,16,256]{2,1,0:T(8,128)(2,1)S(1)}, u32[]{:S(2)}, u32[]{:S(2)}) async-start(bf16[64,16,256]{2,1,0:T(8,128)(2,1)} %scatter_fusion.4), calls=%async_computation.5 | async-start | bytes 1048576 | tf_op jit(solution)/shard_map/all_to_all | solution.py:214
Sparse Core Ops, SparseCore 0:
  156.5 83.3 all-reduce.2
  252.2 40.7 reduce-scatter.1
where the time goes:
time: 321 us; the launch traced here: 319 us
  waiting for transfers between devices  140 us (44%)
  local copies, waits for them, and re-layouts  57.7 us (18%)
  starting transfers between devices  33.6 us (10%)
  matrix products  25 us (8%)
  other arithmetic  20.7 us (6%)
  blocking collectives  15.6 us (5%)
  between operations  14.5 us (5%)
  loops' own time  11.9 us (4%)
    psum x1, waiting for transfers between devices, local(): lax.psum(attention_term.astype(jnp.bfloat16), 'head').astype(jnp.float32)  83.2 us
    all_to_all x1, waiting for transfers between devices, local(): lax.all_to_all(spread(shaped_queries, send_index), 'dp', split_axis=0, co...  21.8 us
    dynamic_slice x40, local copies, waits for them, and re-layouts, local(): lax.map(attend_slot, (owned_queries, cache_keys, cache_values, slot_lengt...  21.6 us
    all_to_all x1, waiting for transfers between devices, local(): lax.all_to_all(spread(owned_part, receive_index), 'dp', split_axis=0, con...  17.5 us
    psum x1, blocking collectives, local(): lax.psum((jnp.sum(second_mixed, axis=1), jnp.sum(second_mixed * second_mi...  15.6 us
    another operation x1, loops' own time, local(): lax.map(attend_slot, (owned_queries, cache_keys, cache_values, slot_lengt...  11.1 us
    scatter x5, local copies, waits for them, and re-layouts, spread(): return holder.at[index].set(values)  9.11 us
    all_to_all x1, starting transfers between devices, local(): lax.all_to_all(spread(shaped_queries, send_index), 'dp', split_axis=0, co...  7.8 us
  transfers between devices with their start and end apart: 7, of which 7 were waited for; matrix products, arithmetic and copies ran while one was open for 9% of the time, Pallas kernels for 0%

commit v1 on v0

--- a/solution.py
+++ b/solution.py
@@ -12,14 +12,6 @@
 EPSILON = 1e-05
 
 
-def for_sending(shard):
-
-    def short(part):
-        return part.astype(jnp.bfloat16) if part.dtype == jnp.float32 else part
-
-    return jax.tree.map(short, shard)
-
-
 def ancestry(parent_row, draft):
     nodes = jnp.arange(draft, dtype=jnp.int32)
     reach = (parent_row[:, None] == nodes[None, :]).astype(jnp.float32) + jnp.eye(
@@ -40,26 +32,6 @@
     center = (sums[0] / model_width)[:, None]
     square = (sums[1] / model_width)[:, None]
     return (mixed - center) * lax.rsqrt(square - center * center + EPSILON) * gain + shift
-
-
-def score_block(query_heads, key_block):
-    return jnp.einsum("qhd,khd->hqk", query_heads, key_block, preferred_element_type=jnp.float32)
-
-
-def silent_scores(query_heads, key_block):
-    return jnp.full(
-        (query_heads.shape[1], query_heads.shape[0], key_block.shape[0]), -jnp.inf, jnp.float32
-    )
-
-
-def mix_block(probs_block, value_block):
-    return jnp.einsum("hqk,khd->qhd", probs_block, value_block, preferred_element_type=jnp.float32)
-
-
-def silent_mix(probs_block, value_block):
-    return jnp.zeros(
-        (probs_block.shape[1], probs_block.shape[0], value_block.shape[2]), jnp.float32
-    )
 
 
 def split_three(values):
@@ -161,48 +133,19 @@
         axis=1,
     )
 
-    def attend_slot(operands):
-        query_slot, keys_slot, values_slot, length = operands
-        query_heads = query_slot.reshape(draft, local_heads, HD)
-        pieces = []
-        for begin in range(0, capacity, block):
-            key_block = keys_slot[begin : begin + block].reshape(block, local_heads, HD)
-            pieces.append(
-                lax.cond(begin < length, score_block, silent_scores, query_heads, key_block)
-            )
-        scores = jnp.concatenate(pieces, axis=2) * scale
-        living = jnp.arange(capacity, dtype=jnp.int32) < length
-        scores = jnp.where(living[None, None, :], scores, -jnp.inf)
-        cache_top = jnp.max(scores, axis=2, keepdims=True)
-        cache_exp = jnp.exp(scores - cache_top)
-        cache_total = jnp.sum(cache_exp, axis=2, keepdims=True)
-        cache_probs = cache_exp.astype(jnp.bfloat16)
-        gathered = jnp.zeros((draft, local_heads, HD), jnp.float32)
-        for begin in range(0, capacity, block):
-            value_block = values_slot[begin : begin + block].reshape(block, local_heads, HD)
-            gathered = gathered + lax.cond(
-                begin < length,
-                mix_block,
-                silent_mix,
-                cache_probs[:, :, begin : begin + block],
-                value_block,
-            )
-        cache_part = (
-            (gathered / jnp.transpose(cache_total, (1, 0, 2)))
-            .astype(jnp.bfloat16)
-            .reshape(draft, width)
-        )
-        cache_lse = (cache_top + jnp.log(cache_total))[..., 0]
-        return (cache_part, cache_lse)
-
     shaped_queries = queries.reshape(requests, draft, width)
     slots_total = shards * PEER_MOST
     send_index = target * PEER_MOST + rank
     receive_index = source * PEER_MOST + source_rank
+    slot_ids = jnp.arange(slots_total, dtype=jnp.int32)
 
     def spread(values, index):
-        holder = jnp.zeros((slots_total,) + values.shape[1:], values.dtype)
-        return holder.at[index].set(values)
+        match = index[None, :] == slot_ids[:, None]
+        filled = jnp.any(match, axis=1)
+        pick = jnp.sum(jnp.where(match, local_ids[None, :], 0), axis=1)
+        taken = values[pick]
+        shape = (slots_total,) + (1,) * (values.ndim - 1)
+        return jnp.where(filled.reshape(shape), taken, jnp.zeros((), values.dtype))
 
     arrived = (
         lax.all_to_all(
@@ -215,26 +158,44 @@
             spread(kept_values, send_index), "dp", split_axis=0, concat_axis=0, tiled=True
         ),
     )
-    owned_queries = arrived[0][receive_index]
+    owned_queries = arrived[0][receive_index].reshape(requests, draft, local_heads, HD)
     new_keys = arrived[1][receive_index]
     new_values = arrived[2][receive_index]
-    owned_part, owned_lse = lax.map(
-        attend_slot, (owned_queries, cache_keys, cache_values, slot_lengths)
-    )
-    returned = (
-        lax.all_to_all(
-            spread(owned_part, receive_index), "dp", split_axis=0, concat_axis=0, tiled=True
-        ),
-        lax.all_to_all(
-            for_sending(spread(split_three(owned_lse), receive_index)),
-            "dp",
-            split_axis=0,
-            concat_axis=0,
-            tiled=True,
-        ),
-    )
-    cache_part = returned[0][send_index]
-    cache_lse = join_three(returned[1][send_index])
+    slot_keys = cache_keys.reshape(requests, capacity, local_heads, HD)
+    slot_values = cache_values.reshape(requests, capacity, local_heads, HD)
+    scores = (
+        jnp.einsum(
+            "sqhd,skhd->shqk", owned_queries, slot_keys, preferred_element_type=jnp.float32
+        )
+        * scale
+    )
+    living = jnp.arange(capacity, dtype=jnp.int32)[None, :] < slot_lengths[:, None]
+    scores = jnp.where(living[:, None, None, :], scores, -jnp.inf)
+    cache_top = jnp.max(scores, axis=3, keepdims=True)
+    cache_exp = jnp.exp(scores - cache_top)
+    cache_total = jnp.sum(cache_exp, axis=3, keepdims=True)
+    cache_probs = cache_exp.astype(jnp.bfloat16)
+    gathered = jnp.einsum(
+        "shqk,skhd->sqhd", cache_probs, slot_values, preferred_element_type=jnp.float32
+    )
+    owned_part = (
+        (gathered / jnp.transpose(cache_total, (0, 2, 1, 3)))
+        .astype(jnp.bfloat16)
+        .reshape(requests, draft, width)
+    )
+    owned_lse = (cache_top + jnp.log(cache_total))[..., 0]
+    lse_flat = split_three(owned_lse).reshape(requests, -1)
+    lse_rows = -(-lse_flat.shape[1] // width)
+    lse_flat = jnp.pad(lse_flat, ((0, 0), (0, lse_rows * width - lse_flat.shape[1])))
+    back = jnp.concatenate(
+        [owned_part, lse_flat.reshape(requests, lse_rows, width)], axis=1
+    )
+    returned = lax.all_to_all(
+        spread(back, receive_index), "dp", split_axis=0, concat_axis=0, tiled=True
+    )[send_index]
+    cache_part = returned[:, :draft]
+    lse_back = returned[:, draft:].reshape(requests, -1)[:, : 3 * local_heads * draft]
+    cache_lse = join_three(lse_back.reshape(requests, 3, local_heads, draft))
     cache_weight = jnp.transpose(cache_lse, (0, 2, 1))[..., None]
     larger = jnp.maximum(cache_weight, tree_lse)
     cache_share = jnp.exp(cache_weight - larger)
@@ -266,7 +227,8 @@
     ).astype(jnp.float32)
     second_mixed = down_share + columns(b_down) + columns(first_normed).astype(jnp.float32)
     second_sums = lax.psum(
-        (jnp.sum(second_mixed, axis=1), jnp.sum(second_mixed * second_mixed, axis=1)), "head"
+        jnp.stack([jnp.sum(second_mixed, axis=1), jnp.sum(second_mixed * second_mixed, axis=1)]),
+        "head",
     )
     layer_out = normalize_shared(
         second_mixed, second_sums, columns(second_gain), columns(second_shift), model_width

time: 321 us -> 270 us (0.84)
  local copies, waits for them, and re-layouts: 57.7 us -> 21.3 us
  blocking collectives: 15.6 us -> 32.6 us
  starting transfers between devices: 33.6 us -> 21.3 us
  loops' own time: 11.9 us -> 0 us
  waiting for transfers between devices: 140 us -> 134 us
    dynamic_slice x40 -> x0, local copies, waits for them, and re-layouts: 21.6 us -> none  [local(): lax.map(attend_slot, (owned_queries, cache_keys, cache_values, slot_lengt...]
    all_to_all x0 -> x1, blocking collectives: none -> 16.9 us  [local(): lax.all_to_all(spread(kept_values, send_index), 'dp', split_axis=0, conca...]
    another operation x33 -> x0, loops' own time: 11.9 us -> none  [the longest x1 11.1 us: local(): lax.map(attend_slot, (owned_queries, cache_keys, cache_values, slot_lengt...]
    all_to_all x3 -> x1, starting transfers between devices: 18.1 us -> 7.65 us  [local(): lax.all_to_all(spread(back, receive_index), 'dp', split_axis=0, concat_ax...]
    scatter x5 -> x0, local copies, waits for them, and re-layouts: 9.11 us -> none  [spread(): return holder.at[index].set(values)]
    select_n x2 -> x7, other arithmetic: 0.78 us -> 8.1 us  [the longest x3 7.31 us: spread(): return jnp.where(filled.reshape(shape), taken, jnp.zeros((), values.dtype))]
    all_to_all x3 -> x1, waiting for transfers between devices: 25.9 us -> 20 us  [local(): lax.all_to_all(spread(back, receive_index), 'dp', split_axis=0, concat_ax...]
    lt x8 -> x1, other arithmetic: 5.28 us -> 0.07 us  [local(): jnp.arange(capacity, dtype=jnp.int32)[None, :] < slot_lengths[:, None]]
  transfers between devices with their start and end apart: 7 -> 5, of which waited for: 7 -> 5; matrix products, arithmetic and copies ran while one was open for 9% -> 8% of each run, Pallas kernels for 0% -> 0%
where the time goes in v1:
time: 270 us; the launch traced here: 269 us
  waiting for transfers between devices  134 us (50%)
  blocking collectives  32.6 us (12%)
  matrix products  25.2 us (9%)
  local copies, waits for them, and re-layouts  21.3 us (8%)
  starting transfers between devices  21.3 us (8%)
  other arithmetic  20.5 us (8%)
  between operations  14.5 us (5%)
    psum x1, waiting for transfers between devices, local(): lax.psum(attention_term.astype(jnp.bfloat16), 'head').astype(jnp.float32)  83.1 us
    all_to_all x1, waiting for transfers between devices, local(): lax.all_to_all(spread(shaped_queries, send_index), 'dp', split_axis=0, co...  21.5 us
    all_to_all x1, waiting for transfers between devices, local(): lax.all_to_all(spread(back, receive_index), 'dp', split_axis=0, concat_ax...  20 us
    all_to_all x1, blocking collectives, local(): lax.all_to_all(spread(kept_values, send_index), 'dp', split_axis=0, conca...  16.9 us
    psum x1, blocking collectives, local(): lax.psum(jnp.stack([jnp.sum(second_mixed, axis=1), jnp.sum(second_mixed *...  15.7 us
    all_to_all x1, starting transfers between devices, local(): lax.all_to_all(spread(shaped_queries, send_index), 'dp', split_axis=0, co...  7.81 us
    all_to_all x1, starting transfers between devices, local(): lax.all_to_all(spread(back, receive_index), 'dp', split_axis=0, concat_ax...  7.65 us
    select_n x3, other arithmetic, spread(): return jnp.where(filled.reshape(shape), taken, jnp.zeros((), values.dtype))  7.31 us
  transfers between devices with their start and end apart: 5, of which 5 were waited for; matrix products, arithmetic and copies ran while one was open for 8% of the time, Pallas kernels for 0%

profile of v1, /device:TPU:2, one launch (start us, length us, event | category | flops | bytes accessed | tf_op | source)
XLA Modules:
  0.0 269.0 jit_solution(11724927402281657406)
XLA Ops:
  9.2 2.6 fusion.24
  11.9 2.0 gather_fusion.1
  13.8 3.1 %broadcast_select_fusion.1 = bf16[64,64,256]{2,1,0:T(8,128)(2,1)} fusion(bf16[64,64,256]{2,1,0:T(8,128)(2,1)} %gather_fusion.1, pred[64]{0:T(512)(128)(4,1)S(1)} %fusion.73), kind=kLoop, calls=%fused_computation.26 | loop fusion | flops 1048576 | bytes 4194368 | tf_op jit(solution)/shard_map/jit(_where)/select_n | solution.py:148
  16.9 7.8 %all-to-all-start = ((bf16[64,64,256]{2,1,0:T(8,128)(2,1)}), bf16[64,64,256]{2,1,0:T(8,128)(2,1)}, u32[]{:S(2)}, u32[]{:S(2)}) async-start(bf16[64,64,256]{2,1,0:T(8,128)(2,1)} %broadcast_select_fusion.1), calls=%async_computation | async-start | bytes 4194304 | tf_op jit(solution)/shard_map/all_to_all | solution.py:151
  26.7 2.6 convolution_convert_fusion.2
  29.3 21.5 %all-to-all-done = bf16[64,64,256]{2,1,0:T(8,128)(2,1)} async-done(((bf16[64,64,256]{2,1,0:T(8,128)(2,1)}), bf16[64,64,256]{2,1,0:T(8,128)(2,1)}, u32[]{:S(2)}, u32[]{:S(2)}) %all-to-all-start) | async-done | bytes 2097184 | tf_op jit(solution)/shard_map/all_to_all | solution.py:151
  50.8 2.2 gather_fusion.2
  52.9 2.5 fusion.7
  58.2 2.1 gather_fusion.3
  60.3 3.3 %broadcast_select_fusion = bf16[64,66,256]{2,1,0:T(8,128)(2,1)} fusion(bf16[64,66,256]{2,1,0:T(8,128)(2,1)} %gather_fusion.3, pred[64]{0:T(512)(128)(4,1)S(1)} %fusion.74), kind=kLoop, calls=%fused_computation.17 | loop fusion | flops 1081344 | bytes 4325440 | tf_op jit(solution)/shard_map/jit(_where)/select_n | solution.py:148
  63.5 7.6 %all-to-all-start.1 = ((bf16[64,66,256]{2,1,0:T(8,128)(2,1)}), bf16[64,66,256]{2,1,0:T(8,128)(2,1)}, u32[]{:S(2)}, u32[]{:S(2)}) async-start(bf16[64,66,256]{2,1,0:T(8,128)(2,1)} %broadcast_select_fusion), calls=%async_computation.1 | async-start | bytes 4718592 | tf_op jit(solution)/shard_map/all_to_all | solution.py:193
  75.4 2.6 fusion.25
  80.1 20.0 %all-to-all-done.1 = bf16[64,66,256]{2,1,0:T(8,128)(2,1)} async-done(((bf16[64,66,256]{2,1,0:T(8,128)(2,1)}), bf16[64,66,256]{2,1,0:T(8,128)(2,1)}, u32[]{:S(2)}, u32[]{:S(2)}) %all-to-all-start.1) | async-done | bytes 2162720 | tf_op jit(solution)/shard_map/all_to_all | solution.py:193
  100.1 2.2 gather_fusion.4
  104.6 2.0 convolution_convert_fusion
  106.9 83.1 %all-reduce.3.cloned.1.call-done = bf16[512,2048]{1,0:T(8,128)(2,1)} async-done(((bf16[512,2048]{1,0:T(8,128)(2,1)}), bf16[512,2048]{1,0:T(8,128)(2,1)}) %all-reduce.3.cloned.1.call-update) | async-done | bytes 2097168 | tf_op jit(solution)/shard_map/psum | solution.py:215
  190.0 3.5 %fusion = (f32[512]{0:T(512)S(1)}, f32[512]{0:T(512)S(1)}) fusion(bf16[512,2048]{1,0:T(8,128)(2,1)} %param.23, bf16[512,2048]{1,0:T(8,128)(2,1)} %all-reduce.3.cloned.1.call-done, f32[2048]{0:T(1024)S(1)} %copy-done.5), kind=kLoop, calls=%fused_computation.14 | loop fusion | flops 7339008 | bytes 4206592 | tf_op jit(solution)/shard_map/reduce_sum | solution.py:26
  193.5 2.6 add_convert_fusion
  196.2 6.1 %convolution_convert_fusion.1 = bf16[512,2048]{1,0:T(8,128)(2,1)} fusion(bf16[512,2048]{1,0:T(8,128)(2,1)S(1)} %copy-done, bf16[512,2048]{1,0:T(8,128)(2,1)} %add_convert_fusion, bf16[2048,512]{1,0:T(8,128)(2,1)} %param.40, f32[512]{0:T(512)S(1)} %copy-done.13), kind=kOutput, calls=%fused_computation.16 | convolution fusion | flops 2151153664 | bytes 8390656 | tf_op jit(solution)/shard_map/dot_general | solution.py:223
  207.1 16.9 %all_to_all.20 = bf16[64,16,256]{2,1,0:T(8,128)(2,1)S(1)} all-to-all(bf16[64,16,256]{2,1,0:T(8,128)(2,1)S(1)} %get-tuple-element.20), channel_id=1, replica_groups=mesh['dp'=32,'head'=8] {'dp'}, dimensions={0} | all-to-all | bytes 1048576 | tf_op jit(solution)/shard_map/all_to_all | solution.py:157
  224.0 5.6 %all-to-all-start.2 = ((bf16[64,16,256]{2,1,0:T(8,128)(2,1)}), bf16[64,16,256]{2,1,0:T(8,128)(2,1)S(1)}, u32[]{:S(2)}, u32[]{:S(2)}) async-start(bf16[64,16,256]{2,1,0:T(8,128)(2,1)} %get-tuple-element.21), calls=%async_computation.3 | async-start | bytes 1048576 | tf_op jit(solution)/shard_map/all_to_all | solution.py:154
  233.1 6.2 %all-to-all-done.2 = bf16[64,16,256]{2,1,0:T(8,128)(2,1)S(1)} async-done(((bf16[64,16,256]{2,1,0:T(8,128)(2,1)}), bf16[64,16,256]{2,1,0:T(8,128)(2,1)S(1)}, u32[]{:S(2)}, u32[]{:S(2)}) %all-to-all-start.2) | async-done | bytes 524320 | tf_op jit(solution)/shard_map/all_to_all | solution.py:154
  240.5 2.7 %reduce-scatter.2.cloned.1.call-done = bf16[512,256]{1,0:T(8,128)(2,1)} async-done(((bf16[512,2048]{1,0:T(8,128)(2,1)}), bf16[512,256]{1,0:T(8,128)(2,1)}) %reduce-scatter.2.cloned.1.call-update) | async-done | bytes 262160 | tf_op jit(solution)/shard_map/reduce_scatter | solution.py:222
  244.5 15.7 %psum.15 = f32[2,512]{1,0:T(2,128)S(1)} all-reduce(f32[2,512]{1,0:T(2,128)S(1)} %pad_maximum_fusion.2), channel_id=1, replica_groups=mesh['dp'=32,'head'=8] {'head'}, use_global_device_ids=true, to_apply=%region_17.18 | all-reduce | flops 1024 | bytes 8192 | tf_op jit(solution)/shard_map/psum | solution.py:229
  (113 shorter events, 28.0 us)
Async XLA Ops:
  7.2 189.0 %copy-start = (bf16[512,2048]{1,0:T(8,128)(2,1)S(1)}, bf16[512,2048]{1,0:T(8,128)(2,1)}, u32[]{:S(2)}) copy-start(bf16[512,2048]{1,0:T(8,128)(2,1)} %param.42) | copy-start | bytes 6291460
  16.9 7.8 %copy-start.8 = (s32[256]{0:T(256)S(1)}, s32[256]{0:T(256)}, u32[]{:S(2)}) copy-start(s32[256]{0:T(256)} %param.25) | copy-start | bytes 3076
  16.9 9.1 %copy-start.11 = (s32[8]{0:T(128)S(1)}, s32[8]{0:T(128)}, u32[]{:S(2)}) copy-start(s32[8]{0:T(128)} %param.26) | copy-start | bytes 100
  16.9 9.2 %copy-start.9 = (s32[8,64]{1,0:T(8,128)S(1)}, s32[8,64]{1,0:T(8,128)}, u32[]{:S(2)}) copy-start(s32[8,64]{1,0:T(8,128)} %param.24) | copy-start | bytes 6148
  16.9 33.8 %all-to-all-start = ((bf16[64,64,256]{2,1,0:T(8,128)(2,1)}), bf16[64,64,256]{2,1,0:T(8,128)(2,1)}, u32[]{:S(2)}, u32[]{:S(2)}) async-start(bf16[64,64,256]{2,1,0:T(8,128)(2,1)} %broadcast_select_fusion.1), calls=%async_computation | async-start | bytes 4194304 | tf_op jit(solution)/shard_map/all_to_all | solution.py:151
  55.4 1.6 copy-start.12
  63.5 36.6 %all-to-all-start.1 = ((bf16[64,66,256]{2,1,0:T(8,128)(2,1)}), bf16[64,66,256]{2,1,0:T(8,128)(2,1)}, u32[]{:S(2)}, u32[]{:S(2)}) async-start(bf16[64,66,256]{2,1,0:T(8,128)(2,1)} %broadcast_select_fusion), calls=%async_computation.1 | async-start | bytes 4718592 | tf_op jit(solution)/shard_map/all_to_all | solution.py:193
  71.2 118.8 %all-reduce.3.cloned.1.call-start = ((), (), s32[]{:S(2)}) async-start(), calls=%async_computation.5 | async-start | bytes 4194304 | tf_op jit(solution)/shard_map/psum | solution.py:215
  72.4 2.9 %copy-start.14 = (f32[256]{0:T(256)S(1)}, f32[256]{0:T(256)}, u32[]{:S(2)}) copy-start(f32[256]{0:T(256)} %param.35) | copy-start | bytes 3076
  75.3 3.4 %copy-start.4 = (bf16[8,64,2,128]{3,2,1,0:T(2,128)(2,1)S(1)}, bf16[8,64,2,128]{3,2,1,0:T(2,128)(2,1)}, u32[]{:S(2)}) copy-start(bf16[8,64,2,128]{3,2,1,0:T(2,128)(2,1)} %reshape.397) | copy-start | bytes 786436
  102.5 2.1 copy-start.3
  104.6 85.4 %copy-start.5 = (f32[2048]{0:T(1024)S(1)}, f32[2048]{0:T(1024)}, u32[]{:S(2)}) copy-start(f32[2048]{0:T(1024)} %param.37) | copy-start | bytes 24580
  106.7 86.8 %copy-start.6 = (f32[2048]{0:T(1024)S(1)}, f32[2048]{0:T(1024)}, u32[]{:S(2)}) copy-start(f32[2048]{0:T(1024)} %param.39) | copy-start | bytes 24580
  106.7 86.8 %copy-start.7 = (f32[2048]{0:T(1024)S(1)}, f32[2048]{0:T(1024)}, u32[]{:S(2)}) copy-start(f32[2048]{0:T(1024)} %param.38) | copy-start | bytes 24580
  106.7 136.5 %reduce-scatter.2.cloned.1.call-start = ((), (), s32[]{:S(2)}) async-start(), calls=%async_computation.6 | async-start | bytes 2359296 | tf_op jit(solution)/shard_map/reduce_scatter | solution.py:222
  190.0 3.5 %copy-start.1 = (bf16[512,2048]{1,0:T(8,128)(2,1)S(1)}, bf16[512,2048]{1,0:T(8,128)(2,1)}, u32[]{:S(2)}) copy-start(bf16[512,2048]{1,0:T(8,128)(2,1)} %param.23) | copy-start | bytes 6291460
  190.0 3.5 %copy-start.2 = (bf16[512,2048]{1,0:T(8,128)(2,1)S(1)}, bf16[512,2048]{1,0:T(8,128)(2,1)}, u32[]{:S(2)}) copy-start(bf16[512,2048]{1,0:T(8,128)(2,1)} %all-reduce.3.cloned.1.call-done) | copy-start | bytes 6291460
  193.5 2.6 copy-start.13
  202.2 0.7 copy-start.10
  202.2 2.6 copy-start.15
  224.0 15.3 %all-to-all-start.2 = ((bf16[64,16,256]{2,1,0:T(8,128)(2,1)}), bf16[64,16,256]{2,1,0:T(8,128)(2,1)S(1)}, u32[]{:S(2)}, u32[]{:S(2)}) async-start(bf16[64,16,256]{2,1,0:T(8,128)(2,1)} %get-tuple-element.21), calls=%async_computation.3 | async-start | bytes 1048576 | tf_op jit(solution)/shard_map/all_to_all | solution.py:154
Sparse Core Ops, SparseCore 0:
  106.8 83.1 all-reduce.2
  202.4 40.7 reduce-scatter.1

commit v2 on v1

--- a/solution.py
+++ b/solution.py
@@ -45,6 +45,9 @@
 def join_three(pieces):
     wide = pieces.astype(jnp.float32)
     return wide[:, 0] + (wide[:, 1] + wide[:, 2])
+
+
+CHUNKS = 2
 
 
 def local(
@@ -74,15 +77,14 @@
 ):
     requests = parents.shape[0]
     draft = parents.shape[1]
-    tokens = hidden.shape[0]
     model_width = hidden.shape[1]
     width = w_query.shape[1]
     local_heads = width // HD
     capacity = cache_keys.shape[1]
-    block = min(capacity, 256)
     shards = lax.axis_size("dp")
     myself = lax.axis_index("dp")
     scale = 1.0 / math.sqrt(HD)
+    rows = draft // CHUNKS
     queries = (jnp.dot(hidden, w_query, preferred_element_type=jnp.float32) + b_query).astype(
         jnp.bfloat16
     )
@@ -132,8 +134,6 @@
         ),
         axis=1,
     )
-
-    shaped_queries = queries.reshape(requests, draft, width)
     slots_total = shards * PEER_MOST
     send_index = target * PEER_MOST + rank
     receive_index = source * PEER_MOST + source_rank
@@ -147,92 +147,125 @@
         shape = (slots_total,) + (1,) * (values.ndim - 1)
         return jnp.where(filled.reshape(shape), taken, jnp.zeros((), values.dtype))
 
-    arrived = (
-        lax.all_to_all(
-            spread(shaped_queries, send_index), "dp", split_axis=0, concat_axis=0, tiled=True
-        ),
-        lax.all_to_all(
-            spread(kept_keys, send_index), "dp", split_axis=0, concat_axis=0, tiled=True
-        ),
-        lax.all_to_all(
-            spread(kept_values, send_index), "dp", split_axis=0, concat_axis=0, tiled=True
-        ),
-    )
-    owned_queries = arrived[0][receive_index].reshape(requests, draft, local_heads, HD)
-    new_keys = arrived[1][receive_index]
-    new_values = arrived[2][receive_index]
+    def exchange(values, there, back):
+        moved = lax.all_to_all(spread(values, there), "dp", split_axis=0, concat_axis=0, tiled=True)
+        return moved[back]
+
     slot_keys = cache_keys.reshape(requests, capacity, local_heads, HD)
     slot_values = cache_values.reshape(requests, capacity, local_heads, HD)
-    scores = (
-        jnp.einsum(
-            "sqhd,skhd->shqk", owned_queries, slot_keys, preferred_element_type=jnp.float32
-        )
-        * scale
-    )
     living = jnp.arange(capacity, dtype=jnp.int32)[None, :] < slot_lengths[:, None]
-    scores = jnp.where(living[:, None, None, :], scores, -jnp.inf)
-    cache_top = jnp.max(scores, axis=3, keepdims=True)
-    cache_exp = jnp.exp(scores - cache_top)
-    cache_total = jnp.sum(cache_exp, axis=3, keepdims=True)
-    cache_probs = cache_exp.astype(jnp.bfloat16)
-    gathered = jnp.einsum(
-        "shqk,skhd->sqhd", cache_probs, slot_values, preferred_element_type=jnp.float32
-    )
-    owned_part = (
-        (gathered / jnp.transpose(cache_total, (0, 2, 1, 3)))
-        .astype(jnp.bfloat16)
-        .reshape(requests, draft, width)
-    )
-    owned_lse = (cache_top + jnp.log(cache_total))[..., 0]
-    lse_flat = split_three(owned_lse).reshape(requests, -1)
-    lse_rows = -(-lse_flat.shape[1] // width)
-    lse_flat = jnp.pad(lse_flat, ((0, 0), (0, lse_rows * width - lse_flat.shape[1])))
-    back = jnp.concatenate(
-        [owned_part, lse_flat.reshape(requests, lse_rows, width)], axis=1
-    )
-    returned = lax.all_to_all(
-        spread(back, receive_index), "dp", split_axis=0, concat_axis=0, tiled=True
-    )[send_index]
-    cache_part = returned[:, :draft]
-    lse_back = returned[:, draft:].reshape(requests, -1)[:, : 3 * local_heads * draft]
-    cache_lse = join_three(lse_back.reshape(requests, 3, local_heads, draft))
-    cache_weight = jnp.transpose(cache_lse, (0, 2, 1))[..., None]
-    larger = jnp.maximum(cache_weight, tree_lse)
-    cache_share = jnp.exp(cache_weight - larger)
-    tree_share = jnp.exp(tree_lse - larger)
-    blended = (
-        cache_share * cache_part.astype(jnp.float32).reshape(requests, draft, local_heads, HD)
-        + tree_share * tree_part
-    ) / (cache_share + tree_share)
-    attended = blended.astype(jnp.bfloat16).reshape(tokens, width)
-    attention_term = jnp.dot(attended, w_out, preferred_element_type=jnp.float32)
+    shaped_queries = queries.reshape(requests, draft, width)
+    shaped_hidden = hidden.reshape(requests, draft, model_width)
     feature = model_width // lax.axis_size("head")
     offset = lax.axis_index("head") * feature
 
     def columns(values):
         return lax.dynamic_slice_in_dim(values, offset, feature, values.ndim - 1)
 
-    attention_sum = lax.psum(attention_term.astype(jnp.bfloat16), "head").astype(jnp.float32)
-    first_normed = normalize(
-        attention_sum + b_out + hidden.astype(jnp.float32), first_gain, first_shift
-    ).astype(jnp.bfloat16)
-    inner = jax.nn.gelu(
-        jnp.dot(first_normed, w_up, preferred_element_type=jnp.float32) + b_up, approximate=True
-    ).astype(jnp.bfloat16)
-    down_share = lax.psum_scatter(
-        jnp.dot(inner, w_down, preferred_element_type=jnp.float32).astype(jnp.bfloat16),
-        "head",
-        scatter_dimension=1,
-        tiled=True,
-    ).astype(jnp.float32)
-    second_mixed = down_share + columns(b_down) + columns(first_normed).astype(jnp.float32)
-    second_sums = lax.psum(
-        jnp.stack([jnp.sum(second_mixed, axis=1), jnp.sum(second_mixed * second_mixed, axis=1)]),
-        "head",
-    )
-    layer_out = normalize_shared(
-        second_mixed, second_sums, columns(second_gain), columns(second_shift), model_width
-    ).astype(jnp.bfloat16)
+    paths = kept_keys.shape[1]
+    kept = exchange(jnp.concatenate([kept_keys, kept_values], axis=1), send_index, receive_index)
+    new_keys = kept[:, :paths]
+    new_values = kept[:, paths:]
+    attention_terms = []
+    attention_sums = []
+    for chunk in range(CHUNKS):
+        low = chunk * rows
+        sent = shaped_queries[:, low : low + rows]
+        if chunk > 0:
+            sent, attention_terms[-1] = lax.optimization_barrier((sent, attention_terms[-1]))
+            attention_sums.append(lax.psum(attention_terms[-1].astype(jnp.bfloat16), "head"))
+        arrived = exchange(sent, send_index, receive_index)
+        owned_queries = arrived[:, :rows].reshape(requests, rows, local_heads, HD)
+        scores = (
+            jnp.einsum(
+                "sqhd,skhd->shqk", owned_queries, slot_keys, preferred_element_type=jnp.float32
+            )
+            * scale
+        )
+        scores = jnp.where(living[:, None, None, :], scores, -jnp.inf)
+        cache_top = jnp.max(scores, axis=3, keepdims=True)
+        cache_exp = jnp.exp(scores - cache_top)
+        cache_total = jnp.sum(cache_exp, axis=3, keepdims=True)
+        cache_probs = cache_exp.astype(jnp.bfloat16)
+        gathered = jnp.einsum(
+            "shqk,skhd->sqhd", cache_probs, slot_values, preferred_element_type=jnp.float32
+        )
+        owned_part = (
+            (gathered / jnp.transpose(cache_total, (0, 2, 1, 3)))
+            .astype(jnp.bfloat16)
+            .reshape(requests, rows, width)
+        )
+        owned_lse = (cache_top + jnp.log(cache_total))[..., 0]
+        lse_flat = split_three(owned_lse).reshape(requests, -1)
+        lse_rows = -(-lse_flat.shape[1] // width)
+        lse_flat = jnp.pad(lse_flat, ((0, 0), (0, lse_rows * width - lse_flat.shape[1])))
+        back = jnp.concatenate([owned_part, lse_flat.reshape(requests, lse_rows, width)], axis=1)
+        returned = exchange(back, receive_index, send_index)
+        cache_part = returned[:, :rows]
+        lse_back = returned[:, rows:].reshape(requests, -1)[:, : 3 * local_heads * rows]
+        cache_lse = join_three(lse_back.reshape(requests, 3, local_heads, rows))
+        cache_weight = jnp.transpose(cache_lse, (0, 2, 1))[..., None]
+        tree_weight = tree_lse[:, low : low + rows]
+        larger = jnp.maximum(cache_weight, tree_weight)
+        cache_share = jnp.exp(cache_weight - larger)
+        tree_share = jnp.exp(tree_weight - larger)
+        blended = (
+            cache_share * cache_part.astype(jnp.float32).reshape(requests, rows, local_heads, HD)
+            + tree_share * tree_part[:, low : low + rows]
+        ) / (cache_share + tree_share)
+        attended = blended.astype(jnp.bfloat16).reshape(requests * rows, width)
+        if chunk > 0:
+            attended, attention_sums[-1] = lax.optimization_barrier(
+                (attended, attention_sums[-1])
+            )
+        attention_terms.append(jnp.dot(attended, w_out, preferred_element_type=jnp.float32))
+    attention_sums.append(lax.psum(attention_terms[-1].astype(jnp.bfloat16), "head"))
+    mixed_parts = []
+    for chunk in range(CHUNKS):
+        low = chunk * rows
+        attention_sum = attention_sums[chunk].astype(jnp.float32)
+        residual = shaped_hidden[:, low : low + rows].reshape(requests * rows, model_width)
+        first_normed = normalize(
+            attention_sum + b_out + residual.astype(jnp.float32), first_gain, first_shift
+        ).astype(jnp.bfloat16)
+        inner = jax.nn.gelu(
+            jnp.dot(first_normed, w_up, preferred_element_type=jnp.float32) + b_up,
+            approximate=True,
+        ).astype(jnp.bfloat16)
+        down_share = lax.psum_scatter(
+            jnp.dot(inner, w_down, preferred_element_type=jnp.float32).astype(jnp.bfloat16),
+            "head",
+            scatter_dimension=1,
+            tiled=True,
+        ).astype(jnp.float32)
+        mixed_parts.append(
+            down_share + columns(b_down) + columns(first_normed).astype(jnp.float32)
+        )
+    row_sums = []
+    for chunk in range(CHUNKS):
+        second_mixed = mixed_parts[chunk]
+        if chunk > 0:
+            second_mixed, row_sums[-1] = lax.optimization_barrier((second_mixed, row_sums[-1]))
+            mixed_parts[chunk] = second_mixed
+        row_sums.append(
+            lax.psum(
+                jnp.stack(
+                    [jnp.sum(second_mixed, axis=1), jnp.sum(second_mixed * second_mixed, axis=1)]
+                ),
+                "head",
+            )
+        )
+    outputs = []
+    for chunk in range(CHUNKS):
+        layer_part = normalize_shared(
+            mixed_parts[chunk],
+            row_sums[chunk],
+            columns(second_gain),
+            columns(second_shift),
+            model_width,
+        ).astype(jnp.bfloat16)
+        outputs.append(layer_part.reshape(requests, rows, feature))
+    layer_out = jnp.concatenate(outputs, axis=1).reshape(requests * draft, feature)
     return (layer_out, new_keys, new_values)
 
 

time: 270 us -> 413 us (1.53)
  waiting for transfers between devices: 134 us -> 224 us
  blocking collectives: 32.6 us -> 51 us
  matrix products: 25.2 us -> 33.9 us
  other arithmetic: 20.5 us -> 29.1 us
  starting transfers between devices: 21.3 us -> 29.9 us
  local copies, waits for them, and re-layouts: 21.3 us -> 29.2 us
    psum x1 -> x2, waiting for transfers between devices: 83.1 us -> 134 us  [local(): lax.psum(attention_terms[-1].astype(jnp.bfloat16), 'head')]
    reduce_scatter x1 -> x2, waiting for transfers between devices: 2.72 us -> 48.3 us  [local(): lax.psum_scatter(jnp.dot(inner, w_down, preferred_element_type=jnp.float3...]
    psum x1 -> x2, blocking collectives: 15.7 us -> 30.3 us  [local(): lax.psum(jnp.stack([jnp.sum(second_mixed, axis=1), jnp.sum(second_mixed *...]
    all_to_all x3 -> x4, starting transfers between devices: 21 us -> 29.7 us  [exchange(): lax.all_to_all(spread(values, there), 'dp', split_axis=0, concat_axis=0,...]
    all_to_all x3 -> x4, waiting for transfers between devices: 47.7 us -> 41.8 us  [exchange(): lax.all_to_all(spread(values, there), 'dp', split_axis=0, concat_axis=0,...]
    slice x0 -> x5, local copies, waits for them, and re-layouts: none -> 4.18 us  [the longest x1 2.72 us: local(): shaped_hidden[:, low:low + rows].reshape(requests * rows, model_width)]
    dot_general x1 -> x2, matrix products: 6.08 us -> 8.51 us  [local(): jnp.dot(inner, w_down, preferred_element_type=jnp.float32)]
    select_n x3 -> x4, other arithmetic: 7.31 us -> 8.74 us  [spread(): return jnp.where(filled.reshape(shape), taken, jnp.zeros((), values.dtype))]
  transfers between devices with their start and end apart: 5 -> 8, of which waited for: 5 -> 7; matrix products, arithmetic and copies ran while one was open for 8% -> 10% of each run, Pallas kernels for 0% -> 0%
where the time goes in v2:
time: 413 us; the launch traced here: 412 us
  waiting for transfers between devices  224 us (54%)
  blocking collectives  51 us (12%)
  matrix products  33.9 us (8%)
  starting transfers between devices  29.9 us (7%)
  local copies, waits for them, and re-layouts  29.2 us (7%)
  other arithmetic  29.1 us (7%)
  between operations  14.6 us (4%)
    psum x2, waiting for transfers between devices, local(): lax.psum(attention_terms[-1].astype(jnp.bfloat16), 'head')  134 us
    reduce_scatter x2, waiting for transfers between devices, local(): lax.psum_scatter(jnp.dot(inner, w_down, preferred_element_type=jnp.float3...  48.3 us
    all_to_all x4, waiting for transfers between devices, exchange(): lax.all_to_all(spread(values, there), 'dp', split_axis=0, concat_axis=0,...  41.8 us
    psum x2, blocking collectives, local(): lax.psum(jnp.stack([jnp.sum(second_mixed, axis=1), jnp.sum(second_mixed *...  30.3 us
    all_to_all x4, starting transfers between devices, exchange(): lax.all_to_all(spread(values, there), 'dp', split_axis=0, concat_axis=0,...  29.7 us
    all_to_all x1, blocking collectives, exchange(): lax.all_to_all(spread(values, there), 'dp', split_axis=0, concat_axis=0,...  20.7 us
    select_n x4, other arithmetic, spread(): return jnp.where(filled.reshape(shape), taken, jnp.zeros((), values.dtype))  8.74 us
    dot_general x2, matrix products, local(): jnp.dot(inner, w_down, preferred_element_type=jnp.float32)  8.51 us
  transfers between devices with their start and end apart: 8, of which 7 were waited for; matrix products, arithmetic and copies ran while one was open for 10% of the time, Pallas kernels for 0%

profile of v2, /device:TPU:2, one launch (start us, length us, event | category | flops | bytes accessed | tf_op | source)
XLA Modules:
  0.0 412.0 jit_solution(18351491330055430950)
XLA Ops:
  10.6 2.6 fusion.28
  15.7 7.6 %all-to-all-start = ((bf16[64,32,256]{2,1,0:T(8,128)(2,1)}), bf16[64,32,256]{2,1,0:T(8,128)(2,1)S(1)}, u32[]{:S(2)}, u32[]{:S(2)}) async-start(bf16[64,32,256]{2,1,0:T(8,128)(2,1)} %broadcast_select_fusion.4), calls=%async_computation | async-start | bytes 2097152 | tf_op jit(solution)/shard_map/all_to_all | solution.py:151
  44.8 2.6 fusion.155
  50.4 2.6 broadcast_select_fusion.1
  53.0 7.6 %all-to-all-start.1 = ((bf16[64,33,256]{2,1,0:T(8,128)(2,1)}), bf16[64,33,256]{2,1,0:T(8,128)(2,1)}, u32[]{:S(2)}, u32[]{:S(2)}) async-start(bf16[64,33,256]{2,1,0:T(8,128)(2,1)} %broadcast_select_fusion.1), calls=%async_computation.1 | async-start | bytes 2621440 | tf_op jit(solution)/shard_map/all_to_all | solution.py:151
  64.9 13.1 %all-to-all-done.1 = bf16[64,33,256]{2,1,0:T(8,128)(2,1)} async-done(((bf16[64,33,256]{2,1,0:T(8,128)(2,1)}), bf16[64,33,256]{2,1,0:T(8,128)(2,1)}, u32[]{:S(2)}, u32[]{:S(2)}) %all-to-all-start.1) | async-done | bytes 1081376 | tf_op jit(solution)/shard_map/all_to_all | solution.py:151
  82.8 2.7 fusion.105
  89.5 20.7 %all_to_all.25 = bf16[64,32,256]{2,1,0:T(8,128)(2,1)S(1)} all-to-all(bf16[64,32,256]{2,1,0:T(8,128)(2,1)S(1)} %get-tuple-element.61), channel_id=1, replica_groups=mesh['dp'=32,'head'=8] {'dp'}, dimensions={0} | all-to-all | bytes 2097152 | tf_op jit(solution)/shard_map/all_to_all | solution.py:151
  110.7 2.6 fusion.157
  118.8 7.1 %all-to-all-start.3 = ((bf16[64,33,256]{2,1,0:T(8,128)(2,1)}), bf16[64,33,256]{2,1,0:T(8,128)(2,1)}, u32[]{:S(2)}, u32[]{:S(2)}) async-start(bf16[64,33,256]{2,1,0:T(8,128)(2,1)} %broadcast_select_fusion), calls=%async_computation.3 | async-start | bytes 2621440 | tf_op jit(solution)/shard_map/all_to_all | solution.py:151
  126.7 16.6 %all-to-all-done.3 = bf16[64,33,256]{2,1,0:T(8,128)(2,1)} async-done(((bf16[64,33,256]{2,1,0:T(8,128)(2,1)}), bf16[64,33,256]{2,1,0:T(8,128)(2,1)}, u32[]{:S(2)}, u32[]{:S(2)}) %all-to-all-start.3) | async-done | bytes 1081376 | tf_op jit(solution)/shard_map/all_to_all | solution.py:151
  146.8 61.0 %all-reduce.5.cloned.1.call-done = bf16[256,2048]{1,0:T(8,128)(2,1)} async-done(((bf16[256,2048]{1,0:T(8,128)(2,1)}), bf16[256,2048]{1,0:T(8,128)(2,1)}) %all-reduce.5.cloned.1.call-update) | async-done | bytes 1048592 | tf_op jit(solution)/shard_map/psum | solution.py:176
  209.4 2.7 fusion.152
  212.2 72.5 %all-reduce.7.cloned.1.call-done = bf16[256,2048]{1,0:T(8,128)(2,1)} async-done(((bf16[256,2048]{1,0:T(8,128)(2,1)}), bf16[256,2048]{1,0:T(8,128)(2,1)}) %all-reduce.7.cloned.1.call-update) | async-done | bytes 1048592 | tf_op jit(solution)/shard_map/psum | solution.py:222
  284.7 3.2 fusion.12
  288.0 2.6 add_convert_fusion.1
  290.6 4.5 %convolution_convert_fusion = bf16[256,2048]{1,0:T(8,128)(2,1)} fusion(bf16[512,2048]{1,0:T(8,128)(2,1)S(1)} %copy-done, bf16[256,2048]{1,0:T(8,128)(2,1)} %get-tuple-element.38, bf16[2048,512]{1,0:T(8,128)(2,1)} %param.40, f32[512]{0:T(512)S(1)} %copy-done.27), kind=kOutput, calls=%fused_computation.13 | convolution fusion | flops 1075576832 | bytes 6293504 | tf_op jit(solution)/shard_map/dot_general | solution.py:236
  295.2 4.0 convolution_convert_fusion.1
  299.2 7.5 %all-to-all-start.4 = ((bf16[64,32,256]{2,1,0:T(8,128)(2,1)}), bf16[64,32,256]{2,1,0:T(8,128)(2,1)}, u32[]{:S(2)}, u32[]{:S(2)}) async-start(bf16[64,32,256]{2,1,0:T(8,128)(2,1)} %get-tuple-element.60), calls=%async_computation.6 | async-start | bytes 2097152 | tf_op jit(solution)/shard_map/all_to_all | solution.py:151
  309.0 12.2 %all-to-all-done.4 = bf16[64,32,256]{2,1,0:T(8,128)(2,1)} async-done(((bf16[64,32,256]{2,1,0:T(8,128)(2,1)}), bf16[64,32,256]{2,1,0:T(8,128)(2,1)}, u32[]{:S(2)}, u32[]{:S(2)}) %all-to-all-start.4) | async-done | bytes 1048608 | tf_op jit(solution)/shard_map/all_to_all | solution.py:151
  323.6 8.5 %reduce-scatter.5.cloned.1.call-done = bf16[256,256]{1,0:T(8,128)(2,1)} async-done(((bf16[256,2048]{1,0:T(8,128)(2,1)}), bf16[256,256]{1,0:T(8,128)(2,1)}) %reduce-scatter.5.cloned.1.call-update) | async-done | bytes 131088 | tf_op jit(solution)/shard_map/reduce_scatter | solution.py:235
  332.1 39.8 %reduce-scatter.3.cloned.1.call-done = bf16[256,256]{1,0:T(8,128)(2,1)} async-done(((bf16[256,2048]{1,0:T(8,128)(2,1)}), bf16[256,256]{1,0:T(8,128)(2,1)}) %reduce-scatter.3.cloned.1.call-update) | async-done | bytes 131088 | tf_op jit(solution)/shard_map/reduce_scatter | solution.py:235
  373.1 15.5 %psum.30 = f32[2,256]{1,0:T(2,128)S(1)} all-reduce(f32[2,256]{1,0:T(2,128)S(1)} %pad_maximum_fusion.6), channel_id=1, replica_groups=mesh['dp'=32,'head'=8] {'head'}, use_global_device_ids=true, to_apply=%region_23.24 | all-reduce | flops 512 | bytes 4096 | tf_op jit(solution)/shard_map/psum | solution.py:251
  388.8 14.8 %psum.31 = f32[2,256]{1,0:T(2,128)S(1)} all-reduce(f32[2,256]{1,0:T(2,128)S(1)} %pad_maximum_fusion.7), channel_id=1, replica_groups=mesh['dp'=32,'head'=8] {'head'}, use_global_device_ids=true, to_apply=%region_26.27 | all-reduce | flops 512 | bytes 4096 | tf_op jit(solution)/shard_map/psum | solution.py:251
  (189 shorter events, 62.9 us)
Async XLA Ops:
  7.2 283.4 %copy-start = (bf16[512,2048]{1,0:T(8,128)(2,1)S(1)}, bf16[512,2048]{1,0:T(8,128)(2,1)}, u32[]{:S(2)}) copy-start(bf16[512,2048]{1,0:T(8,128)(2,1)} %param.42) | copy-start | bytes 6291460
  10.5 4.1 copy-start.18
  14.6 8.8 %copy-start.15 = (s32[256]{0:T(256)S(1)}, s32[256]{0:T(256)}, u32[]{:S(2)}) copy-start(s32[256]{0:T(256)} %param.25) | copy-start | bytes 3076
  14.6 9.5 %copy-start.21 = (s32[8]{0:T(128)S(1)}, s32[8]{0:T(128)}, u32[]{:S(2)}) copy-start(s32[8]{0:T(128)} %get-tuple-element.68) | copy-start | bytes 100
  14.6 11.3 %copy-start.17 = (s32[8,16]{1,0:T(8,128)S(1)}, s32[8,16]{1,0:T(8,128)}, u32[]{:S(2)}) copy-start(s32[8,16]{1,0:T(8,128)} %param.27) | copy-start | bytes 1540
  15.7 28.5 %all-to-all-start = ((bf16[64,32,256]{2,1,0:T(8,128)(2,1)}), bf16[64,32,256]{2,1,0:T(8,128)(2,1)S(1)}, u32[]{:S(2)}, u32[]{:S(2)}) async-start(bf16[64,32,256]{2,1,0:T(8,128)(2,1)} %broadcast_select_fusion.4), calls=%async_computation | async-start | bytes 2097152 | tf_op jit(solution)/shard_map/all_to_all | solution.py:151
  26.1 4.8 %copy-start.28 = (f32[256]{0:T(256)S(1)}, f32[256]{0:T(256)}, u32[]{:S(2)}) copy-start(f32[256]{0:T(256)} %param.35) | copy-start | bytes 3076
  30.9 7.2 %copy-start.16 = (s32[8,64]{1,0:T(8,128)S(1)}, s32[8,64]{1,0:T(8,128)}, u32[]{:S(2)}) copy-start(s32[8,64]{1,0:T(8,128)} %param.24) | copy-start | bytes 6148
  39.9 3.6 copy-start.7
  50.4 10.2 %copy-start.9 = (bf16[8,16,256]{2,1,0:T(8,128)(2,1)S(1)}, bf16[8,16,256]{2,1,0:T(8,128)(2,1)}, u32[]{:S(2)}) copy-start(bf16[8,16,256]{2,1,0:T(8,128)(2,1)} %get-tuple-element.53) | copy-start | bytes 196612
  50.4 10.2 %copy-start.10 = (bf16[8,16,256]{2,1,0:T(8,128)(2,1)S(1)}, bf16[8,16,256]{2,1,0:T(8,128)(2,1)}, u32[]{:S(2)}) copy-start(bf16[8,16,256]{2,1,0:T(8,128)(2,1)} %get-tuple-element.54) | copy-start | bytes 196612
  53.0 8.2 %copy-start.20 = (s32[8]{0:T(128)S(1)}, s32[8]{0:T(128)}, u32[]{:S(2)}) copy-start(s32[8]{0:T(128)} %get-tuple-element.29) | copy-start | bytes 100
  53.0 8.3 %copy-start.11 = (pred[8,64,64]{1,2,0:T(8,128)(4,1)S(1)}, pred[8,64,64]{1,2,0:T(8,128)(4,1)}, u32[]{:S(2)}) copy-start(pred[8,64,64]{1,2,0:T(8,128)(4,1)} %copy.62) | copy-start | bytes 98308
  53.0 24.9 %all-to-all-start.1 = ((bf16[64,33,256]{2,1,0:T(8,128)(2,1)}), bf16[64,33,256]{2,1,0:T(8,128)(2,1)}, u32[]{:S(2)}, u32[]{:S(2)}) async-start(bf16[64,33,256]{2,1,0:T(8,128)(2,1)} %broadcast_select_fusion.1), calls=%async_computation.1 | async-start | bytes 2621440 | tf_op jit(solution)/shard_map/all_to_all | solution.py:151
  82.8 4.3 %copy-start.19 = (pred[64]{0:T(512)(128)(4,1)S(1)}, pred[64]{0:T(512)(128)(4,1)}, u32[]{:S(2)}) copy-start(pred[64]{0:T(512)(128)(4,1)} %copy-done.18) | copy-start | bytes 196
  118.8 89.0 %copy-start.2 = (bf16[256,2048]{1,0:T(8,128)(2,1)S(1)}, bf16[256,2048]{1,0:T(8,128)(2,1)}, u32[]{:S(2)}) copy-start(bf16[256,2048]{1,0:T(8,128)(2,1)} %param.36) | copy-start | bytes 3145732
  118.8 24.4 %all-to-all-start.3 = ((bf16[64,33,256]{2,1,0:T(8,128)(2,1)}), bf16[64,33,256]{2,1,0:T(8,128)(2,1)}, u32[]{:S(2)}, u32[]{:S(2)}) async-start(bf16[64,33,256]{2,1,0:T(8,128)(2,1)} %broadcast_select_fusion), calls=%async_computation.3 | async-start | bytes 2621440 | tf_op jit(solution)/shard_map/all_to_all | solution.py:151
  125.9 82.0 %all-reduce.5.cloned.1.call-start = ((), (), s32[]{:S(2)}) async-start(), calls=%async_computation.7 | async-start | bytes 2097152 | tf_op jit(solution)/shard_map/psum | solution.py:176
  126.6 158.0 %all-reduce.7.cloned.1.call-start = ((), (), s32[]{:S(2)}) async-start(), calls=%async_computation.9 | async-start | bytes 2097152 | tf_op jit(solution)/shard_map/psum | solution.py:222
  209.4 122.7 %reduce-scatter.5.cloned.1.call-start = ((), (), s32[]{:S(2)}) async-start(), calls=%async_computation.10 | async-start | bytes 1179648 | tf_op jit(solution)/shard_map/reduce_scatter | solution.py:235
  209.4 75.2 %copy-start.12 = (f32[2048]{0:T(1024)S(1)}, f32[2048]{0:T(1024)}, u32[]{:S(2)}) copy-start(f32[2048]{0:T(1024)} %param.37) | copy-start | bytes 24580
  290.6 4.6 %copy-start.5 = (bf16[256,2048]{1,0:T(8,128)(2,1)S(1)}, bf16[256,2048]{1,0:T(8,128)(2,1)}, u32[]{:S(2)}) copy-start(bf16[256,2048]{1,0:T(8,128)(2,1)} %get-tuple-element.37) | copy-start | bytes 3145732
  295.1 76.8 %reduce-scatter.3.cloned.1.call-start = ((), (), s32[]{:S(2)}) async-start(), calls=%async_computation.8 | async-start | bytes 1179648 | tf_op jit(solution)/shard_map/reduce_scatter | solution.py:235
  299.2 22.0 %all-to-all-start.4 = ((bf16[64,32,256]{2,1,0:T(8,128)(2,1)}), bf16[64,32,256]{2,1,0:T(8,128)(2,1)}, u32[]{:S(2)}, u32[]{:S(2)}) async-start(bf16[64,32,256]{2,1,0:T(8,128)(2,1)} %get-tuple-element.60), calls=%async_computation.6 | async-start | bytes 2097152 | tf_op jit(solution)/shard_map/all_to_all | solution.py:151
  (15 other events, 44.2 us)
Sparse Core Ops, SparseCore 0:
  129.1 78.7 all-reduce.4
  210.2 74.3 all-reduce.6
  295.2 36.8 reduce-scatter.4
  334.5 37.3 reduce-scatter.2

commit v3 on v1

--- a/solution.py
+++ b/solution.py
@@ -140,27 +140,24 @@
     slot_ids = jnp.arange(slots_total, dtype=jnp.int32)
 
     def spread(values, index):
-        match = index[None, :] == slot_ids[:, None]
-        filled = jnp.any(match, axis=1)
-        pick = jnp.sum(jnp.where(match, local_ids[None, :], 0), axis=1)
-        taken = values[pick]
-        shape = (slots_total,) + (1,) * (values.ndim - 1)
-        return jnp.where(filled.reshape(shape), taken, jnp.zeros((), values.dtype))
-
-    arrived = (
-        lax.all_to_all(
-            spread(shaped_queries, send_index), "dp", split_axis=0, concat_axis=0, tiled=True
-        ),
-        lax.all_to_all(
-            spread(kept_keys, send_index), "dp", split_axis=0, concat_axis=0, tiled=True
-        ),
-        lax.all_to_all(
-            spread(kept_values, send_index), "dp", split_axis=0, concat_axis=0, tiled=True
-        ),
-    )
-    owned_queries = arrived[0][receive_index].reshape(requests, draft, local_heads, HD)
-    new_keys = arrived[1][receive_index]
-    new_values = arrived[2][receive_index]
+        placing = (index[None, :] == slot_ids[:, None]).astype(values.dtype)
+        flat = values.reshape(values.shape[0], -1)
+        placed = jnp.dot(placing, flat, preferred_element_type=jnp.float32).astype(values.dtype)
+        return placed.reshape((slots_total,) + values.shape[1:])
+
+    arrived = lax.all_to_all(
+        spread(shaped_queries, send_index), "dp", split_axis=0, concat_axis=0, tiled=True
+    )
+    kept = lax.all_to_all(
+        spread(jnp.concatenate([kept_keys, kept_values], axis=1), send_index),
+        "dp",
+        split_axis=0,
+        concat_axis=0,
+        tiled=True,
+    )[receive_index]
+    owned_queries = arrived[receive_index].reshape(requests, draft, local_heads, HD)
+    new_keys = kept[:, : kept_keys.shape[1]]
+    new_values = kept[:, kept_keys.shape[1] :]
     slot_keys = cache_keys.reshape(requests, capacity, local_heads, HD)
     slot_values = cache_values.reshape(requests, capacity, local_heads, HD)
     scores = (
@@ -226,9 +223,19 @@
         tiled=True,
     ).astype(jnp.float32)
     second_mixed = down_share + columns(b_down) + columns(first_normed).astype(jnp.float32)
-    second_sums = lax.psum(
-        jnp.stack([jnp.sum(second_mixed, axis=1), jnp.sum(second_mixed * second_mixed, axis=1)]),
-        "head",
+    heads_along = lax.axis_size("head")
+    own_sums = jnp.stack(
+        [jnp.sum(second_mixed, axis=1), jnp.sum(second_mixed * second_mixed, axis=1)]
+    )
+    second_sums = jnp.sum(
+        lax.all_to_all(
+            jnp.broadcast_to(own_sums[None], (heads_along,) + own_sums.shape),
+            "head",
+            0,
+            0,
+            tiled=False,
+        ),
+        axis=0,
     )
     layer_out = normalize_shared(
         second_mixed, second_sums, columns(second_gain), columns(second_shift), model_width

time: 270 us -> 266 us (0.985)
  blocking collectives: 32.6 us -> 0 us
  waiting for transfers between devices: 134 us -> 159 us
  other arithmetic: 20.5 us -> 12.9 us
  starting transfers between devices: 21.3 us -> 27.7 us
  matrix products: 25.2 us -> 28.2 us
    all_to_all x1 -> x0, blocking collectives: 16.9 us -> none  [local(): lax.all_to_all(spread(kept_values, send_index), 'dp', split_axis=0, conca...]
    psum x1 -> x0, blocking collectives: 15.7 us -> none  [local(): lax.psum(jnp.stack([jnp.sum(second_mixed, axis=1), jnp.sum(second_mixed *...]
    all_to_all x1 -> x2, waiting for transfers between devices: 6.22 us -> 19.5 us  [the longest x1 12.1 us: local(): lax.all_to_all(spread(jnp.concatenate([kept_keys, kept_values], axis=1),...]
    reduce_scatter x1, waiting for transfers between devices: 2.72 us -> 14.1 us  [local(): lax.psum_scatter(jnp.dot(inner, w_down, preferred_element_type=jnp.float3...]
    select_n x7 -> x1, other arithmetic: 7.43 us -> 0.02 us  [local(): arrived[receive_index].reshape(requests, draft, local_heads, HD)]
    gather x7 -> x2, local copies, waits for them, and re-layouts: 9.76 us -> 2.71 us  [the longest x1 2.15 us: local(): arrived[receive_index].reshape(requests, draft, local_heads, HD)]
    all_to_all x1 -> x2, starting transfers between devices: 5.56 us -> 12 us  [the longest x1 7.42 us: local(): lax.all_to_all(spread(jnp.concatenate([kept_keys, kept_values], axis=1),...]
    reshape x0 -> x1, local copies, waits for them, and re-layouts: none -> 4.3 us  [spread(): return placed.reshape((slots_total,) + values.shape[1:])]
  transfers between devices with their start and end apart: 5 -> 6, of which waited for: 5 -> 6; matrix products, arithmetic and copies ran while one was open for 8% -> 7% of each run, Pallas kernels for 0% -> 0%
where the time goes in v3:
time: 266 us; the launch traced here: 265 us
  waiting for transfers between devices  159 us (60%)
  matrix products  28.2 us (11%)
  starting transfers between devices  27.7 us (10%)
  local copies, waits for them, and re-layouts  22.4 us (8%)
  between operations  14.6 us (5%)
  other arithmetic  12.9 us (5%)
    psum x1, waiting for transfers between devices, local(): lax.psum(attention_term.astype(jnp.bfloat16), 'head').astype(jnp.float32)  83.3 us
    all_to_all x1, waiting for transfers between devices, local(): lax.all_to_all(spread(shaped_queries, send_index), 'dp', split_axis=0, co...  21.7 us
    all_to_all x1, waiting for transfers between devices, local(): lax.all_to_all(spread(back, receive_index), 'dp', split_axis=0, concat_ax...  20.6 us
    reduce_scatter x1, waiting for transfers between devices, local(): lax.psum_scatter(jnp.dot(inner, w_down, preferred_element_type=jnp.float3...  14.1 us
    all_to_all x1, waiting for transfers between devices, local(): lax.all_to_all(spread(jnp.concatenate([kept_keys, kept_values], axis=1),...  12.1 us
    all_to_all x1, starting transfers between devices, local(): lax.all_to_all(spread(shaped_queries, send_index), 'dp', split_axis=0, co...  7.81 us
    all_to_all x1, starting transfers between devices, local(): lax.all_to_all(spread(back, receive_index), 'dp', split_axis=0, concat_ax...  7.64 us
    all_to_all x1, starting transfers between devices, local(): lax.all_to_all(spread(jnp.concatenate([kept_keys, kept_values], axis=1),...  7.42 us
  transfers between devices with their start and end apart: 6, of which 6 were waited for; matrix products, arithmetic and copies ran while one was open for 7% of the time, Pallas kernels for 0%

profile of v3, /device:TPU:2, one launch (start us, length us, event | category | flops | bytes accessed | tf_op | source)
XLA Modules:
  0.0 265.1 jit_solution(1458935570208163813)
XLA Ops:
  9.0 2.6 fusion.24
  12.5 1.8 copy.76
  14.3 7.8 %all-to-all-start = ((bf16[64,64,256]{2,1,0:T(8,128)(2,1)}), bf16[64,64,256]{2,1,0:T(8,128)(2,1)}, u32[]{:S(2)}, u32[]{:S(2)}) async-start(bf16[64,64,256]{2,1,0:T(8,128)(2,1)} %bitcast.173), calls=%async_computation | async-start | bytes 4194304 | tf_op jit(solution)/shard_map/all_to_all | solution.py:148
  23.9 2.6 convolution_convert_fusion.5
  26.5 21.7 %all-to-all-done = bf16[64,64,256]{2,1,0:T(8,128)(2,1)} async-done(((bf16[64,64,256]{2,1,0:T(8,128)(2,1)}), bf16[64,64,256]{2,1,0:T(8,128)(2,1)}, u32[]{:S(2)}, u32[]{:S(2)}) %all-to-all-start) | async-done | bytes 2097184 | tf_op jit(solution)/shard_map/all_to_all | solution.py:148
  48.1 2.2 gather_fusion.1
  50.3 2.5 fusion.7
  55.6 2.0 convolution_convert_fusion
  57.6 4.3 %reshape.378 = bf16[64,66,256]{2,1,0:T(8,128)(2,1)} reshape(bf16[64,16896]{1,0:T(8,128)(2,1)} %convolution_convert_fusion) | data formatting | bytes 4325376 | tf_op jit(solution)/shard_map/reshape | solution.py:146
  61.9 7.6 %all-to-all-start.1 = ((bf16[64,66,256]{2,1,0:T(8,128)(2,1)}), bf16[64,66,256]{2,1,0:T(8,128)(2,1)}, u32[]{:S(2)}, u32[]{:S(2)}) async-start(bf16[64,66,256]{2,1,0:T(8,128)(2,1)} %reshape.378), calls=%async_computation.1 | async-start | bytes 4718592 | tf_op jit(solution)/shard_map/all_to_all | solution.py:190
  73.2 2.6 fusion.25
  77.9 20.6 %all-to-all-done.1 = bf16[64,66,256]{2,1,0:T(8,128)(2,1)} async-done(((bf16[64,66,256]{2,1,0:T(8,128)(2,1)}), bf16[64,66,256]{2,1,0:T(8,128)(2,1)}, u32[]{:S(2)}, u32[]{:S(2)}) %all-to-all-start.1) | async-done | bytes 2162720 | tf_op jit(solution)/shard_map/all_to_all | solution.py:190
  98.5 2.2 gather_fusion.2
  103.0 2.0 convolution_convert_fusion.3
  105.1 83.3 %all-reduce.3.cloned.1.call-done = bf16[512,2048]{1,0:T(8,128)(2,1)} async-done(((bf16[512,2048]{1,0:T(8,128)(2,1)}), bf16[512,2048]{1,0:T(8,128)(2,1)}) %all-reduce.3.cloned.1.call-update) | async-done | bytes 2097168 | tf_op jit(solution)/shard_map/psum | solution.py:212
  188.4 3.5 %fusion = (f32[512]{0:T(512)S(1)}, f32[512]{0:T(512)S(1)}) fusion(bf16[512,2048]{1,0:T(8,128)(2,1)} %param.23, bf16[512,2048]{1,0:T(8,128)(2,1)} %all-reduce.3.cloned.1.call-done, f32[2048]{0:T(1024)S(1)} %copy-done.4), kind=kLoop, calls=%fused_computation.12 | loop fusion | flops 7339008 | bytes 4206592 | tf_op jit(solution)/shard_map/reduce_sum | solution.py:26
  192.0 2.6 add_convert_fusion
  194.6 6.1 %convolution_convert_fusion.4 = bf16[512,2048]{1,0:T(8,128)(2,1)} fusion(bf16[512,2048]{1,0:T(8,128)(2,1)S(1)} %copy-done, bf16[512,2048]{1,0:T(8,128)(2,1)} %add_convert_fusion, bf16[2048,512]{1,0:T(8,128)(2,1)} %param.40, f32[512]{0:T(512)S(1)} %copy-done.12), kind=kOutput, calls=%fused_computation.14 | convolution fusion | flops 2151153664 | bytes 8390656 | tf_op jit(solution)/shard_map/dot_general | solution.py:220
  205.1 7.4 %all-to-all-start.3 = ((bf16[64,32,256]{2,1,0:T(8,128)(2,1)}), bf16[64,32,256]{2,1,0:T(8,128)(2,1)S(1)}, u32[]{:S(2)}, u32[]{:S(2)}) async-start(bf16[64,32,256]{2,1,0:T(8,128)(2,1)} %bitcast.49), calls=%async_computation.4 | async-start | bytes 2097152 | tf_op jit(solution)/shard_map/all_to_all | solution.py:151
  214.9 12.1 %all-to-all-done.3 = bf16[64,32,256]{2,1,0:T(8,128)(2,1)S(1)} async-done(((bf16[64,32,256]{2,1,0:T(8,128)(2,1)}), bf16[64,32,256]{2,1,0:T(8,128)(2,1)S(1)}, u32[]{:S(2)}, u32[]{:S(2)}) %all-to-all-start.3) | async-done | bytes 1048608 | tf_op jit(solution)/shard_map/all_to_all | solution.py:151
  227.6 14.1 %reduce-scatter.2.cloned.1.call-done = bf16[512,256]{1,0:T(8,128)(2,1)} async-done(((bf16[512,2048]{1,0:T(8,128)(2,1)}), bf16[512,256]{1,0:T(8,128)(2,1)}) %reduce-scatter.2.cloned.1.call-update) | async-done | bytes 262160 | tf_op jit(solution)/shard_map/reduce_scatter | solution.py:219
  243.6 4.6 %all-to-all-start.2 = ((f32[8,2,512]{2,1,0:T(2,128)}), f32[8,2,512]{2,1,0:T(2,128)S(1)}, u32[]{:S(2)}, u32[]{:S(2)}) async-start(f32[8,2,512]{2,1,0:T(2,128)} %broadcast_in_dim.71), calls=%async_computation.3 | async-start | bytes 65536 | tf_op jit(solution)/shard_map/all_to_all | solution.py:231
  248.9 7.4 %all-to-all-done.2 = f32[8,2,512]{2,1,0:T(2,128)S(1)} async-done(((f32[8,2,512]{2,1,0:T(2,128)}), f32[8,2,512]{2,1,0:T(2,128)S(1)}, u32[]{:S(2)}, u32[]{:S(2)}) %all-to-all-start.2) | async-done | bytes 32800 | tf_op jit(solution)/shard_map/all_to_all | solution.py:231
  256.3 1.9 add_convert_fusion.1
  (108 shorter events, 24.9 us)
Async XLA Ops:
  7.2 187.4 %copy-start = (bf16[512,2048]{1,0:T(8,128)(2,1)S(1)}, bf16[512,2048]{1,0:T(8,128)(2,1)}, u32[]{:S(2)}) copy-start(bf16[512,2048]{1,0:T(8,128)(2,1)} %param.42) | copy-start | bytes 6291460
  14.3 7.8 %copy-start.7 = (s32[256]{0:T(256)S(1)}, s32[256]{0:T(256)}, u32[]{:S(2)}) copy-start(s32[256]{0:T(256)} %param.25) | copy-start | bytes 3076
  14.3 9.0 %copy-start.10 = (s32[8]{0:T(128)S(1)}, s32[8]{0:T(128)}, u32[]{:S(2)}) copy-start(s32[8]{0:T(128)} %param.26) | copy-start | bytes 100
  14.3 9.0 %copy-start.8 = (s32[8,64]{1,0:T(8,128)S(1)}, s32[8,64]{1,0:T(8,128)}, u32[]{:S(2)}) copy-start(s32[8,64]{1,0:T(8,128)} %param.24) | copy-start | bytes 6148
  14.3 33.8 %all-to-all-start = ((bf16[64,64,256]{2,1,0:T(8,128)(2,1)}), bf16[64,64,256]{2,1,0:T(8,128)(2,1)}, u32[]{:S(2)}, u32[]{:S(2)}) async-start(bf16[64,64,256]{2,1,0:T(8,128)(2,1)} %bitcast.173), calls=%async_computation | async-start | bytes 4194304 | tf_op jit(solution)/shard_map/all_to_all | solution.py:148
  52.8 1.6 copy-start.11
  61.9 36.6 %all-to-all-start.1 = ((bf16[64,66,256]{2,1,0:T(8,128)(2,1)}), bf16[64,66,256]{2,1,0:T(8,128)(2,1)}, u32[]{:S(2)}, u32[]{:S(2)}) async-start(bf16[64,66,256]{2,1,0:T(8,128)(2,1)} %reshape.378), calls=%async_computation.1 | async-start | bytes 4718592 | tf_op jit(solution)/shard_map/all_to_all | solution.py:190
  69.6 118.8 %all-reduce.3.cloned.1.call-start = ((), (), s32[]{:S(2)}) async-start(), calls=%async_computation.5 | async-start | bytes 4194304 | tf_op jit(solution)/shard_map/psum | solution.py:212
  70.3 2.9 %copy-start.13 = (f32[256]{0:T(256)S(1)}, f32[256]{0:T(256)}, u32[]{:S(2)}) copy-start(f32[256]{0:T(256)} %param.35) | copy-start | bytes 3076
  100.9 2.1 copy-start.3
  103.0 85.4 %copy-start.4 = (f32[2048]{0:T(1024)S(1)}, f32[2048]{0:T(1024)}, u32[]{:S(2)}) copy-start(f32[2048]{0:T(1024)} %param.37) | copy-start | bytes 24580
  105.1 86.8 %copy-start.5 = (f32[2048]{0:T(1024)S(1)}, f32[2048]{0:T(1024)}, u32[]{:S(2)}) copy-start(f32[2048]{0:T(1024)} %param.39) | copy-start | bytes 24580
  105.1 86.8 %copy-start.6 = (f32[2048]{0:T(1024)S(1)}, f32[2048]{0:T(1024)}, u32[]{:S(2)}) copy-start(f32[2048]{0:T(1024)} %param.38) | copy-start | bytes 24580
  105.1 136.6 %reduce-scatter.2.cloned.1.call-start = ((), (), s32[]{:S(2)}) async-start(), calls=%async_computation.6 | async-start | bytes 2359296 | tf_op jit(solution)/shard_map/reduce_scatter | solution.py:219
  188.4 3.5 %copy-start.1 = (bf16[512,2048]{1,0:T(8,128)(2,1)S(1)}, bf16[512,2048]{1,0:T(8,128)(2,1)}, u32[]{:S(2)}) copy-start(bf16[512,2048]{1,0:T(8,128)(2,1)} %param.23) | copy-start | bytes 6291460
  188.4 3.5 %copy-start.2 = (bf16[512,2048]{1,0:T(8,128)(2,1)S(1)}, bf16[512,2048]{1,0:T(8,128)(2,1)}, u32[]{:S(2)}) copy-start(bf16[512,2048]{1,0:T(8,128)(2,1)} %all-reduce.3.cloned.1.call-done) | copy-start | bytes 6291460
  191.9 2.6 copy-start.12
  200.7 0.7 copy-start.9
  200.7 2.6 copy-start.14
  205.1 21.9 %all-to-all-start.3 = ((bf16[64,32,256]{2,1,0:T(8,128)(2,1)}), bf16[64,32,256]{2,1,0:T(8,128)(2,1)S(1)}, u32[]{:S(2)}, u32[]{:S(2)}) async-start(bf16[64,32,256]{2,1,0:T(8,128)(2,1)} %bitcast.49), calls=%async_computation.4 | async-start | bytes 2097152 | tf_op jit(solution)/shard_map/all_to_all | solution.py:151
  243.6 12.6 %all-to-all-start.2 = ((f32[8,2,512]{2,1,0:T(2,128)}), f32[8,2,512]{2,1,0:T(2,128)S(1)}, u32[]{:S(2)}, u32[]{:S(2)}) async-start(f32[8,2,512]{2,1,0:T(2,128)} %broadcast_in_dim.71), calls=%async_computation.3 | async-start | bytes 65536 | tf_op jit(solution)/shard_map/all_to_all | solution.py:231
Sparse Core Ops, SparseCore 0:
  105.2 83.2 all-reduce.2
  200.8 40.8 reduce-scatter.1

commit v4 on v3

--- a/solution.py
+++ b/solution.py
@@ -185,11 +185,13 @@
     lse_rows = -(-lse_flat.shape[1] // width)
     lse_flat = jnp.pad(lse_flat, ((0, 0), (0, lse_rows * width - lse_flat.shape[1])))
     back = jnp.concatenate(
-        [owned_part, lse_flat.reshape(requests, lse_rows, width)], axis=1
-    )
-    returned = lax.all_to_all(
-        spread(back, receive_index), "dp", split_axis=0, concat_axis=0, tiled=True
-    )[send_index]
+        [
+            spread(owned_part, receive_index),
+            spread(lse_flat, receive_index).reshape(slots_total, lse_rows, width),
+        ],
+        axis=1,
+    )
+    returned = lax.all_to_all(back, "dp", split_axis=0, concat_axis=0, tiled=True)[send_index]
     cache_part = returned[:, :draft]
     lse_back = returned[:, draft:].reshape(requests, -1)[:, : 3 * local_heads * draft]
     cache_lse = join_three(lse_back.reshape(requests, 3, local_heads, draft))

time: 266 us -> 266 us (level)
  other arithmetic: 12.9 us -> 16.1 us
    reshape x3 -> x1, local copies, waits for them, and re-layouts: 4.36 us -> 0.02 us  [local(): spread(lse_flat, receive_index).reshape(slots_total, lse_rows, width)]
    concatenate x0 -> x1, other arithmetic: none -> 3.22 us  [local(): jnp.concatenate([spread(owned_part, receive_index), spread(lse_flat, rece...]
where the time goes in v4:
time: 266 us; the launch traced here: 265 us
  waiting for transfers between devices  159 us (60%)
  starting transfers between devices  27.8 us (10%)
  matrix products  27 us (10%)
  local copies, waits for them, and re-layouts  20.3 us (8%)
  other arithmetic  16.1 us (6%)
  between operations  14.6 us (5%)
    psum x1, waiting for transfers between devices, local(): lax.psum(attention_term.astype(jnp.bfloat16), 'head').astype(jnp.float32)  83.3 us
    all_to_all x1, waiting for transfers between devices, local(): lax.all_to_all(spread(shaped_queries, send_index), 'dp', split_axis=0, co...  21.7 us
    all_to_all x1, waiting for transfers between devices, local(): lax.all_to_all(back, 'dp', split_axis=0, concat_axis=0, tiled=True)  20.6 us
    reduce_scatter x1, waiting for transfers between devices, local(): lax.psum_scatter(jnp.dot(inner, w_down, preferred_element_type=jnp.float3...  14.1 us
    all_to_all x1, waiting for transfers between devices, local(): lax.all_to_all(spread(jnp.concatenate([kept_keys, kept_values], axis=1),...  12.1 us
    all_to_all x1, starting transfers between devices, local(): lax.all_to_all(spread(shaped_queries, send_index), 'dp', split_axis=0, co...  7.81 us
    all_to_all x1, starting transfers between devices, local(): lax.all_to_all(back, 'dp', split_axis=0, concat_axis=0, tiled=True)  7.64 us
    all_to_all x1, starting transfers between devices, local(): lax.all_to_all(spread(jnp.concatenate([kept_keys, kept_values], axis=1),...  7.42 us
  transfers between devices with their start and end apart: 6, of which 6 were waited for; matrix products, arithmetic and copies ran while one was open for 7% of the time, Pallas kernels for 0%

profile of v4, /device:TPU:2, one launch (start us, length us, event | category | flops | bytes accessed | tf_op | source)
XLA Modules:
  0.0 265.0 jit_solution(14753216439915072856)
XLA Ops:
  9.0 2.6 fusion.24
  12.5 1.8 copy.75
  14.3 7.8 %all-to-all-start = ((bf16[64,64,256]{2,1,0:T(8,128)(2,1)}), bf16[64,64,256]{2,1,0:T(8,128)(2,1)}, u32[]{:S(2)}, u32[]{:S(2)}) async-start(bf16[64,64,256]{2,1,0:T(8,128)(2,1)} %bitcast.164), calls=%async_computation | async-start | bytes 4194304 | tf_op jit(solution)/shard_map/all_to_all | solution.py:148
  23.9 2.6 convolution_convert_fusion.5
  26.5 21.7 %all-to-all-done = bf16[64,64,256]{2,1,0:T(8,128)(2,1)} async-done(((bf16[64,64,256]{2,1,0:T(8,128)(2,1)}), bf16[64,64,256]{2,1,0:T(8,128)(2,1)}, u32[]{:S(2)}, u32[]{:S(2)}) %all-to-all-start) | async-done | bytes 2097184 | tf_op jit(solution)/shard_map/all_to_all | solution.py:148
  48.1 2.2 gather_fusion.1
  50.3 2.5 fusion.7
  56.5 1.9 copy.76
  58.6 3.2 %pad_maximum_fusion = bf16[64,66,256]{2,1,0:T(8,128)(2,1)} fusion(bf16[64,2,256]{2,1,0:T(2,128)(2,1)S(1)} %reshape.370, bf16[64,64,256]{2,1,0:T(8,128)(2,1)} %bitcast.165), kind=kLoop, calls=%fused_computation.15 | loop fusion | flops 4325376 | bytes 4325376 | tf_op jit(solution)/shard_map/concatenate | solution.py:187
  61.8 7.6 %all-to-all-start.1 = ((bf16[64,66,256]{2,1,0:T(8,128)(2,1)}), bf16[64,66,256]{2,1,0:T(8,128)(2,1)}, u32[]{:S(2)}, u32[]{:S(2)}) async-start(bf16[64,66,256]{2,1,0:T(8,128)(2,1)} %pad_maximum_fusion), calls=%async_computation.1 | async-start | bytes 4718592 | tf_op jit(solution)/shard_map/all_to_all | solution.py:194
  73.1 2.6 fusion.25
  77.8 20.6 %all-to-all-done.1 = bf16[64,66,256]{2,1,0:T(8,128)(2,1)} async-done(((bf16[64,66,256]{2,1,0:T(8,128)(2,1)}), bf16[64,66,256]{2,1,0:T(8,128)(2,1)}, u32[]{:S(2)}, u32[]{:S(2)}) %all-to-all-start.1) | async-done | bytes 2162720 | tf_op jit(solution)/shard_map/all_to_all | solution.py:194
  98.4 2.2 gather_fusion.2
  102.9 2.0 convolution_convert_fusion.3
  105.0 83.3 %all-reduce.3.cloned.1.call-done = bf16[512,2048]{1,0:T(8,128)(2,1)} async-done(((bf16[512,2048]{1,0:T(8,128)(2,1)}), bf16[512,2048]{1,0:T(8,128)(2,1)}) %all-reduce.3.cloned.1.call-update) | async-done | bytes 2097168 | tf_op jit(solution)/shard_map/psum | solution.py:214
  188.3 3.5 %fusion = (f32[512]{0:T(512)S(1)}, f32[512]{0:T(512)S(1)}) fusion(bf16[512,2048]{1,0:T(8,128)(2,1)} %param.23, bf16[512,2048]{1,0:T(8,128)(2,1)} %all-reduce.3.cloned.1.call-done, f32[2048]{0:T(1024)S(1)} %copy-done.4), kind=kLoop, calls=%fused_computation.12 | loop fusion | flops 7339008 | bytes 4206592 | tf_op jit(solution)/shard_map/reduce_sum | solution.py:26
  191.8 2.6 add_convert_fusion
  194.5 6.1 %convolution_convert_fusion.4 = bf16[512,2048]{1,0:T(8,128)(2,1)} fusion(bf16[512,2048]{1,0:T(8,128)(2,1)S(1)} %copy-done, bf16[512,2048]{1,0:T(8,128)(2,1)} %add_convert_fusion, bf16[2048,512]{1,0:T(8,128)(2,1)} %param.40, f32[512]{0:T(512)S(1)} %copy-done.12), kind=kOutput, calls=%fused_computation.14 | convolution fusion | flops 2151153664 | bytes 8390656 | tf_op jit(solution)/shard_map/dot_general | solution.py:222
  205.0 7.4 %all-to-all-start.3 = ((bf16[64,32,256]{2,1,0:T(8,128)(2,1)}), bf16[64,32,256]{2,1,0:T(8,128)(2,1)S(1)}, u32[]{:S(2)}, u32[]{:S(2)}) async-start(bf16[64,32,256]{2,1,0:T(8,128)(2,1)} %bitcast.47), calls=%async_computation.4 | async-start | bytes 2097152 | tf_op jit(solution)/shard_map/all_to_all | solution.py:151
  214.7 12.1 %all-to-all-done.3 = bf16[64,32,256]{2,1,0:T(8,128)(2,1)S(1)} async-done(((bf16[64,32,256]{2,1,0:T(8,128)(2,1)}), bf16[64,32,256]{2,1,0:T(8,128)(2,1)S(1)}, u32[]{:S(2)}, u32[]{:S(2)}) %all-to-all-start.3) | async-done | bytes 1048608 | tf_op jit(solution)/shard_map/all_to_all | solution.py:151
  227.5 14.1 %reduce-scatter.2.cloned.1.call-done = bf16[512,256]{1,0:T(8,128)(2,1)} async-done(((bf16[512,2048]{1,0:T(8,128)(2,1)}), bf16[512,256]{1,0:T(8,128)(2,1)}) %reduce-scatter.2.cloned.1.call-update) | async-done | bytes 262160 | tf_op jit(solution)/shard_map/reduce_scatter | solution.py:221
  243.5 4.7 %all-to-all-start.2 = ((f32[8,2,512]{2,1,0:T(2,128)}), f32[8,2,512]{2,1,0:T(2,128)S(1)}, u32[]{:S(2)}, u32[]{:S(2)}) async-start(f32[8,2,512]{2,1,0:T(2,128)} %broadcast_in_dim.71), calls=%async_computation.3 | async-start | bytes 65536 | tf_op jit(solution)/shard_map/all_to_all | solution.py:233
  248.8 7.4 %all-to-all-done.2 = f32[8,2,512]{2,1,0:T(2,128)S(1)} async-done(((f32[8,2,512]{2,1,0:T(2,128)}), f32[8,2,512]{2,1,0:T(2,128)S(1)}, u32[]{:S(2)}, u32[]{:S(2)}) %all-to-all-start.2) | async-done | bytes 32800 | tf_op jit(solution)/shard_map/all_to_all | solution.py:233
  256.3 1.9 add_convert_fusion.1
  (108 shorter events, 26.0 us)
Async XLA Ops:
  7.2 187.3 %copy-start = (bf16[512,2048]{1,0:T(8,128)(2,1)S(1)}, bf16[512,2048]{1,0:T(8,128)(2,1)}, u32[]{:S(2)}) copy-start(bf16[512,2048]{1,0:T(8,128)(2,1)} %param.42) | copy-start | bytes 6291460
  14.3 7.8 %copy-start.7 = (s32[256]{0:T(256)S(1)}, s32[256]{0:T(256)}, u32[]{:S(2)}) copy-start(s32[256]{0:T(256)} %param.25) | copy-start | bytes 3076
  14.3 9.0 %copy-start.10 = (s32[8]{0:T(128)S(1)}, s32[8]{0:T(128)}, u32[]{:S(2)}) copy-start(s32[8]{0:T(128)} %param.26) | copy-start | bytes 100
  14.3 9.0 %copy-start.8 = (s32[8,64]{1,0:T(8,128)S(1)}, s32[8,64]{1,0:T(8,128)}, u32[]{:S(2)}) copy-start(s32[8,64]{1,0:T(8,128)} %param.24) | copy-start | bytes 6148
  14.3 33.8 %all-to-all-start = ((bf16[64,64,256]{2,1,0:T(8,128)(2,1)}), bf16[64,64,256]{2,1,0:T(8,128)(2,1)}, u32[]{:S(2)}, u32[]{:S(2)}) async-start(bf16[64,64,256]{2,1,0:T(8,128)(2,1)} %bitcast.164), calls=%async_computation | async-start | bytes 4194304 | tf_op jit(solution)/shard_map/all_to_all | solution.py:148
  52.8 1.6 copy-start.11
  61.8 36.6 %all-to-all-start.1 = ((bf16[64,66,256]{2,1,0:T(8,128)(2,1)}), bf16[64,66,256]{2,1,0:T(8,128)(2,1)}, u32[]{:S(2)}, u32[]{:S(2)}) async-start(bf16[64,66,256]{2,1,0:T(8,128)(2,1)} %pad_maximum_fusion), calls=%async_computation.1 | async-start | bytes 4718592 | tf_op jit(solution)/shard_map/all_to_all | solution.py:194
  69.5 118.8 %all-reduce.3.cloned.1.call-start = ((), (), s32[]{:S(2)}) async-start(), calls=%async_computation.5 | async-start | bytes 4194304 | tf_op jit(solution)/shard_map/psum | solution.py:214
  70.2 2.9 %copy-start.13 = (f32[256]{0:T(256)S(1)}, f32[256]{0:T(256)}, u32[]{:S(2)}) copy-start(f32[256]{0:T(256)} %param.35) | copy-start | bytes 3076
  100.8 2.1 copy-start.3
  102.9 85.4 %copy-start.4 = (f32[2048]{0:T(1024)S(1)}, f32[2048]{0:T(1024)}, u32[]{:S(2)}) copy-start(f32[2048]{0:T(1024)} %param.37) | copy-start | bytes 24580
  104.9 86.9 %copy-start.5 = (f32[2048]{0:T(1024)S(1)}, f32[2048]{0:T(1024)}, u32[]{:S(2)}) copy-start(f32[2048]{0:T(1024)} %param.39) | copy-start | bytes 24580
  105.0 86.8 %copy-start.6 = (f32[2048]{0:T(1024)S(1)}, f32[2048]{0:T(1024)}, u32[]{:S(2)}) copy-start(f32[2048]{0:T(1024)} %param.38) | copy-start | bytes 24580
  105.0 136.6 %reduce-scatter.2.cloned.1.call-start = ((), (), s32[]{:S(2)}) async-start(), calls=%async_computation.6 | async-start | bytes 2359296 | tf_op jit(solution)/shard_map/reduce_scatter | solution.py:221
  188.3 3.5 %copy-start.1 = (bf16[512,2048]{1,0:T(8,128)(2,1)S(1)}, bf16[512,2048]{1,0:T(8,128)(2,1)}, u32[]{:S(2)}) copy-start(bf16[512,2048]{1,0:T(8,128)(2,1)} %param.23) | copy-start | bytes 6291460
  188.3 3.5 %copy-start.2 = (bf16[512,2048]{1,0:T(8,128)(2,1)S(1)}, bf16[512,2048]{1,0:T(8,128)(2,1)}, u32[]{:S(2)}) copy-start(bf16[512,2048]{1,0:T(8,128)(2,1)} %all-reduce.3.cloned.1.call-done) | copy-start | bytes 6291460
  191.8 2.6 copy-start.12
  200.5 0.7 copy-start.9
  200.5 2.6 copy-start.14
  205.0 21.9 %all-to-all-start.3 = ((bf16[64,32,256]{2,1,0:T(8,128)(2,1)}), bf16[64,32,256]{2,1,0:T(8,128)(2,1)S(1)}, u32[]{:S(2)}, u32[]{:S(2)}) async-start(bf16[64,32,256]{2,1,0:T(8,128)(2,1)} %bitcast.47), calls=%async_computation.4 | async-start | bytes 2097152 | tf_op jit(solution)/shard_map/all_to_all | solution.py:151
  243.5 12.7 %all-to-all-start.2 = ((f32[8,2,512]{2,1,0:T(2,128)}), f32[8,2,512]{2,1,0:T(2,128)S(1)}, u32[]{:S(2)}, u32[]{:S(2)}) async-start(f32[8,2,512]{2,1,0:T(2,128)} %broadcast_in_dim.71), calls=%async_computation.3 | async-start | bytes 65536 | tf_op jit(solution)/shard_map/all_to_all | solution.py:233
Sparse Core Ops, SparseCore 0:
  105.1 83.2 all-reduce.2
  200.7 40.8 reduce-scatter.1

commit v5 on v4

--- a/solution.py
+++ b/solution.py
@@ -3,6 +3,7 @@
 import jax
 import jax.numpy as jnp
 from jax import lax
+from jax.experimental import pallas as pl
 from jax.sharding import PartitionSpec as P
 
 HD = 128
@@ -45,6 +46,40 @@
 def join_three(pieces):
     wide = pieces.astype(jnp.float32)
     return wide[:, 0] + (wide[:, 1] + wide[:, 2])
+
+
+def ffn_block(attn_ref, hid_ref, bout_ref, gain_ref, shift_ref, wup_ref, bup_ref, wdown_ref, normed_ref, down_ref):
+    mixed = attn_ref[...].astype(jnp.float32) + bout_ref[...] + hid_ref[...].astype(jnp.float32)
+    center = jnp.mean(mixed, axis=-1, keepdims=True)
+    square = jnp.mean(mixed * mixed, axis=-1, keepdims=True)
+    normed = ((mixed - center) * lax.rsqrt(square - center * center + EPSILON) * gain_ref[...] + shift_ref[...]).astype(jnp.bfloat16)
+    normed_ref[...] = normed
+    raised = jnp.dot(normed, wup_ref[...], preferred_element_type=jnp.float32) + bup_ref[...]
+    inner = jax.nn.gelu(raised, approximate=True).astype(jnp.bfloat16)
+    down_ref[...] = jnp.dot(inner, wdown_ref[...], preferred_element_type=jnp.float32).astype(jnp.bfloat16)
+
+def feed_forward(attn, hidden, b_out, gain, shift, w_up, b_up, w_down, block=128):
+    tokens, model = hidden.shape
+    units = w_up.shape[1]
+    row = lambda i: (i, 0)
+    fixed = lambda i: (0, 0)
+    return pl.pallas_call(
+        ffn_block,
+        grid=(tokens // block,),
+        in_specs=[
+            pl.BlockSpec((block, model), row),
+            pl.BlockSpec((block, model), row),
+            pl.BlockSpec((1, model), fixed),
+            pl.BlockSpec((1, model), fixed),
+            pl.BlockSpec((1, model), fixed),
+            pl.BlockSpec((model, units), fixed),
+            pl.BlockSpec((1, units), fixed),
+            pl.BlockSpec((units, model), fixed),
+        ],
+        out_specs=[pl.BlockSpec((block, model), row), pl.BlockSpec((block, model), row)],
+        out_shape=[jax.ShapeDtypeStruct((tokens, model), jnp.bfloat16)] * 2,
+        cost_estimate=pl.CostEstimate(flops=4 * tokens * model * units, transcendentals=tokens * units, bytes_accessed=2 * (4 * tokens * model + 2 * model * units)),
+    )(attn, hidden, b_out.reshape(1, -1), gain.reshape(1, -1), shift.reshape(1, -1), w_up, b_up.reshape(1, -1), w_down)
 
 
 def local(
@@ -211,18 +246,12 @@
     def columns(values):
         return lax.dynamic_slice_in_dim(values, offset, feature, values.ndim - 1)
 
-    attention_sum = lax.psum(attention_term.astype(jnp.bfloat16), "head").astype(jnp.float32)
-    first_normed = normalize(
-        attention_sum + b_out + hidden.astype(jnp.float32), first_gain, first_shift
-    ).astype(jnp.bfloat16)
-    inner = jax.nn.gelu(
-        jnp.dot(first_normed, w_up, preferred_element_type=jnp.float32) + b_up, approximate=True
-    ).astype(jnp.bfloat16)
+    attention_sum = lax.psum(attention_term.astype(jnp.bfloat16), "head")
+    first_normed, down_part = feed_forward(
+        attention_sum, hidden, b_out, first_gain, first_shift, w_up, b_up, w_down
+    )
     down_share = lax.psum_scatter(
-        jnp.dot(inner, w_down, preferred_element_type=jnp.float32).astype(jnp.bfloat16),
-        "head",
-        scatter_dimension=1,
-        tiled=True,
+        down_part, "head", scatter_dimension=1, tiled=True
     ).astype(jnp.float32)
     second_mixed = down_share + columns(b_down) + columns(first_normed).astype(jnp.float32)
     heads_along = lax.axis_size("head")

time: 266 us -> 258 us (0.970)
  Pallas kernels: 0 us -> 8.51 us
  other arithmetic: 16.1 us -> 8.41 us
  matrix products: 27 us -> 19.4 us
    pallas_call x0 -> x1, Pallas kernels: none -> 8.51 us  [feed_forward(): pl.pallas_call(ffn_block, grid=(tokens // block,), in_specs=[pl.BlockSpec...]
    dot_general x1 -> x0, matrix products: 6.08 us -> none  [local(): jnp.dot(inner, w_down, preferred_element_type=jnp.float32)]
    reduce_sum x1 -> x0, other arithmetic: 3.45 us -> none  [normalize(): center = jnp.mean(mixed, axis=-1, keepdims=True)]
    unnamed x36 -> x24, local copies, waits for them, and re-layouts: 6.6 us -> 5.25 us
  transfers between devices with their start and end apart: 6 -> 6, of which waited for: 6 -> 6; matrix products, arithmetic and copies ran while one was open for 7% -> 8% of each run, Pallas kernels for 0% -> 0%
where the time goes in v5:
time: 258 us; the launch traced here: 257 us
  waiting for transfers between devices  159 us (62%)
  starting transfers between devices  27.8 us (11%)
  matrix products  19.4 us (8%)
  local copies, waits for them, and re-layouts  19 us (7%)
  between operations  14.5 us (6%)
  Pallas kernels  8.51 us (3%)
  other arithmetic  8.41 us (3%)
    psum x1, waiting for transfers between devices, local(): attention_sum = lax.psum(attention_term.astype(jnp.bfloat16), 'head')  83.3 us
    all_to_all x1, waiting for transfers between devices, local(): lax.all_to_all(spread(shaped_queries, send_index), 'dp', split_axis=0, co...  23.9 us
    all_to_all x1, waiting for transfers between devices, local(): lax.all_to_all(back, 'dp', split_axis=0, concat_axis=0, tiled=True)  18.4 us
    reduce_scatter x1, waiting for transfers between devices, local(): lax.psum_scatter(down_part, 'head', scatter_dimension=1, tiled=True)  14.1 us
    all_to_all x1, waiting for transfers between devices, local(): lax.all_to_all(spread(jnp.concatenate([kept_keys, kept_values], axis=1),...  12.1 us
    pallas_call x1, Pallas kernels, feed_forward(): pl.pallas_call(ffn_block, grid=(tokens // block,), in_specs=[pl.BlockSpec...  8.51 us
    all_to_all x1, starting transfers between devices, local(): lax.all_to_all(spread(shaped_queries, send_index), 'dp', split_axis=0, co...  7.81 us
    all_to_all x1, starting transfers between devices, local(): lax.all_to_all(back, 'dp', split_axis=0, concat_axis=0, tiled=True)  7.62 us
  transfers between devices with their start and end apart: 6, of which 6 were waited for; matrix products, arithmetic and copies ran while one was open for 8% of the time, Pallas kernels for 0%

profile of v5, /device:TPU:2, one launch (start us, length us, event | category | flops | bytes accessed | tf_op | source)
XLA Modules:
  0.0 256.9 jit_solution(7738962741900420424)
XLA Ops:
  9.0 2.6 %fusion.23 = bf16[512,256]{1,0:T(8,128)(2,1)S(1)} fusion(bf16[512,2048]{1,0:T(8,128)(2,1)} %hid_ref.1, bf16[2048,256]{1,0:T(8,128)(2,1)} %param.31, f32[256]{0:T(256)} %param.32), kind=kOutput, calls=%fused_computation.34 | convolution fusion | flops 537133056 | bytes 3408896 | tf_op jit(solution)/shard_map/dot_general | solution.py:121
  12.5 1.8 copy.75
  14.3 7.8 %all-to-all-start = ((bf16[64,64,256]{2,1,0:T(8,128)(2,1)}), bf16[64,64,256]{2,1,0:T(8,128)(2,1)}, u32[]{:S(2)}, u32[]{:S(2)}) async-start(bf16[64,64,256]{2,1,0:T(8,128)(2,1)} %bitcast.165), calls=%async_computation | async-start | bytes 4194304 | tf_op jit(solution)/shard_map/all_to_all | solution.py:183
  24.3 23.9 %all-to-all-done = bf16[64,64,256]{2,1,0:T(8,128)(2,1)} async-done(((bf16[64,64,256]{2,1,0:T(8,128)(2,1)}), bf16[64,64,256]{2,1,0:T(8,128)(2,1)}, u32[]{:S(2)}, u32[]{:S(2)}) %all-to-all-start) | async-done | bytes 2097184 | tf_op jit(solution)/shard_map/all_to_all | solution.py:183
  48.1 2.2 gather_fusion.1
  55.7 1.6 pad_maximum_fusion
  57.4 7.6 %all-to-all-start.1 = ((bf16[64,66,256]{2,1,0:T(8,128)(2,1)}), bf16[64,66,256]{2,1,0:T(8,128)(2,1)}, u32[]{:S(2)}, u32[]{:S(2)}) async-start(bf16[64,66,256]{2,1,0:T(8,128)(2,1)} %pad_maximum_fusion), calls=%async_computation.1 | async-start | bytes 4718592 | tf_op jit(solution)/shard_map/all_to_all | solution.py:229
  67.5 2.6 %convolution_convert_fusion.4 = bf16[512,256]{1,0:T(8,128)(2,1)S(1)} fusion(bf16[512,2048]{1,0:T(8,128)(2,1)} %hid_ref.1, bf16[2048,256]{1,0:T(8,128)(2,1)} %param.33), kind=kOutput, calls=%fused_computation.37 | convolution fusion | flops 537001984 | bytes 3407872 | tf_op jit(solution)/shard_map/dot_general | solution.py:124
  70.8 2.6 fusion.24
  74.2 1.2 fusion.73
  75.5 18.4 %all-to-all-done.1 = bf16[64,66,256]{2,1,0:T(8,128)(2,1)} async-done(((bf16[64,66,256]{2,1,0:T(8,128)(2,1)}), bf16[64,66,256]{2,1,0:T(8,128)(2,1)}, u32[]{:S(2)}, u32[]{:S(2)}) %all-to-all-start.1) | async-done | bytes 2162720 | tf_op jit(solution)/shard_map/all_to_all | solution.py:229
  93.9 2.2 gather_fusion.2
  96.4 1.8 fusion.25
  98.4 2.1 convolution_convert_fusion.3
  100.6 83.3 %all-reduce.3.cloned.1.call-done.attn_ref = bf16[512,2048]{1,0:T(8,128)(2,1)} async-done(((bf16[512,2048]{1,0:T(8,128)(2,1)}), bf16[512,2048]{1,0:T(8,128)(2,1)}) %all-reduce.3.cloned.1.call-update) | async-done | bytes 2097168 | tf_op jit(solution)/shard_map/psum | solution.py:249
  183.9 8.5 %shard_map.238 = (bf16[512,2048]{1,0:T(8,128)(2,1)}, bf16[512,2048]{1,0:T(8,128)(2,1)}) custom-call(bf16[512,2048]{1,0:T(8,128)(2,1)} %all-reduce.3.cloned.1.call-done.attn_ref, bf16[512,2048]{1,0:T(8,128)(2,1)} %hid_ref.1, f32[1,2048]{1,0:T(1,128)} %bitcast.180, f32[1,2048]{1,0:T(1,128)} %bitcast.181, f32[1,2048]{1,0:T(1,128)} %bitcast.182, ...), custom_call_target="tpu_custom_call" | custom-call | flops 2147483648 | bytes 12582912 | tf_op jit(solution)/shard_map/pallas_call | solution.py:66
  195.6 1.2 copy.80
  196.9 7.4 %all-to-all-start.3 = ((bf16[64,32,256]{2,1,0:T(8,128)(2,1)}), bf16[64,32,256]{2,1,0:T(8,128)(2,1)S(1)}, u32[]{:S(2)}, u32[]{:S(2)}) async-start(bf16[64,32,256]{2,1,0:T(8,128)(2,1)} %bitcast.51), calls=%async_computation.4 | async-start | bytes 2097152 | tf_op jit(solution)/shard_map/all_to_all | solution.py:186
  206.6 12.1 %all-to-all-done.3 = bf16[64,32,256]{2,1,0:T(8,128)(2,1)S(1)} async-done(((bf16[64,32,256]{2,1,0:T(8,128)(2,1)}), bf16[64,32,256]{2,1,0:T(8,128)(2,1)S(1)}, u32[]{:S(2)}, u32[]{:S(2)}) %all-to-all-start.3) | async-done | bytes 1048608 | tf_op jit(solution)/shard_map/all_to_all | solution.py:186
  219.3 14.1 %reduce-scatter.2.cloned.1.call-done = bf16[512,256]{1,0:T(8,128)(2,1)} async-done(((bf16[512,2048]{1,0:T(8,128)(2,1)}), bf16[512,256]{1,0:T(8,128)(2,1)}) %reduce-scatter.2.cloned.1.call-update) | async-done | bytes 262160 | tf_op jit(solution)/shard_map/reduce_scatter | solution.py:253
  233.4 1.3 fusion.34
  235.3 4.7 %all-to-all-start.2 = ((f32[8,2,512]{2,1,0:T(2,128)}), f32[8,2,512]{2,1,0:T(2,128)S(1)}, u32[]{:S(2)}, u32[]{:S(2)}) async-start(f32[8,2,512]{2,1,0:T(2,128)} %broadcast_in_dim.71), calls=%async_computation.3 | async-start | bytes 65536 | tf_op jit(solution)/shard_map/all_to_all | solution.py:262
  240.7 7.4 %all-to-all-done.2 = f32[8,2,512]{2,1,0:T(2,128)S(1)} async-done(((f32[8,2,512]{2,1,0:T(2,128)}), f32[8,2,512]{2,1,0:T(2,128)S(1)}, u32[]{:S(2)}, u32[]{:S(2)}) %all-to-all-start.2) | async-done | bytes 32800 | tf_op jit(solution)/shard_map/all_to_all | solution.py:262
  248.1 1.9 add_convert_fusion
  (93 shorter events, 22.0 us)
Async XLA Ops:
  7.2 43.1 %copy-start = (bf16[8,512,256]{2,1,0:T(8,128)(2,1)S(1)}, bf16[8,512,256]{2,1,0:T(8,128)(2,1)}, u32[]{:S(2)}) copy-start(bf16[8,512,256]{2,1,0:T(8,128)(2,1)} %param.29) | copy-start | bytes 6291460
  14.3 7.8 %copy-start.2 = (s32[256]{0:T(256)S(1)}, s32[256]{0:T(256)}, u32[]{:S(2)}) copy-start(s32[256]{0:T(256)} %param.25) | copy-start | bytes 3076
  14.3 9.0 %copy-start.5 = (s32[8]{0:T(128)S(1)}, s32[8]{0:T(128)}, u32[]{:S(2)}) copy-start(s32[8]{0:T(128)} %param.26) | copy-start | bytes 100
  14.3 9.0 %copy-start.3 = (s32[8,64]{1,0:T(8,128)S(1)}, s32[8,64]{1,0:T(8,128)}, u32[]{:S(2)}) copy-start(s32[8,64]{1,0:T(8,128)} %param.24) | copy-start | bytes 6148
  14.3 33.8 %all-to-all-start = ((bf16[64,64,256]{2,1,0:T(8,128)(2,1)}), bf16[64,64,256]{2,1,0:T(8,128)(2,1)}, u32[]{:S(2)}, u32[]{:S(2)}) async-start(bf16[64,64,256]{2,1,0:T(8,128)(2,1)} %bitcast.165), calls=%async_computation | async-start | bytes 4194304 | tf_op jit(solution)/shard_map/all_to_all | solution.py:183
  51.3 1.6 copy-start.6
  57.4 36.6 %all-to-all-start.1 = ((bf16[64,66,256]{2,1,0:T(8,128)(2,1)}), bf16[64,66,256]{2,1,0:T(8,128)(2,1)}, u32[]{:S(2)}, u32[]{:S(2)}) async-start(bf16[64,66,256]{2,1,0:T(8,128)(2,1)} %pad_maximum_fusion), calls=%async_computation.1 | async-start | bytes 4718592 | tf_op jit(solution)/shard_map/all_to_all | solution.py:229
  65.0 118.9 %all-reduce.3.cloned.1.call-start = ((), (), s32[]{:S(2)}) async-start(), calls=%async_computation.5 | async-start | bytes 4194304 | tf_op jit(solution)/shard_map/psum | solution.py:249
  67.4 3.4 %copy-start.7 = (f32[256]{0:T(256)S(1)}, f32[256]{0:T(256)}, u32[]{:S(2)}) copy-start(f32[256]{0:T(256)} %param.35) | copy-start | bytes 3076
  96.3 2.1 copy-start.1
  100.5 132.9 %reduce-scatter.2.cloned.1.call-start = ((), (), s32[]{:S(2)}) async-start(), calls=%async_computation.6 | async-start | bytes 2359296 | tf_op jit(solution)/shard_map/reduce_scatter | solution.py:253
  192.4 0.7 copy-start.4
  192.4 2.6 copy-start.8
  196.9 21.9 %all-to-all-start.3 = ((bf16[64,32,256]{2,1,0:T(8,128)(2,1)}), bf16[64,32,256]{2,1,0:T(8,128)(2,1)S(1)}, u32[]{:S(2)}, u32[]{:S(2)}) async-start(bf16[64,32,256]{2,1,0:T(8,128)(2,1)} %bitcast.51), calls=%async_computation.4 | async-start | bytes 2097152 | tf_op jit(solution)/shard_map/all_to_all | solution.py:186
  235.3 12.8 %all-to-all-start.2 = ((f32[8,2,512]{2,1,0:T(2,128)}), f32[8,2,512]{2,1,0:T(2,128)S(1)}, u32[]{:S(2)}, u32[]{:S(2)}) async-start(f32[8,2,512]{2,1,0:T(2,128)} %broadcast_in_dim.71), calls=%async_computation.3 | async-start | bytes 65536 | tf_op jit(solution)/shard_map/all_to_all | solution.py:262
Sparse Core Ops, SparseCore 0:
  100.6 83.2 all-reduce.2
  192.5 40.8 reduce-scatter.1

commit v6 on v5

--- a/solution.py
+++ b/solution.py
@@ -4,6 +4,7 @@
 import jax.numpy as jnp
 from jax import lax
 from jax.experimental import pallas as pl
+from jax.experimental.pallas import tpu as pltpu
 from jax.sharding import PartitionSpec as P
 
 HD = 128
@@ -33,19 +34,6 @@
     center = (sums[0] / model_width)[:, None]
     square = (sums[1] / model_width)[:, None]
     return (mixed - center) * lax.rsqrt(square - center * center + EPSILON) * gain + shift
-
-
-def split_three(values):
-    high = values.astype(jnp.bfloat16)
-    rest = values - high.astype(jnp.float32)
-    middle = rest.astype(jnp.bfloat16)
-    low = (rest - middle.astype(jnp.float32)).astype(jnp.bfloat16)
-    return jnp.stack([high, middle, low], axis=1)
-
-
-def join_three(pieces):
-    wide = pieces.astype(jnp.float32)
-    return wide[:, 0] + (wide[:, 1] + wide[:, 2])
 
 
 def ffn_block(attn_ref, hid_ref, bout_ref, gain_ref, shift_ref, wup_ref, bup_ref, wdown_ref, normed_ref, down_ref):
@@ -80,6 +68,58 @@
         out_shape=[jax.ShapeDtypeStruct((tokens, model), jnp.bfloat16)] * 2,
         cost_estimate=pl.CostEstimate(flops=4 * tokens * model * units, transcendentals=tokens * units, bytes_accessed=2 * (4 * tokens * model + 2 * model * units)),
     )(attn, hidden, b_out.reshape(1, -1), gain.reshape(1, -1), shift.reshape(1, -1), w_up, b_up.reshape(1, -1), w_down)
+
+
+def attend_block(where_ref, length_ref, query_ref, key_ref, value_ref, back_ref):
+    slot = pl.program_id(0)
+    length = length_ref[slot]
+    draft = query_ref.shape[1]
+    heads = query_ref.shape[2] // HD
+    width = query_ref.shape[2]
+    capacity = key_ref.shape[1]
+    living = lax.broadcasted_iota(jnp.int32, (draft, capacity), 1) < length
+    back_ref[0, draft:, :] = jnp.zeros((back_ref.shape[1] - draft, width), back_ref.dtype)
+    for head in range(heads):
+        cols = slice(head * HD, (head + 1) * HD)
+        query = query_ref[0, :, cols]
+        scores = lax.dot_general(
+            query, key_ref[0, :, cols], (((1,), (1,)), ((), ())), preferred_element_type=jnp.float32
+        ) * (1.0 / math.sqrt(HD))
+        scores = jnp.where(living, scores, -jnp.inf)
+        top = jnp.max(scores, axis=1, keepdims=True)
+        weights = jnp.exp(scores - top)
+        total = jnp.sum(weights, axis=1, keepdims=True)
+        mixed = jnp.dot(weights.astype(jnp.bfloat16), value_ref[0, :, cols], preferred_element_type=jnp.float32)
+        back_ref[0, :draft, cols] = (mixed / total).astype(back_ref.dtype)
+        lse = jnp.broadcast_to(top + jnp.log(total), (draft, 128)).T[0:1, :draft]
+        high = lse.astype(jnp.bfloat16)
+        rest = lse - high.astype(jnp.float32)
+        middle = rest.astype(jnp.bfloat16)
+        low = (rest - middle.astype(jnp.float32)).astype(jnp.bfloat16)
+        back_ref[0, draft + head : draft + head + 1, 0:draft] = high
+        back_ref[0, draft + head : draft + head + 1, draft : 2 * draft] = middle
+        back_ref[0, draft + head : draft + head + 1, 2 * draft : 3 * draft] = low
+
+def attend(arrived, where, lengths, keys, values):
+    positions, draft, width = arrived.shape
+    slots, capacity, _ = keys.shape
+    heads = width // HD
+    rows = draft + heads
+    grid_spec = pltpu.PrefetchScalarGridSpec(
+        num_scalar_prefetch=2,
+        grid=(slots,),
+        in_specs=[
+            pl.BlockSpec((1, draft, width), lambda s, w, n: (w[s], 0, 0)),
+            pl.BlockSpec((1, capacity, width), lambda s, w, n: (s, 0, 0)),
+            pl.BlockSpec((1, capacity, width), lambda s, w, n: (s, 0, 0)),
+        ],
+        out_specs=pl.BlockSpec((1, rows, width), lambda s, w, n: (w[s], 0, 0)),
+    )
+    return pl.pallas_call(
+        attend_block,
+        grid_spec=grid_spec,
+        out_shape=jax.ShapeDtypeStruct((positions, rows, width), arrived.dtype),
+    )(where, lengths, arrived, keys, values)
 
 
 def local(
@@ -190,46 +230,15 @@
         concat_axis=0,
         tiled=True,
     )[receive_index]
-    owned_queries = arrived[receive_index].reshape(requests, draft, local_heads, HD)
     new_keys = kept[:, : kept_keys.shape[1]]
     new_values = kept[:, kept_keys.shape[1] :]
-    slot_keys = cache_keys.reshape(requests, capacity, local_heads, HD)
-    slot_values = cache_values.reshape(requests, capacity, local_heads, HD)
-    scores = (
-        jnp.einsum(
-            "sqhd,skhd->shqk", owned_queries, slot_keys, preferred_element_type=jnp.float32
-        )
-        * scale
-    )
-    living = jnp.arange(capacity, dtype=jnp.int32)[None, :] < slot_lengths[:, None]
-    scores = jnp.where(living[:, None, None, :], scores, -jnp.inf)
-    cache_top = jnp.max(scores, axis=3, keepdims=True)
-    cache_exp = jnp.exp(scores - cache_top)
-    cache_total = jnp.sum(cache_exp, axis=3, keepdims=True)
-    cache_probs = cache_exp.astype(jnp.bfloat16)
-    gathered = jnp.einsum(
-        "shqk,skhd->sqhd", cache_probs, slot_values, preferred_element_type=jnp.float32
-    )
-    owned_part = (
-        (gathered / jnp.transpose(cache_total, (0, 2, 1, 3)))
-        .astype(jnp.bfloat16)
-        .reshape(requests, draft, width)
-    )
-    owned_lse = (cache_top + jnp.log(cache_total))[..., 0]
-    lse_flat = split_three(owned_lse).reshape(requests, -1)
-    lse_rows = -(-lse_flat.shape[1] // width)
-    lse_flat = jnp.pad(lse_flat, ((0, 0), (0, lse_rows * width - lse_flat.shape[1])))
-    back = jnp.concatenate(
-        [
-            spread(owned_part, receive_index),
-            spread(lse_flat, receive_index).reshape(slots_total, lse_rows, width),
-        ],
-        axis=1,
-    )
+    back = attend(arrived, receive_index, slot_lengths, cache_keys, cache_values)
     returned = lax.all_to_all(back, "dp", split_axis=0, concat_axis=0, tiled=True)[send_index]
     cache_part = returned[:, :draft]
-    lse_back = returned[:, draft:].reshape(requests, -1)[:, : 3 * local_heads * draft]
-    cache_lse = join_three(lse_back.reshape(requests, 3, local_heads, draft))
+    lse_rows = returned[:, draft : draft + local_heads].astype(jnp.float32)
+    cache_lse = lse_rows[..., :draft] + (
+        lse_rows[..., draft : 2 * draft] + lse_rows[..., 2 * draft : 3 * draft]
+    )
     cache_weight = jnp.transpose(cache_lse, (0, 2, 1))[..., None]
     larger = jnp.maximum(cache_weight, tree_lse)
     cache_share = jnp.exp(cache_weight - larger)

time: 258 us -> 258 us (level)
  waiting for transfers between devices: 159 us -> 149 us
  Pallas kernels: 8.51 us -> 17.8 us
    pallas_call x0 -> x1, Pallas kernels: none -> 9.27 us  [attend(): pl.pallas_call(attend_block, grid_spec=grid_spec, out_shape=jax.ShapeDtyp...]
    all_to_all x1, waiting for transfers between devices: 18.4 us -> 9.94 us  [local(): lax.all_to_all(back, 'dp', split_axis=0, concat_axis=0, tiled=True)]
    dot_general x7, matrix products: 2.83 us -> 6.3 us  [ancestry(): jnp.dot(reach, reach, precision=lax.Precision.HIGHEST)]
    unnamed x24 -> x25, local copies, waits for them, and re-layouts: 5.25 us -> 6.07 us
  transfers between devices with their start and end apart: 6 -> 6, of which waited for: 6 -> 6; matrix products, arithmetic and copies ran while one was open for 8% -> 11% of each run, Pallas kernels for 0% -> 0%
where the time goes in v6:
time: 258 us; the launch traced here: 257 us
  waiting for transfers between devices  149 us (58%)
  starting transfers between devices  27 us (10%)
  matrix products  21.8 us (8%)
  local copies, waits for them, and re-layouts  19.6 us (8%)
  Pallas kernels  17.8 us (7%)
  between operations  14.4 us (6%)
  other arithmetic  7.25 us (3%)
    psum x1, waiting for transfers between devices, local(): attention_sum = lax.psum(attention_term.astype(jnp.bfloat16), 'head')  83.2 us
    all_to_all x1, waiting for transfers between devices, local(): lax.all_to_all(spread(shaped_queries, send_index), 'dp', split_axis=0, co...  22.7 us
    reduce_scatter x1, waiting for transfers between devices, local(): lax.psum_scatter(down_part, 'head', scatter_dimension=1, tiled=True)  14.1 us
    all_to_all x1, waiting for transfers between devices, local(): lax.all_to_all(spread(jnp.concatenate([kept_keys, kept_values], axis=1),...  12.1 us
    all_to_all x1, waiting for transfers between devices, local(): lax.all_to_all(back, 'dp', split_axis=0, concat_axis=0, tiled=True)  9.94 us
    pallas_call x1, Pallas kernels, attend(): pl.pallas_call(attend_block, grid_spec=grid_spec, out_shape=jax.ShapeDtyp...  9.27 us
    pallas_call x1, Pallas kernels, feed_forward(): pl.pallas_call(ffn_block, grid=(tokens // block,), in_specs=[pl.BlockSpec...  8.48 us
    all_to_all x1, starting transfers between devices, local(): lax.all_to_all(spread(shaped_queries, send_index), 'dp', split_axis=0, co...  7.75 us
  transfers between devices with their start and end apart: 6, of which 6 were waited for; matrix products, arithmetic and copies ran while one was open for 11% of the time, Pallas kernels for 0%

profile of v6, /device:TPU:2, one launch (start us, length us, event | category | flops | bytes accessed | tf_op | source)
XLA Modules:
  0.0 257.3 jit_solution(12941633234248686066)
XLA Ops:
  9.0 2.6 %fusion.5 = bf16[512,256]{1,0:T(8,128)(2,1)S(1)} fusion(bf16[512,2048]{1,0:T(8,128)(2,1)} %hid_ref.1, bf16[2048,256]{1,0:T(8,128)(2,1)} %param.31, f32[256]{0:T(256)} %param.32), kind=kOutput, calls=%fused_computation.17 | convolution fusion | flops 537133056 | bytes 3408896 | tf_op jit(solution)/shard_map/dot_general | solution.py:161
  12.4 1.9 copy.59
  14.3 7.8 %all-to-all-start = ((bf16[64,64,256]{2,1,0:T(8,128)(2,1)}), bf16[64,64,256]{2,1,0:T(8,128)(2,1)S(1)}, u32[]{:S(2)}, u32[]{:S(2)}) async-start(bf16[64,64,256]{2,1,0:T(8,128)(2,1)} %bitcast.101), calls=%async_computation | async-start | bytes 4194304 | tf_op jit(solution)/shard_map/all_to_all | solution.py:223
  25.3 22.7 %all-to-all-done.query_ref = bf16[64,64,256]{2,1,0:T(8,128)(2,1)S(1)} async-done(((bf16[64,64,256]{2,1,0:T(8,128)(2,1)}), bf16[64,64,256]{2,1,0:T(8,128)(2,1)S(1)}, u32[]{:S(2)}, u32[]{:S(2)}) %all-to-all-start) | async-done | bytes 2097184 | tf_op jit(solution)/shard_map/all_to_all | solution.py:223
  49.3 9.3 %shard_map.238 = bf16[64,66,256]{2,1,0:T(8,128)(2,1)} custom-call(s32[8]{0:T(128)} %multiply_add_fusion.1.where_ref, s32[8]{0:T(128)} %length_ref.1, bf16[64,64,256]{2,1,0:T(8,128)(2,1)} %copy-done.1, bf16[8,512,256]{2,1,0:T(8,128)(2,1)} %key_ref.1, bf16[8,512,256]{2,1,0:T(8,128)(2,1)} %value_ref.1), custom_call_target="tpu_custom_call" | custom-call | tf_op jit(solution)/shard_map/pallas_call | solution.py:118
  58.6 7.0 %all-to-all-start.1 = ((bf16[64,66,256]{2,1,0:T(8,128)(2,1)}), bf16[64,66,256]{2,1,0:T(8,128)(2,1)S(1)}, u32[]{:S(2)}, u32[]{:S(2)}) async-start(bf16[64,66,256]{2,1,0:T(8,128)(2,1)} %shard_map.238), calls=%async_computation.1 | async-start | bytes 4718592 | tf_op jit(solution)/shard_map/all_to_all | solution.py:236
  65.6 2.1 convolution_minimum_fusion.4
  67.8 1.7 reshape.233
  69.5 1.4 convolution_minimum_fusion.3
  72.3 3.3 %convolution_convert_fusion.3 = bf16[512,256]{1,0:T(8,128)(2,1)} fusion(bf16[512,2048]{1,0:T(8,128)(2,1)} %hid_ref.1, bf16[2048,256]{1,0:T(8,128)(2,1)} %param.33), kind=kOutput, calls=%fused_computation.20 | convolution fusion | flops 537001984 | bytes 3407872 | tf_op jit(solution)/shard_map/dot_general | solution.py:164
  75.5 1.7 reshape.234
  77.2 3.3 %fusion.6 = bf16[512,256]{1,0:T(8,128)(2,1)} fusion(bf16[512,2048]{1,0:T(8,128)(2,1)} %hid_ref.1, bf16[2048,256]{1,0:T(8,128)(2,1)} %param.34, f32[256]{0:T(256)S(1)} %copy-done.9), kind=kOutput, calls=%fused_computation.18 | convolution fusion | flops 537133056 | bytes 3408896 | tf_op jit(solution)/shard_map/dot_general | solution.py:165
  80.5 1.7 reshape.237
  84.5 9.9 %all-to-all-done.1 = bf16[64,66,256]{2,1,0:T(8,128)(2,1)S(1)} async-done(((bf16[64,66,256]{2,1,0:T(8,128)(2,1)}), bf16[64,66,256]{2,1,0:T(8,128)(2,1)S(1)}, u32[]{:S(2)}, u32[]{:S(2)}) %all-to-all-start.1) | async-done | bytes 2162720 | tf_op jit(solution)/shard_map/all_to_all | solution.py:236
  96.6 1.9 fusion.7
  98.8 2.1 convolution_convert_fusion.2
  101.1 83.2 %all-reduce.2.cloned.1.call-done.attn_ref = bf16[512,2048]{1,0:T(8,128)(2,1)} async-done(((bf16[512,2048]{1,0:T(8,128)(2,1)}), bf16[512,2048]{1,0:T(8,128)(2,1)}) %all-reduce.2.cloned.1.call-update) | async-done | bytes 2097168 | tf_op jit(solution)/shard_map/psum | solution.py:258
  184.3 8.5 %shard_map.239 = (bf16[512,2048]{1,0:T(8,128)(2,1)}, bf16[512,2048]{1,0:T(8,128)(2,1)}) custom-call(bf16[512,2048]{1,0:T(8,128)(2,1)} %all-reduce.2.cloned.1.call-done.attn_ref, bf16[512,2048]{1,0:T(8,128)(2,1)} %hid_ref.1, f32[1,2048]{1,0:T(1,128)} %bitcast.113, f32[1,2048]{1,0:T(1,128)} %bitcast.114, f32[1,2048]{1,0:T(1,128)} %bitcast.115, ...), custom_call_target="tpu_custom_call" | custom-call | flops 2147483648 | bytes 12582912 | tf_op jit(solution)/shard_map/pallas_call | solution.py:54
  197.4 7.4 %all-to-all-start.3 = ((bf16[64,32,256]{2,1,0:T(8,128)(2,1)}), bf16[64,32,256]{2,1,0:T(8,128)(2,1)S(1)}, u32[]{:S(2)}, u32[]{:S(2)}) async-start(bf16[64,32,256]{2,1,0:T(8,128)(2,1)} %bitcast.32), calls=%async_computation.4 | async-start | bytes 2097152 | tf_op jit(solution)/shard_map/all_to_all | solution.py:226
  207.2 12.1 %all-to-all-done.3 = bf16[64,32,256]{2,1,0:T(8,128)(2,1)S(1)} async-done(((bf16[64,32,256]{2,1,0:T(8,128)(2,1)}), bf16[64,32,256]{2,1,0:T(8,128)(2,1)S(1)}, u32[]{:S(2)}, u32[]{:S(2)}) %all-to-all-start.3) | async-done | bytes 1048608 | tf_op jit(solution)/shard_map/all_to_all | solution.py:226
  219.8 14.1 %reduce-scatter.2.cloned.1.call-done = bf16[512,256]{1,0:T(8,128)(2,1)} async-done(((bf16[512,2048]{1,0:T(8,128)(2,1)}), bf16[512,256]{1,0:T(8,128)(2,1)}) %reduce-scatter.2.cloned.1.call-update) | async-done | bytes 262160 | tf_op jit(solution)/shard_map/reduce_scatter | solution.py:262
  235.8 4.6 %all-to-all-start.2 = ((f32[8,2,512]{2,1,0:T(2,128)}), f32[8,2,512]{2,1,0:T(2,128)S(1)}, u32[]{:S(2)}, u32[]{:S(2)}) async-start(f32[8,2,512]{2,1,0:T(2,128)} %broadcast_in_dim.54), calls=%async_computation.3 | async-start | bytes 65536 | tf_op jit(solution)/shard_map/all_to_all | solution.py:271
  241.1 7.4 %all-to-all-done.2 = f32[8,2,512]{2,1,0:T(2,128)S(1)} async-done(((f32[8,2,512]{2,1,0:T(2,128)}), f32[8,2,512]{2,1,0:T(2,128)S(1)}, u32[]{:S(2)}, u32[]{:S(2)}) %all-to-all-start.2) | async-done | bytes 32800 | tf_op jit(solution)/shard_map/all_to_all | solution.py:271
  248.5 1.9 add_convert_fusion
  (79 shorter events, 23.3 us)
Async XLA Ops:
  7.2 91.6 %copy-start = (bf16[256,2048]{1,0:T(8,128)(2,1)S(1)}, bf16[256,2048]{1,0:T(8,128)(2,1)}, u32[]{:S(2)}) copy-start(bf16[256,2048]{1,0:T(8,128)(2,1)} %param.36) | copy-start | bytes 3145732
  11.6 2.7 %copy-start.4 = (bf16[512,256]{1,0:T(8,128)(2,1)}, bf16[512,256]{1,0:T(8,128)(2,1)S(1)}, u32[]{:S(2)}) copy-start(bf16[512,256]{1,0:T(8,128)(2,1)S(1)} %fusion.5) | copy-start | bytes 786436
  14.3 7.8 %copy-start.6 = (s32[256]{0:T(256)S(1)}, s32[256]{0:T(256)}, u32[]{:S(2)}) copy-start(s32[256]{0:T(256)} %param.25) | copy-start | bytes 3076
  14.3 9.4 %copy-start.7 = (s32[8,64]{1,0:T(8,128)S(1)}, s32[8,64]{1,0:T(8,128)}, u32[]{:S(2)}) copy-start(s32[8,64]{1,0:T(8,128)} %param.24) | copy-start | bytes 6148
  14.3 33.7 %all-to-all-start = ((bf16[64,64,256]{2,1,0:T(8,128)(2,1)}), bf16[64,64,256]{2,1,0:T(8,128)(2,1)S(1)}, u32[]{:S(2)}, u32[]{:S(2)}) async-start(bf16[64,64,256]{2,1,0:T(8,128)(2,1)} %bitcast.101), calls=%async_computation | async-start | bytes 4194304 | tf_op jit(solution)/shard_map/all_to_all | solution.py:223
  48.0 1.3 copy-start.1
  58.6 35.8 %all-to-all-start.1 = ((bf16[64,66,256]{2,1,0:T(8,128)(2,1)}), bf16[64,66,256]{2,1,0:T(8,128)(2,1)S(1)}, u32[]{:S(2)}, u32[]{:S(2)}) async-start(bf16[64,66,256]{2,1,0:T(8,128)(2,1)} %shard_map.238), calls=%async_computation.1 | async-start | bytes 4718592 | tf_op jit(solution)/shard_map/all_to_all | solution.py:236
  65.6 118.7 %all-reduce.2.cloned.1.call-start = ((), (), s32[]{:S(2)}) async-start(), calls=%async_computation.5 | async-start | bytes 4194304 | tf_op jit(solution)/shard_map/psum | solution.py:258
  72.2 5.0 %copy-start.9 = (f32[256]{0:T(256)S(1)}, f32[256]{0:T(256)}, u32[]{:S(2)}) copy-start(f32[256]{0:T(256)} %param.35) | copy-start | bytes 3076
  83.6 0.8 copy-start.5
  100.9 133.1 %reduce-scatter.2.cloned.1.call-start = ((), (), s32[]{:S(2)}) async-start(), calls=%async_computation.6 | async-start | bytes 2359296 | tf_op jit(solution)/shard_map/reduce_scatter | solution.py:262
  192.8 0.7 copy-start.8
  192.8 1.0 copy-start.2
  192.8 1.8 copy-start.3
  192.8 2.7 %copy-start.10 = (s32[8]{0:T(128)S(1)}, s32[8]{0:T(128)}, u32[]{:S(2)}) copy-start(s32[8]{0:T(128)} %param.28) | copy-start | bytes 100
  197.4 21.9 %all-to-all-start.3 = ((bf16[64,32,256]{2,1,0:T(8,128)(2,1)}), bf16[64,32,256]{2,1,0:T(8,128)(2,1)S(1)}, u32[]{:S(2)}, u32[]{:S(2)}) async-start(bf16[64,32,256]{2,1,0:T(8,128)(2,1)} %bitcast.32), calls=%async_computation.4 | async-start | bytes 2097152 | tf_op jit(solution)/shard_map/all_to_all | solution.py:226
  235.8 12.6 %all-to-all-start.2 = ((f32[8,2,512]{2,1,0:T(2,128)}), f32[8,2,512]{2,1,0:T(2,128)S(1)}, u32[]{:S(2)}, u32[]{:S(2)}) async-start(f32[8,2,512]{2,1,0:T(2,128)} %broadcast_in_dim.54), calls=%async_computation.3 | async-start | bytes 65536 | tf_op jit(solution)/shard_map/all_to_all | solution.py:271
Sparse Core Ops, SparseCore 0:
  101.0 83.2 all-reduce.1
  193.0 40.8 reduce-scatter.1

commit v7 on v6

--- a/solution.py
+++ b/solution.py
@@ -120,6 +120,41 @@
         grid_spec=grid_spec,
         out_shape=jax.ShapeDtypeStruct((positions, rows, width), arrived.dtype),
     )(where, lengths, arrived, keys, values)
+
+
+def project_block(where_ref, hidden_ref, weight_ref, bias_ref, query_ref, placed_ref):
+    rows = (
+        jnp.dot(hidden_ref[...], weight_ref[...], preferred_element_type=jnp.float32)
+        + bias_ref[...]
+    ).astype(query_ref.dtype)
+    query_ref[...] = rows
+    placed_ref[0] = rows
+
+
+def project(hidden, weight, bias, where, positions, draft):
+    tokens, model = hidden.shape
+    width = weight.shape[1]
+    grid_spec = pltpu.PrefetchScalarGridSpec(
+        num_scalar_prefetch=1,
+        grid=(tokens // draft,),
+        in_specs=[
+            pl.BlockSpec((draft, model), lambda r, w: (r, 0)),
+            pl.BlockSpec((model, width), lambda r, w: (0, 0)),
+            pl.BlockSpec((1, width), lambda r, w: (0, 0)),
+        ],
+        out_specs=[
+            pl.BlockSpec((draft, width), lambda r, w: (r, 0)),
+            pl.BlockSpec((1, draft, width), lambda r, w: (w[r], 0, 0)),
+        ],
+    )
+    return pl.pallas_call(
+        project_block,
+        grid_spec=grid_spec,
+        out_shape=[
+            jax.ShapeDtypeStruct((tokens, width), jnp.bfloat16),
+            jax.ShapeDtypeStruct((positions, draft, width), jnp.bfloat16),
+        ],
+    )(where, hidden, weight, bias.reshape(1, -1))
 
 
 def local(
@@ -158,14 +193,34 @@
     shards = lax.axis_size("dp")
     myself = lax.axis_index("dp")
     scale = 1.0 / math.sqrt(HD)
-    queries = (jnp.dot(hidden, w_query, preferred_element_type=jnp.float32) + b_query).astype(
-        jnp.bfloat16
-    )
+    local_ids = jnp.arange(requests, dtype=jnp.int32)
+    my_owner = lax.dynamic_slice_in_dim(owner_slot, myself * requests, requests)
+    target = my_owner // requests
+    earlier = local_ids[None, :] < local_ids[:, None]
+    same_target = target[None, :] == target[:, None]
+    rank = jnp.sum((earlier & same_target).astype(jnp.int32), axis=1)
+    my_slots = myself * requests + local_ids
+    every_id = jnp.arange(owner_slot.shape[0], dtype=jnp.int32)
+    source_request = jnp.sum(
+        jnp.where(owner_slot[None, :] == my_slots[:, None], every_id[None, :], 0), axis=1
+    )
+    source = source_request // requests
+    source_local = source_request % requests
+    source_targets = owner_slot.reshape(shards, requests)[source] // requests
+    source_rank = jnp.sum(
+        ((local_ids[None, :] < source_local[:, None]) & (source_targets == myself)).astype(
+            jnp.int32
+        ),
+        axis=1,
+    )
+    slots_total = shards * PEER_MOST
+    send_index = target * PEER_MOST + rank
+    receive_index = source * PEER_MOST + source_rank
+    queries, placed_queries = project(hidden, w_query, b_query, send_index, slots_total, draft)
     key_rows = jnp.dot(hidden, w_key, preferred_element_type=jnp.float32).astype(jnp.bfloat16)
     value_rows = (jnp.dot(hidden, w_value, preferred_element_type=jnp.float32) + b_value).astype(
         jnp.bfloat16
     )
-    local_ids = jnp.arange(requests, dtype=jnp.int32)
     levels = jnp.arange(accepted_path.shape[1], dtype=jnp.int32)
     chosen = local_ids[:, None] * draft + accepted_path
     usable = (levels[None, :] < accepted_count[:, None])[..., None]
@@ -188,30 +243,6 @@
         "rhqk,rkhd->rqhd", tree_probs, tree_values, preferred_element_type=jnp.float32
     ) / jnp.transpose(tree_total, (0, 2, 1, 3))
     tree_lse = jnp.transpose((tree_top + jnp.log(tree_total))[..., 0], (0, 2, 1))[..., None]
-    my_owner = lax.dynamic_slice_in_dim(owner_slot, myself * requests, requests)
-    target = my_owner // requests
-    earlier = local_ids[None, :] < local_ids[:, None]
-    same_target = target[None, :] == target[:, None]
-    rank = jnp.sum((earlier & same_target).astype(jnp.int32), axis=1)
-    my_slots = myself * requests + local_ids
-    every_id = jnp.arange(owner_slot.shape[0], dtype=jnp.int32)
-    source_request = jnp.sum(
-        jnp.where(owner_slot[None, :] == my_slots[:, None], every_id[None, :], 0), axis=1
-    )
-    source = source_request // requests
-    source_local = source_request % requests
-    source_targets = owner_slot.reshape(shards, requests)[source] // requests
-    source_rank = jnp.sum(
-        ((local_ids[None, :] < source_local[:, None]) & (source_targets == myself)).astype(
-            jnp.int32
-        ),
-        axis=1,
-    )
-
-    shaped_queries = queries.reshape(requests, draft, width)
-    slots_total = shards * PEER_MOST
-    send_index = target * PEER_MOST + rank
-    receive_index = source * PEER_MOST + source_rank
     slot_ids = jnp.arange(slots_total, dtype=jnp.int32)
 
     def spread(values, index):
@@ -220,9 +251,7 @@
         placed = jnp.dot(placing, flat, preferred_element_type=jnp.float32).astype(values.dtype)
         return placed.reshape((slots_total,) + values.shape[1:])
 
-    arrived = lax.all_to_all(
-        spread(shaped_queries, send_index), "dp", split_axis=0, concat_axis=0, tiled=True
-    )
+    arrived = lax.all_to_all(placed_queries, "dp", split_axis=0, concat_axis=0, tiled=True)
     kept = lax.all_to_all(
         spread(jnp.concatenate([kept_keys, kept_values], axis=1), send_index),
         "dp",

time: 258 us -> 261 us (1.012)
  matrix products: 21.8 us -> 12.7 us
  waiting for transfers between devices: 149 us -> 158 us
  Pallas kernels: 17.8 us -> 25.2 us
  local copies, waits for them, and re-layouts: 19.6 us -> 15.3 us
    all_to_all x1, waiting for transfers between devices: 9.94 us -> 17.9 us  [local(): lax.all_to_all(back, 'dp', split_axis=0, concat_axis=0, tiled=True)]
    pallas_call x0 -> x1, Pallas kernels: none -> 7.47 us  [project(): pl.pallas_call(project_block, grid_spec=grid_spec, out_shape=[jax.ShapeDt...]
    unnamed x25 -> x24, local copies, waits for them, and re-layouts: 6.07 us -> 3.3 us
    dot_general x7, matrix products: 6.3 us -> 3.54 us  [ancestry(): jnp.dot(reach, reach, precision=lax.Precision.HIGHEST)]
    dot_general x1 -> x0, matrix products: 2.63 us -> none  [local(): jnp.dot(hidden, w_query, preferred_element_type=jnp.float32) + b_query]
  transfers between devices with their start and end apart: 6 -> 6, of which waited for: 6 -> 6; matrix products, arithmetic and copies ran while one was open for 11% -> 8% of each run, Pallas kernels for 0% -> 0%
where the time goes in v7:
time: 261 us; the launch traced here: 260 us
  waiting for transfers between devices  158 us (61%)
  starting transfers between devices  27.7 us (11%)
  Pallas kernels  25.2 us (10%)
  local copies, waits for them, and re-layouts  15.3 us (6%)
  between operations  14.4 us (6%)
  matrix products  12.7 us (5%)
  other arithmetic  7 us (3%)
    psum x1, waiting for transfers between devices, local(): attention_sum = lax.psum(attention_term.astype(jnp.bfloat16), 'head')  83.4 us
    all_to_all x1, waiting for transfers between devices, local(): lax.all_to_all(placed_queries, 'dp', split_axis=0, concat_axis=0, tiled=T...  22.7 us
    all_to_all x1, waiting for transfers between devices, local(): lax.all_to_all(back, 'dp', split_axis=0, concat_axis=0, tiled=True)  17.9 us
    reduce_scatter x1, waiting for transfers between devices, local(): lax.psum_scatter(down_part, 'head', scatter_dimension=1, tiled=True)  14.1 us
    all_to_all x1, waiting for transfers between devices, local(): lax.all_to_all(spread(jnp.concatenate([kept_keys, kept_values], axis=1),...  12.1 us
    pallas_call x1, Pallas kernels, attend(): pl.pallas_call(attend_block, grid_spec=grid_spec, out_shape=jax.ShapeDtyp...  9.28 us
    pallas_call x1, Pallas kernels, feed_forward(): pl.pallas_call(ffn_block, grid=(tokens // block,), in_specs=[pl.BlockSpec...  8.48 us
    all_to_all x1, starting transfers between devices, local(): lax.all_to_all(back, 'dp', split_axis=0, concat_axis=0, tiled=True)  7.79 us
  transfers between devices with their start and end apart: 6, of which 6 were waited for; matrix products, arithmetic and copies ran while one was open for 8% of the time, Pallas kernels for 0%

profile of v7, /device:TPU:2, one launch (start us, length us, event | category | flops | bytes accessed | tf_op | source)
XLA Modules:
  0.0 260.0 jit_solution(11970188831751378293)
XLA Ops:
  8.2 1.3 compare_select_fusion.2
  9.5 7.5 %shard_map.238 = (bf16[512,256]{1,0:T(8,128)(2,1)}, bf16[64,64,256]{2,1,0:T(8,128)(2,1)}) custom-call(s32[8]{0:T(128)} %get-tuple-element.17.where_ref, bf16[512,2048]{1,0:T(8,128)(2,1)} %hid_ref.1, bf16[2048,256]{1,0:T(8,128)(2,1)} %weight_ref.1, f32[1,256]{1,0:T(1,128)} %bitcast.111), custom_call_target="tpu_custom_call" | custom-call | tf_op jit(solution)/shard_map/pallas_call | solution.py:150
  17.0 7.7 %all-to-all-start = ((bf16[64,64,256]{2,1,0:T(8,128)(2,1)}), bf16[64,64,256]{2,1,0:T(8,128)(2,1)S(1)}, u32[]{:S(2)}, u32[]{:S(2)}) async-start(bf16[64,64,256]{2,1,0:T(8,128)(2,1)} %get-tuple-element.7), calls=%async_computation | async-start | bytes 4194304 | tf_op jit(solution)/shard_map/all_to_all | solution.py:254
  26.9 1.1 convolution_minimum_fusion.5
  27.9 22.7 %all-to-all-done.query_ref = bf16[64,64,256]{2,1,0:T(8,128)(2,1)S(1)} async-done(((bf16[64,64,256]{2,1,0:T(8,128)(2,1)}), bf16[64,64,256]{2,1,0:T(8,128)(2,1)S(1)}, u32[]{:S(2)}, u32[]{:S(2)}) %all-to-all-start) | async-done | bytes 2097184 | tf_op jit(solution)/shard_map/all_to_all | solution.py:254
  50.7 1.3 copy-done.1
  52.0 9.3 %shard_map.239 = bf16[64,66,256]{2,1,0:T(8,128)(2,1)} custom-call(s32[8]{0:T(128)} %multiply_add_fusion.1.where_ref, s32[8]{0:T(128)} %length_ref.1, bf16[64,64,256]{2,1,0:T(8,128)(2,1)} %copy-done.1, bf16[8,512,256]{2,1,0:T(8,128)(2,1)} %key_ref.1, bf16[8,512,256]{2,1,0:T(8,128)(2,1)} %value_ref.1), custom_call_target="tpu_custom_call" | custom-call | tf_op jit(solution)/shard_map/pallas_call | solution.py:118
  61.3 7.8 %all-to-all-start.1 = ((bf16[64,66,256]{2,1,0:T(8,128)(2,1)}), bf16[64,66,256]{2,1,0:T(8,128)(2,1)}, u32[]{:S(2)}, u32[]{:S(2)}) async-start(bf16[64,66,256]{2,1,0:T(8,128)(2,1)} %shard_map.239), calls=%async_computation.1 | async-start | bytes 4718592 | tf_op jit(solution)/shard_map/all_to_all | solution.py:265
  71.3 1.9 convolution_convert_fusion.2
  74.0 2.6 %fusion.5 = bf16[512,256]{1,0:T(8,128)(2,1)} fusion(bf16[512,2048]{1,0:T(8,128)(2,1)S(1)} %copy-done.2, bf16[2048,256]{1,0:T(8,128)(2,1)} %param.34, f32[256]{0:T(256)S(1)} %copy-done.9), kind=kOutput, calls=%fused_computation.15 | convolution fusion | flops 537133056 | bytes 3408896 | tf_op jit(solution)/shard_map/dot_general | solution.py:221
  78.7 1.2 fusion.39
  80.1 17.9 %all-to-all-done.1 = bf16[64,66,256]{2,1,0:T(8,128)(2,1)} async-done(((bf16[64,66,256]{2,1,0:T(8,128)(2,1)}), bf16[64,66,256]{2,1,0:T(8,128)(2,1)}, u32[]{:S(2)}, u32[]{:S(2)}) %all-to-all-start.1) | async-done | bytes 2162720 | tf_op jit(solution)/shard_map/all_to_all | solution.py:265
  98.0 2.2 gather_fusion.1
  101.5 2.1 convolution_convert_fusion.1
  103.7 83.4 %all-reduce.2.cloned.1.call-done.attn_ref = bf16[512,2048]{1,0:T(8,128)(2,1)} async-done(((bf16[512,2048]{1,0:T(8,128)(2,1)}), bf16[512,2048]{1,0:T(8,128)(2,1)}) %all-reduce.2.cloned.1.call-update) | async-done | bytes 2097168 | tf_op jit(solution)/shard_map/psum | solution.py:287
  187.0 8.5 %shard_map.240 = (bf16[512,2048]{1,0:T(8,128)(2,1)}, bf16[512,2048]{1,0:T(8,128)(2,1)}) custom-call(bf16[512,2048]{1,0:T(8,128)(2,1)} %all-reduce.2.cloned.1.call-done.attn_ref, bf16[512,2048]{1,0:T(8,128)(2,1)} %hid_ref.1, f32[1,2048]{1,0:T(1,128)} %bitcast.107, f32[1,2048]{1,0:T(1,128)} %bitcast.108, f32[1,2048]{1,0:T(1,128)} %bitcast.109, ...), custom_call_target="tpu_custom_call" | custom-call | flops 2147483648 | bytes 12582912 | tf_op jit(solution)/shard_map/pallas_call | solution.py:54
  198.8 1.2 copy.61
  200.0 7.4 %all-to-all-start.3 = ((bf16[64,32,256]{2,1,0:T(8,128)(2,1)}), bf16[64,32,256]{2,1,0:T(8,128)(2,1)S(1)}, u32[]{:S(2)}, u32[]{:S(2)}) async-start(bf16[64,32,256]{2,1,0:T(8,128)(2,1)} %bitcast.31), calls=%async_computation.4 | async-start | bytes 2097152 | tf_op jit(solution)/shard_map/all_to_all | solution.py:255
  209.8 12.1 %all-to-all-done.3 = bf16[64,32,256]{2,1,0:T(8,128)(2,1)S(1)} async-done(((bf16[64,32,256]{2,1,0:T(8,128)(2,1)}), bf16[64,32,256]{2,1,0:T(8,128)(2,1)S(1)}, u32[]{:S(2)}, u32[]{:S(2)}) %all-to-all-start.3) | async-done | bytes 1048608 | tf_op jit(solution)/shard_map/all_to_all | solution.py:255
  222.5 14.1 %reduce-scatter.2.cloned.1.call-done = bf16[512,256]{1,0:T(8,128)(2,1)} async-done(((bf16[512,2048]{1,0:T(8,128)(2,1)}), bf16[512,256]{1,0:T(8,128)(2,1)}) %reduce-scatter.2.cloned.1.call-update) | async-done | bytes 262160 | tf_op jit(solution)/shard_map/reduce_scatter | solution.py:291
  236.6 1.3 fusion.10
  238.5 4.6 %all-to-all-start.2 = ((f32[8,2,512]{2,1,0:T(2,128)}), f32[8,2,512]{2,1,0:T(2,128)S(1)}, u32[]{:S(2)}, u32[]{:S(2)}) async-start(f32[8,2,512]{2,1,0:T(2,128)} %broadcast_in_dim.54), calls=%async_computation.3 | async-start | bytes 65536 | tf_op jit(solution)/shard_map/all_to_all | solution.py:300
  243.8 7.4 %all-to-all-done.2 = f32[8,2,512]{2,1,0:T(2,128)S(1)} async-done(((f32[8,2,512]{2,1,0:T(2,128)}), f32[8,2,512]{2,1,0:T(2,128)S(1)}, u32[]{:S(2)}, u32[]{:S(2)}) %all-to-all-start.2) | async-done | bytes 32800 | tf_op jit(solution)/shard_map/all_to_all | solution.py:300
  251.2 1.9 add_convert_fusion
  (76 shorter events, 16.9 us)
Async XLA Ops:
  7.2 94.4 %copy-start = (bf16[256,2048]{1,0:T(8,128)(2,1)S(1)}, bf16[256,2048]{1,0:T(8,128)(2,1)}, u32[]{:S(2)}) copy-start(bf16[256,2048]{1,0:T(8,128)(2,1)} %param.36) | copy-start | bytes 3145732
  17.0 7.8 %copy-start.5 = (s32[256]{0:T(256)S(1)}, s32[256]{0:T(256)}, u32[]{:S(2)}) copy-start(s32[256]{0:T(256)} %param.25) | copy-start | bytes 3076
  17.0 9.4 %copy-start.7 = (s32[8,64]{1,0:T(8,128)S(1)}, s32[8,64]{1,0:T(8,128)}, u32[]{:S(2)}) copy-start(s32[8,64]{1,0:T(8,128)} %param.24) | copy-start | bytes 6148
  17.0 33.7 %all-to-all-start = ((bf16[64,64,256]{2,1,0:T(8,128)(2,1)}), bf16[64,64,256]{2,1,0:T(8,128)(2,1)S(1)}, u32[]{:S(2)}, u32[]{:S(2)}) async-start(bf16[64,64,256]{2,1,0:T(8,128)(2,1)} %get-tuple-element.7), calls=%async_computation | async-start | bytes 4194304 | tf_op jit(solution)/shard_map/all_to_all | solution.py:254
  50.7 1.3 copy-start.1
  61.3 7.9 %copy-start.4 = (f32[8,64,64]{2,1,0:T(8,128)S(1)}, f32[8,64,64]{2,1,0:T(8,128)}, u32[]{:S(2)}) copy-start(f32[8,64,64]{2,1,0:T(8,128)} %convolution_minimum_fusion.5) | copy-start | bytes 393220
  61.3 36.7 %all-to-all-start.1 = ((bf16[64,66,256]{2,1,0:T(8,128)(2,1)}), bf16[64,66,256]{2,1,0:T(8,128)(2,1)}, u32[]{:S(2)}, u32[]{:S(2)}) async-start(bf16[64,66,256]{2,1,0:T(8,128)(2,1)} %shard_map.239), calls=%async_computation.1 | async-start | bytes 4718592 | tf_op jit(solution)/shard_map/all_to_all | solution.py:265
  69.1 2.2 copy-start.2
  69.1 118.0 %all-reduce.2.cloned.1.call-start = ((), (), s32[]{:S(2)}) async-start(), calls=%async_computation.5 | async-start | bytes 4194304 | tf_op jit(solution)/shard_map/psum | solution.py:287
  71.3 2.7 %copy-start.9 = (f32[256]{0:T(256)S(1)}, f32[256]{0:T(256)}, u32[]{:S(2)}) copy-start(f32[256]{0:T(256)} %param.35) | copy-start | bytes 3076
  103.6 133.0 %reduce-scatter.2.cloned.1.call-start = ((), (), s32[]{:S(2)}) async-start(), calls=%async_computation.6 | async-start | bytes 2359296 | tf_op jit(solution)/shard_map/reduce_scatter | solution.py:291
  195.5 0.7 copy-start.8
  195.5 1.7 copy-start.3
  195.5 2.6 copy-start.10
  195.5 2.8 %copy-start.6 = (s32[8]{0:T(128)S(1)}, s32[8]{0:T(128)}, u32[]{:S(2)}) copy-start(s32[8]{0:T(128)} %get-tuple-element.17.where_ref) | copy-start | bytes 100
  200.0 21.9 %all-to-all-start.3 = ((bf16[64,32,256]{2,1,0:T(8,128)(2,1)}), bf16[64,32,256]{2,1,0:T(8,128)(2,1)S(1)}, u32[]{:S(2)}, u32[]{:S(2)}) async-start(bf16[64,32,256]{2,1,0:T(8,128)(2,1)} %bitcast.31), calls=%async_computation.4 | async-start | bytes 2097152 | tf_op jit(solution)/shard_map/all_to_all | solution.py:255
  238.5 12.7 %all-to-all-start.2 = ((f32[8,2,512]{2,1,0:T(2,128)}), f32[8,2,512]{2,1,0:T(2,128)S(1)}, u32[]{:S(2)}, u32[]{:S(2)}) async-start(f32[8,2,512]{2,1,0:T(2,128)} %broadcast_in_dim.54), calls=%async_computation.3 | async-start | bytes 65536 | tf_op jit(solution)/shard_map/all_to_all | solution.py:300
Sparse Core Ops, SparseCore 0:
  103.7 83.2 all-reduce.1
  195.7 40.8 reduce-scatter.1

commit v8 on v7

--- a/solution.py
+++ b/solution.py
@@ -123,12 +123,14 @@
 
 
 def project_block(where_ref, hidden_ref, weight_ref, bias_ref, query_ref, placed_ref):
+    draft = placed_ref.shape[1]
     rows = (
         jnp.dot(hidden_ref[...], weight_ref[...], preferred_element_type=jnp.float32)
         + bias_ref[...]
     ).astype(query_ref.dtype)
     query_ref[...] = rows
-    placed_ref[0] = rows
+    for request in range(query_ref.shape[0] // draft):
+        placed_ref[where_ref[request]] = rows[request * draft : (request + 1) * draft]
 
 
 def project(hidden, weight, bias, where, positions, draft):
@@ -136,15 +138,15 @@
     width = weight.shape[1]
     grid_spec = pltpu.PrefetchScalarGridSpec(
         num_scalar_prefetch=1,
-        grid=(tokens // draft,),
+        grid=(1,),
         in_specs=[
-            pl.BlockSpec((draft, model), lambda r, w: (r, 0)),
+            pl.BlockSpec((tokens, model), lambda r, w: (0, 0)),
             pl.BlockSpec((model, width), lambda r, w: (0, 0)),
             pl.BlockSpec((1, width), lambda r, w: (0, 0)),
         ],
         out_specs=[
-            pl.BlockSpec((draft, width), lambda r, w: (r, 0)),
-            pl.BlockSpec((1, draft, width), lambda r, w: (w[r], 0, 0)),
+            pl.BlockSpec((tokens, width), lambda r, w: (0, 0)),
+            pl.BlockSpec((positions, draft, width), lambda r, w: (0, 0, 0)),
         ],
     )
     return pl.pallas_call(

time: 261 us -> 258 us (0.989)
  Pallas kernels: 25.2 us -> 22.5 us
    pallas_call x1, Pallas kernels: 7.47 us -> 4.7 us  [project(): pl.pallas_call(project_block, grid_spec=grid_spec, out_shape=[jax.ShapeDt...]
where the time goes in v8:
time: 258 us; the launch traced here: 257 us
  waiting for transfers between devices  158 us (61%)
  starting transfers between devices  27.4 us (11%)
  Pallas kernels  22.5 us (9%)
  local copies, waits for them, and re-layouts  15.3 us (6%)
  between operations  14.4 us (6%)
  matrix products  12.7 us (5%)
  other arithmetic  7 us (3%)
    psum x1, waiting for transfers between devices, local(): attention_sum = lax.psum(attention_term.astype(jnp.bfloat16), 'head')  83.4 us
    all_to_all x1, waiting for transfers between devices, local(): lax.all_to_all(placed_queries, 'dp', split_axis=0, concat_axis=0, tiled=T...  22.7 us
    all_to_all x1, waiting for transfers between devices, local(): lax.all_to_all(back, 'dp', split_axis=0, concat_axis=0, tiled=True)  17.9 us
    reduce_scatter x1, waiting for transfers between devices, local(): lax.psum_scatter(down_part, 'head', scatter_dimension=1, tiled=True)  14.2 us
    all_to_all x1, waiting for transfers between devices, local(): lax.all_to_all(spread(jnp.concatenate([kept_keys, kept_values], axis=1),...  12.1 us
    pallas_call x1, Pallas kernels, attend(): pl.pallas_call(attend_block, grid_spec=grid_spec, out_shape=jax.ShapeDtyp...  9.28 us
    pallas_call x1, Pallas kernels, feed_forward(): pl.pallas_call(ffn_block, grid=(tokens // block,), in_specs=[pl.BlockSpec...  8.49 us
    all_to_all x1, starting transfers between devices, local(): lax.all_to_all(back, 'dp', split_axis=0, concat_axis=0, tiled=True)  7.78 us
  transfers between devices with their start and end apart: 6, of which 6 were waited for; matrix products, arithmetic and copies ran while one was open for 8% of the time, Pallas kernels for 0%

profile of v8, /device:TPU:2, one launch (start us, length us, event | category | flops | bytes accessed | tf_op | source)
XLA Modules:
  0.0 257.1 jit_solution(3988708913944735049)
XLA Ops:
  8.2 1.3 compare_select_fusion.2
  9.5 4.7 %shard_map.238 = (bf16[512,256]{1,0:T(8,128)(2,1)}, bf16[64,64,256]{2,1,0:T(8,128)(2,1)}) custom-call(s32[8]{0:T(128)} %get-tuple-element.17.where_ref, bf16[512,2048]{1,0:T(8,128)(2,1)} %hid_ref.1, bf16[2048,256]{1,0:T(8,128)(2,1)} %weight_ref.1, f32[1,256]{1,0:T(1,128)} %bitcast.111), custom_call_target="tpu_custom_call" | custom-call | tf_op jit(solution)/shard_map/pallas_call | solution.py:152
  14.2 7.8 %all-to-all-start = ((bf16[64,64,256]{2,1,0:T(8,128)(2,1)}), bf16[64,64,256]{2,1,0:T(8,128)(2,1)S(1)}, u32[]{:S(2)}, u32[]{:S(2)}) async-start(bf16[64,64,256]{2,1,0:T(8,128)(2,1)} %get-tuple-element.7), calls=%async_computation | async-start | bytes 4194304 | tf_op jit(solution)/shard_map/all_to_all | solution.py:256
  24.1 1.1 convolution_minimum_fusion.5
  25.2 22.7 %all-to-all-done.query_ref = bf16[64,64,256]{2,1,0:T(8,128)(2,1)S(1)} async-done(((bf16[64,64,256]{2,1,0:T(8,128)(2,1)}), bf16[64,64,256]{2,1,0:T(8,128)(2,1)S(1)}, u32[]{:S(2)}, u32[]{:S(2)}) %all-to-all-start) | async-done | bytes 2097184 | tf_op jit(solution)/shard_map/all_to_all | solution.py:256
  47.9 1.3 copy-done.1
  49.2 9.3 %shard_map.239 = bf16[64,66,256]{2,1,0:T(8,128)(2,1)} custom-call(s32[8]{0:T(128)} %multiply_add_fusion.1.where_ref, s32[8]{0:T(128)} %length_ref.1, bf16[64,64,256]{2,1,0:T(8,128)(2,1)} %copy-done.1, bf16[8,512,256]{2,1,0:T(8,128)(2,1)} %key_ref.1, bf16[8,512,256]{2,1,0:T(8,128)(2,1)} %value_ref.1), custom_call_target="tpu_custom_call" | custom-call | tf_op jit(solution)/shard_map/pallas_call | solution.py:118
  58.5 7.8 %all-to-all-start.1 = ((bf16[64,66,256]{2,1,0:T(8,128)(2,1)}), bf16[64,66,256]{2,1,0:T(8,128)(2,1)}, u32[]{:S(2)}, u32[]{:S(2)}) async-start(bf16[64,66,256]{2,1,0:T(8,128)(2,1)} %shard_map.239), calls=%async_computation.1 | async-start | bytes 4718592 | tf_op jit(solution)/shard_map/all_to_all | solution.py:267
  68.5 1.9 convolution_convert_fusion.2
  71.2 2.6 %fusion.5 = bf16[512,256]{1,0:T(8,128)(2,1)} fusion(bf16[512,2048]{1,0:T(8,128)(2,1)S(1)} %copy-done.2, bf16[2048,256]{1,0:T(8,128)(2,1)} %param.34, f32[256]{0:T(256)S(1)} %copy-done.9), kind=kOutput, calls=%fused_computation.15 | convolution fusion | flops 537133056 | bytes 3408896 | tf_op jit(solution)/shard_map/dot_general | solution.py:223
  75.9 1.2 fusion.39
  77.3 17.9 %all-to-all-done.1 = bf16[64,66,256]{2,1,0:T(8,128)(2,1)} async-done(((bf16[64,66,256]{2,1,0:T(8,128)(2,1)}), bf16[64,66,256]{2,1,0:T(8,128)(2,1)}, u32[]{:S(2)}, u32[]{:S(2)}) %all-to-all-start.1) | async-done | bytes 2162720 | tf_op jit(solution)/shard_map/all_to_all | solution.py:267
  95.2 2.2 gather_fusion.1
  98.8 2.1 convolution_convert_fusion.1
  100.9 83.4 %all-reduce.2.cloned.1.call-done.attn_ref = bf16[512,2048]{1,0:T(8,128)(2,1)} async-done(((bf16[512,2048]{1,0:T(8,128)(2,1)}), bf16[512,2048]{1,0:T(8,128)(2,1)}) %all-reduce.2.cloned.1.call-update) | async-done | bytes 2097168 | tf_op jit(solution)/shard_map/psum | solution.py:289
  184.3 8.5 %shard_map.240 = (bf16[512,2048]{1,0:T(8,128)(2,1)}, bf16[512,2048]{1,0:T(8,128)(2,1)}) custom-call(bf16[512,2048]{1,0:T(8,128)(2,1)} %all-reduce.2.cloned.1.call-done.attn_ref, bf16[512,2048]{1,0:T(8,128)(2,1)} %hid_ref.1, f32[1,2048]{1,0:T(1,128)} %bitcast.107, f32[1,2048]{1,0:T(1,128)} %bitcast.108, f32[1,2048]{1,0:T(1,128)} %bitcast.109, ...), custom_call_target="tpu_custom_call" | custom-call | flops 2147483648 | bytes 12582912 | tf_op jit(solution)/shard_map/pallas_call | solution.py:54
  196.0 1.2 copy.61
  197.3 7.4 %all-to-all-start.3 = ((bf16[64,32,256]{2,1,0:T(8,128)(2,1)}), bf16[64,32,256]{2,1,0:T(8,128)(2,1)S(1)}, u32[]{:S(2)}, u32[]{:S(2)}) async-start(bf16[64,32,256]{2,1,0:T(8,128)(2,1)} %bitcast.31), calls=%async_computation.4 | async-start | bytes 2097152 | tf_op jit(solution)/shard_map/all_to_all | solution.py:257
  207.0 12.1 %all-to-all-done.3 = bf16[64,32,256]{2,1,0:T(8,128)(2,1)S(1)} async-done(((bf16[64,32,256]{2,1,0:T(8,128)(2,1)}), bf16[64,32,256]{2,1,0:T(8,128)(2,1)S(1)}, u32[]{:S(2)}, u32[]{:S(2)}) %all-to-all-start.3) | async-done | bytes 1048608 | tf_op jit(solution)/shard_map/all_to_all | solution.py:257
  219.7 14.2 %reduce-scatter.2.cloned.1.call-done = bf16[512,256]{1,0:T(8,128)(2,1)} async-done(((bf16[512,2048]{1,0:T(8,128)(2,1)}), bf16[512,256]{1,0:T(8,128)(2,1)}) %reduce-scatter.2.cloned.1.call-update) | async-done | bytes 262160 | tf_op jit(solution)/shard_map/reduce_scatter | solution.py:293
  233.9 1.3 fusion.10
  235.8 4.4 %all-to-all-start.2 = ((f32[8,2,512]{2,1,0:T(2,128)}), f32[8,2,512]{2,1,0:T(2,128)S(1)}, u32[]{:S(2)}, u32[]{:S(2)}) async-start(f32[8,2,512]{2,1,0:T(2,128)} %broadcast_in_dim.54), calls=%async_computation.3 | async-start | bytes 65536 | tf_op jit(solution)/shard_map/all_to_all | solution.py:302
  240.8 7.4 %all-to-all-done.2 = f32[8,2,512]{2,1,0:T(2,128)S(1)} async-done(((f32[8,2,512]{2,1,0:T(2,128)}), f32[8,2,512]{2,1,0:T(2,128)S(1)}, u32[]{:S(2)}, u32[]{:S(2)}) %all-to-all-start.2) | async-done | bytes 32800 | tf_op jit(solution)/shard_map/all_to_all | solution.py:302
  248.3 1.9 add_convert_fusion
  (76 shorter events, 16.9 us)
Async XLA Ops:
  7.2 91.6 %copy-start = (bf16[256,2048]{1,0:T(8,128)(2,1)S(1)}, bf16[256,2048]{1,0:T(8,128)(2,1)}, u32[]{:S(2)}) copy-start(bf16[256,2048]{1,0:T(8,128)(2,1)} %param.36) | copy-start | bytes 3145732
  14.2 7.8 %copy-start.5 = (s32[256]{0:T(256)S(1)}, s32[256]{0:T(256)}, u32[]{:S(2)}) copy-start(s32[256]{0:T(256)} %param.25) | copy-start | bytes 3076
  14.2 9.4 %copy-start.7 = (s32[8,64]{1,0:T(8,128)S(1)}, s32[8,64]{1,0:T(8,128)}, u32[]{:S(2)}) copy-start(s32[8,64]{1,0:T(8,128)} %param.24) | copy-start | bytes 6148
  14.2 33.7 %all-to-all-start = ((bf16[64,64,256]{2,1,0:T(8,128)(2,1)}), bf16[64,64,256]{2,1,0:T(8,128)(2,1)S(1)}, u32[]{:S(2)}, u32[]{:S(2)}) async-start(bf16[64,64,256]{2,1,0:T(8,128)(2,1)} %get-tuple-element.7), calls=%async_computation | async-start | bytes 4194304 | tf_op jit(solution)/shard_map/all_to_all | solution.py:256
  47.9 1.3 copy-start.1
  58.5 7.9 %copy-start.4 = (f32[8,64,64]{2,1,0:T(8,128)S(1)}, f32[8,64,64]{2,1,0:T(8,128)}, u32[]{:S(2)}) copy-start(f32[8,64,64]{2,1,0:T(8,128)} %convolution_minimum_fusion.5) | copy-start | bytes 393220
  58.5 36.7 %all-to-all-start.1 = ((bf16[64,66,256]{2,1,0:T(8,128)(2,1)}), bf16[64,66,256]{2,1,0:T(8,128)(2,1)}, u32[]{:S(2)}, u32[]{:S(2)}) async-start(bf16[64,66,256]{2,1,0:T(8,128)(2,1)} %shard_map.239), calls=%async_computation.1 | async-start | bytes 4718592 | tf_op jit(solution)/shard_map/all_to_all | solution.py:267
  66.3 2.2 copy-start.2
  66.3 118.0 %all-reduce.2.cloned.1.call-start = ((), (), s32[]{:S(2)}) async-start(), calls=%async_computation.5 | async-start | bytes 4194304 | tf_op jit(solution)/shard_map/psum | solution.py:289
  68.5 2.7 %copy-start.9 = (f32[256]{0:T(256)S(1)}, f32[256]{0:T(256)}, u32[]{:S(2)}) copy-start(f32[256]{0:T(256)} %param.35) | copy-start | bytes 3076
  100.8 133.0 %reduce-scatter.2.cloned.1.call-start = ((), (), s32[]{:S(2)}) async-start(), calls=%async_computation.6 | async-start | bytes 2359296 | tf_op jit(solution)/shard_map/reduce_scatter | solution.py:293
  192.8 0.7 copy-start.8
  192.8 1.7 copy-start.3
  192.8 2.6 copy-start.10
  192.8 2.8 %copy-start.6 = (s32[8]{0:T(128)S(1)}, s32[8]{0:T(128)}, u32[]{:S(2)}) copy-start(s32[8]{0:T(128)} %get-tuple-element.17.where_ref) | copy-start | bytes 100
  197.3 21.9 %all-to-all-start.3 = ((bf16[64,32,256]{2,1,0:T(8,128)(2,1)}), bf16[64,32,256]{2,1,0:T(8,128)(2,1)S(1)}, u32[]{:S(2)}, u32[]{:S(2)}) async-start(bf16[64,32,256]{2,1,0:T(8,128)(2,1)} %bitcast.31), calls=%async_computation.4 | async-start | bytes 2097152 | tf_op jit(solution)/shard_map/all_to_all | solution.py:257
  235.8 12.4 %all-to-all-start.2 = ((f32[8,2,512]{2,1,0:T(2,128)}), f32[8,2,512]{2,1,0:T(2,128)S(1)}, u32[]{:S(2)}, u32[]{:S(2)}) async-start(f32[8,2,512]{2,1,0:T(2,128)} %broadcast_in_dim.54), calls=%async_computation.3 | async-start | bytes 65536 | tf_op jit(solution)/shard_map/all_to_all | solution.py:302
Sparse Core Ops, SparseCore 0:
  101.0 83.2 all-reduce.1
  192.9 40.8 reduce-scatter.1

commit v9 on v8

--- a/solution.py
+++ b/solution.py
@@ -46,7 +46,7 @@
     inner = jax.nn.gelu(raised, approximate=True).astype(jnp.bfloat16)
     down_ref[...] = jnp.dot(inner, wdown_ref[...], preferred_element_type=jnp.float32).astype(jnp.bfloat16)
 
-def feed_forward(attn, hidden, b_out, gain, shift, w_up, b_up, w_down, block=128):
+def feed_forward(attn, hidden, b_out, gain, shift, w_up, b_up, w_down, block=256):
     tokens, model = hidden.shape
     units = w_up.shape[1]
     row = lambda i: (i, 0)

time: 258 us -> 258 us (level)
  no operation moved by 1% of the time
where the time goes in v9:
time: 258 us; the launch traced here: 257 us
  waiting for transfers between devices  158 us (61%)
  starting transfers between devices  27.7 us (11%)
  Pallas kernels  22 us (9%)
  local copies, waits for them, and re-layouts  15.3 us (6%)
  between operations  14.4 us (6%)
  matrix products  12.7 us (5%)
  other arithmetic  7 us (3%)
    psum x1, waiting for transfers between devices, local(): attention_sum = lax.psum(attention_term.astype(jnp.bfloat16), 'head')  83.4 us
    all_to_all x1, waiting for transfers between devices, local(): lax.all_to_all(placed_queries, 'dp', split_axis=0, concat_axis=0, tiled=T...  22.7 us
    all_to_all x1, waiting for transfers between devices, local(): lax.all_to_all(back, 'dp', split_axis=0, concat_axis=0, tiled=True)  17.9 us
    reduce_scatter x1, waiting for transfers between devices, local(): lax.psum_scatter(down_part, 'head', scatter_dimension=1, tiled=True)  14.1 us
    all_to_all x1, waiting for transfers between devices, local(): lax.all_to_all(spread(jnp.concatenate([kept_keys, kept_values], axis=1),...  12.1 us
    pallas_call x1, Pallas kernels, attend(): pl.pallas_call(attend_block, grid_spec=grid_spec, out_shape=jax.ShapeDtyp...  9.27 us
    pallas_call x1, Pallas kernels, feed_forward(): pl.pallas_call(ffn_block, grid=(tokens // block,), in_specs=[pl.BlockSpec...  8 us
    all_to_all x1, starting transfers between devices, local(): lax.all_to_all(back, 'dp', split_axis=0, concat_axis=0, tiled=True)  7.78 us
  transfers between devices with their start and end apart: 6, of which 6 were waited for; matrix products, arithmetic and copies ran while one was open for 8% of the time, Pallas kernels for 0%

profile of v9, /device:TPU:2, one launch (start us, length us, event | category | flops | bytes accessed | tf_op | source)
XLA Modules:
  0.0 256.8 jit_solution(5807678091938545978)
XLA Ops:
  8.2 1.3 compare_select_fusion.2
  9.5 4.7 %shard_map.238 = (bf16[512,256]{1,0:T(8,128)(2,1)}, bf16[64,64,256]{2,1,0:T(8,128)(2,1)}) custom-call(s32[8]{0:T(128)} %get-tuple-element.17.where_ref, bf16[512,2048]{1,0:T(8,128)(2,1)} %hid_ref.1, bf16[2048,256]{1,0:T(8,128)(2,1)} %weight_ref.1, f32[1,256]{1,0:T(1,128)} %bitcast.111), custom_call_target="tpu_custom_call" | custom-call | tf_op jit(solution)/shard_map/pallas_call | solution.py:152
  14.2 7.8 %all-to-all-start = ((bf16[64,64,256]{2,1,0:T(8,128)(2,1)}), bf16[64,64,256]{2,1,0:T(8,128)(2,1)S(1)}, u32[]{:S(2)}, u32[]{:S(2)}) async-start(bf16[64,64,256]{2,1,0:T(8,128)(2,1)} %get-tuple-element.7), calls=%async_computation | async-start | bytes 4194304 | tf_op jit(solution)/shard_map/all_to_all | solution.py:256
  24.1 1.1 convolution_minimum_fusion.5
  25.2 22.7 %all-to-all-done.query_ref = bf16[64,64,256]{2,1,0:T(8,128)(2,1)S(1)} async-done(((bf16[64,64,256]{2,1,0:T(8,128)(2,1)}), bf16[64,64,256]{2,1,0:T(8,128)(2,1)S(1)}, u32[]{:S(2)}, u32[]{:S(2)}) %all-to-all-start) | async-done | bytes 2097184 | tf_op jit(solution)/shard_map/all_to_all | solution.py:256
  47.9 1.3 copy-done.1
  49.2 9.3 %shard_map.239 = bf16[64,66,256]{2,1,0:T(8,128)(2,1)} custom-call(s32[8]{0:T(128)} %multiply_add_fusion.1.where_ref, s32[8]{0:T(128)} %length_ref.1, bf16[64,64,256]{2,1,0:T(8,128)(2,1)} %copy-done.1, bf16[8,512,256]{2,1,0:T(8,128)(2,1)} %key_ref.1, bf16[8,512,256]{2,1,0:T(8,128)(2,1)} %value_ref.1), custom_call_target="tpu_custom_call" | custom-call | tf_op jit(solution)/shard_map/pallas_call | solution.py:118
  58.5 7.8 %all-to-all-start.1 = ((bf16[64,66,256]{2,1,0:T(8,128)(2,1)}), bf16[64,66,256]{2,1,0:T(8,128)(2,1)}, u32[]{:S(2)}, u32[]{:S(2)}) async-start(bf16[64,66,256]{2,1,0:T(8,128)(2,1)} %shard_map.239), calls=%async_computation.1 | async-start | bytes 4718592 | tf_op jit(solution)/shard_map/all_to_all | solution.py:267
  68.5 1.9 convolution_convert_fusion.2
  71.2 2.6 %fusion.5 = bf16[512,256]{1,0:T(8,128)(2,1)} fusion(bf16[512,2048]{1,0:T(8,128)(2,1)S(1)} %copy-done.2, bf16[2048,256]{1,0:T(8,128)(2,1)} %param.34, f32[256]{0:T(256)S(1)} %copy-done.9), kind=kOutput, calls=%fused_computation.15 | convolution fusion | flops 537133056 | bytes 3408896 | tf_op jit(solution)/shard_map/dot_general | solution.py:223
  75.9 1.2 fusion.39
  77.3 17.9 %all-to-all-done.1 = bf16[64,66,256]{2,1,0:T(8,128)(2,1)} async-done(((bf16[64,66,256]{2,1,0:T(8,128)(2,1)}), bf16[64,66,256]{2,1,0:T(8,128)(2,1)}, u32[]{:S(2)}, u32[]{:S(2)}) %all-to-all-start.1) | async-done | bytes 2162720 | tf_op jit(solution)/shard_map/all_to_all | solution.py:267
  95.2 2.2 gather_fusion.1
  98.7 2.1 convolution_convert_fusion.1
  100.9 83.4 %all-reduce.2.cloned.1.call-done.attn_ref = bf16[512,2048]{1,0:T(8,128)(2,1)} async-done(((bf16[512,2048]{1,0:T(8,128)(2,1)}), bf16[512,2048]{1,0:T(8,128)(2,1)}) %all-reduce.2.cloned.1.call-update) | async-done | bytes 2097168 | tf_op jit(solution)/shard_map/psum | solution.py:289
  184.3 8.0 %shard_map.240 = (bf16[512,2048]{1,0:T(8,128)(2,1)}, bf16[512,2048]{1,0:T(8,128)(2,1)}) custom-call(bf16[512,2048]{1,0:T(8,128)(2,1)} %all-reduce.2.cloned.1.call-done.attn_ref, bf16[512,2048]{1,0:T(8,128)(2,1)} %hid_ref.1, f32[1,2048]{1,0:T(1,128)} %bitcast.107, f32[1,2048]{1,0:T(1,128)} %bitcast.108, f32[1,2048]{1,0:T(1,128)} %bitcast.109, ...), custom_call_target="tpu_custom_call" | custom-call | flops 2147483648 | bytes 12582912 | tf_op jit(solution)/shard_map/pallas_call | solution.py:54
  195.5 1.2 copy.61
  196.8 7.4 %all-to-all-start.3 = ((bf16[64,32,256]{2,1,0:T(8,128)(2,1)}), bf16[64,32,256]{2,1,0:T(8,128)(2,1)S(1)}, u32[]{:S(2)}, u32[]{:S(2)}) async-start(bf16[64,32,256]{2,1,0:T(8,128)(2,1)} %bitcast.31), calls=%async_computation.4 | async-start | bytes 2097152 | tf_op jit(solution)/shard_map/all_to_all | solution.py:257
  206.5 12.1 %all-to-all-done.3 = bf16[64,32,256]{2,1,0:T(8,128)(2,1)S(1)} async-done(((bf16[64,32,256]{2,1,0:T(8,128)(2,1)}), bf16[64,32,256]{2,1,0:T(8,128)(2,1)S(1)}, u32[]{:S(2)}, u32[]{:S(2)}) %all-to-all-start.3) | async-done | bytes 1048608 | tf_op jit(solution)/shard_map/all_to_all | solution.py:257
  219.2 14.1 %reduce-scatter.2.cloned.1.call-done = bf16[512,256]{1,0:T(8,128)(2,1)} async-done(((bf16[512,2048]{1,0:T(8,128)(2,1)}), bf16[512,256]{1,0:T(8,128)(2,1)}) %reduce-scatter.2.cloned.1.call-update) | async-done | bytes 262160 | tf_op jit(solution)/shard_map/reduce_scatter | solution.py:293
  233.3 1.3 fusion.10
  235.2 4.7 %all-to-all-start.2 = ((f32[8,2,512]{2,1,0:T(2,128)}), f32[8,2,512]{2,1,0:T(2,128)S(1)}, u32[]{:S(2)}, u32[]{:S(2)}) async-start(f32[8,2,512]{2,1,0:T(2,128)} %broadcast_in_dim.54), calls=%async_computation.3 | async-start | bytes 65536 | tf_op jit(solution)/shard_map/all_to_all | solution.py:302
  240.6 7.4 %all-to-all-done.2 = f32[8,2,512]{2,1,0:T(2,128)S(1)} async-done(((f32[8,2,512]{2,1,0:T(2,128)}), f32[8,2,512]{2,1,0:T(2,128)S(1)}, u32[]{:S(2)}, u32[]{:S(2)}) %all-to-all-start.2) | async-done | bytes 32800 | tf_op jit(solution)/shard_map/all_to_all | solution.py:302
  248.0 1.9 add_convert_fusion
  (76 shorter events, 16.9 us)
Async XLA Ops:
  7.2 91.6 %copy-start = (bf16[256,2048]{1,0:T(8,128)(2,1)S(1)}, bf16[256,2048]{1,0:T(8,128)(2,1)}, u32[]{:S(2)}) copy-start(bf16[256,2048]{1,0:T(8,128)(2,1)} %param.36) | copy-start | bytes 3145732
  14.2 7.8 %copy-start.5 = (s32[256]{0:T(256)S(1)}, s32[256]{0:T(256)}, u32[]{:S(2)}) copy-start(s32[256]{0:T(256)} %param.25) | copy-start | bytes 3076
  14.2 9.4 %copy-start.7 = (s32[8,64]{1,0:T(8,128)S(1)}, s32[8,64]{1,0:T(8,128)}, u32[]{:S(2)}) copy-start(s32[8,64]{1,0:T(8,128)} %param.24) | copy-start | bytes 6148
  14.2 33.7 %all-to-all-start = ((bf16[64,64,256]{2,1,0:T(8,128)(2,1)}), bf16[64,64,256]{2,1,0:T(8,128)(2,1)S(1)}, u32[]{:S(2)}, u32[]{:S(2)}) async-start(bf16[64,64,256]{2,1,0:T(8,128)(2,1)} %get-tuple-element.7), calls=%async_computation | async-start | bytes 4194304 | tf_op jit(solution)/shard_map/all_to_all | solution.py:256
  47.9 1.3 copy-start.1
  58.5 7.9 %copy-start.4 = (f32[8,64,64]{2,1,0:T(8,128)S(1)}, f32[8,64,64]{2,1,0:T(8,128)}, u32[]{:S(2)}) copy-start(f32[8,64,64]{2,1,0:T(8,128)} %convolution_minimum_fusion.5) | copy-start | bytes 393220
  58.5 36.7 %all-to-all-start.1 = ((bf16[64,66,256]{2,1,0:T(8,128)(2,1)}), bf16[64,66,256]{2,1,0:T(8,128)(2,1)}, u32[]{:S(2)}, u32[]{:S(2)}) async-start(bf16[64,66,256]{2,1,0:T(8,128)(2,1)} %shard_map.239), calls=%async_computation.1 | async-start | bytes 4718592 | tf_op jit(solution)/shard_map/all_to_all | solution.py:267
  66.3 2.2 copy-start.2
  66.3 118.0 %all-reduce.2.cloned.1.call-start = ((), (), s32[]{:S(2)}) async-start(), calls=%async_computation.5 | async-start | bytes 4194304 | tf_op jit(solution)/shard_map/psum | solution.py:289
  68.5 2.7 %copy-start.9 = (f32[256]{0:T(256)S(1)}, f32[256]{0:T(256)}, u32[]{:S(2)}) copy-start(f32[256]{0:T(256)} %param.35) | copy-start | bytes 3076
  100.8 132.5 %reduce-scatter.2.cloned.1.call-start = ((), (), s32[]{:S(2)}) async-start(), calls=%async_computation.6 | async-start | bytes 2359296 | tf_op jit(solution)/shard_map/reduce_scatter | solution.py:293
  192.3 0.7 copy-start.8
  192.3 1.7 copy-start.3
  192.3 2.6 copy-start.10
  192.3 2.8 %copy-start.6 = (s32[8]{0:T(128)S(1)}, s32[8]{0:T(128)}, u32[]{:S(2)}) copy-start(s32[8]{0:T(128)} %get-tuple-element.17.where_ref) | copy-start | bytes 100
  196.8 21.9 %all-to-all-start.3 = ((bf16[64,32,256]{2,1,0:T(8,128)(2,1)}), bf16[64,32,256]{2,1,0:T(8,128)(2,1)S(1)}, u32[]{:S(2)}, u32[]{:S(2)}) async-start(bf16[64,32,256]{2,1,0:T(8,128)(2,1)} %bitcast.31), calls=%async_computation.4 | async-start | bytes 2097152 | tf_op jit(solution)/shard_map/all_to_all | solution.py:257
  235.2 12.7 %all-to-all-start.2 = ((f32[8,2,512]{2,1,0:T(2,128)}), f32[8,2,512]{2,1,0:T(2,128)S(1)}, u32[]{:S(2)}, u32[]{:S(2)}) async-start(f32[8,2,512]{2,1,0:T(2,128)} %broadcast_in_dim.54), calls=%async_computation.3 | async-start | bytes 65536 | tf_op jit(solution)/shard_map/all_to_all | solution.py:302
Sparse Core Ops, SparseCore 0:
  100.9 83.2 all-reduce.1
  192.4 40.8 reduce-scatter.1

commit v10 on v9

--- a/solution.py
+++ b/solution.py
@@ -157,6 +157,53 @@
             jax.ShapeDtypeStruct((positions, draft, width), jnp.bfloat16),
         ],
     )(where, hidden, weight, bias.reshape(1, -1))
+
+
+def blend_block(
+    where_ref, received_ref, tree_ref, cache_share_ref, tree_share_ref, weight_ref, out_ref, mixed_ref
+):
+    draft = tree_ref.shape[0] // where_ref.shape[0]
+    heads = cache_share_ref.shape[1]
+    for request in range(where_ref.shape[0]):
+        rows = slice(request * draft, (request + 1) * draft)
+        part = received_ref[where_ref[request], :draft, :].astype(jnp.float32)
+        tree = tree_ref[rows, :]
+        cache_share = cache_share_ref[rows, :]
+        tree_share = tree_share_ref[rows, :]
+        for head in range(heads):
+            cols = slice(head * HD, (head + 1) * HD)
+            ours = cache_share[:, head : head + 1]
+            theirs = tree_share[:, head : head + 1]
+            mixed_ref[rows, cols] = (
+                (ours * part[:, cols] + theirs * tree[:, cols]) / (ours + theirs)
+            ).astype(mixed_ref.dtype)
+    out_ref[...] = jnp.dot(
+        mixed_ref[...], weight_ref[...], preferred_element_type=jnp.float32
+    ).astype(out_ref.dtype)
+
+
+def blend_out(received, where, tree_part, cache_share, tree_share, weight):
+    tokens, width = tree_part.shape
+    model = weight.shape[1]
+    whole = lambda r, w: (0, 0)
+    grid_spec = pltpu.PrefetchScalarGridSpec(
+        num_scalar_prefetch=1,
+        grid=(1,),
+        in_specs=[
+            pl.BlockSpec(received.shape, lambda r, w: (0, 0, 0)),
+            pl.BlockSpec(tree_part.shape, whole),
+            pl.BlockSpec(cache_share.shape, whole),
+            pl.BlockSpec(tree_share.shape, whole),
+            pl.BlockSpec(weight.shape, whole),
+        ],
+        out_specs=pl.BlockSpec((tokens, model), whole),
+        scratch_shapes=[pltpu.VMEM((tokens, width), jnp.bfloat16)],
+    )
+    return pl.pallas_call(
+        blend_block,
+        grid_spec=grid_spec,
+        out_shape=jax.ShapeDtypeStruct((tokens, model), jnp.bfloat16),
+    )(where, received, tree_part, cache_share, tree_share, weight)
 
 
 def local(
@@ -264,9 +311,8 @@
     new_keys = kept[:, : kept_keys.shape[1]]
     new_values = kept[:, kept_keys.shape[1] :]
     back = attend(arrived, receive_index, slot_lengths, cache_keys, cache_values)
-    returned = lax.all_to_all(back, "dp", split_axis=0, concat_axis=0, tiled=True)[send_index]
-    cache_part = returned[:, :draft]
-    lse_rows = returned[:, draft : draft + local_heads].astype(jnp.float32)
+    received = lax.all_to_all(back, "dp", split_axis=0, concat_axis=0, tiled=True)
+    lse_rows = received[send_index, draft : draft + local_heads].astype(jnp.float32)
     cache_lse = lse_rows[..., :draft] + (
         lse_rows[..., draft : 2 * draft] + lse_rows[..., 2 * draft : 3 * draft]
     )
@@ -274,19 +320,21 @@
     larger = jnp.maximum(cache_weight, tree_lse)
     cache_share = jnp.exp(cache_weight - larger)
     tree_share = jnp.exp(tree_lse - larger)
-    blended = (
-        cache_share * cache_part.astype(jnp.float32).reshape(requests, draft, local_heads, HD)
-        + tree_share * tree_part
-    ) / (cache_share + tree_share)
-    attended = blended.astype(jnp.bfloat16).reshape(tokens, width)
-    attention_term = jnp.dot(attended, w_out, preferred_element_type=jnp.float32)
+    attention_term = blend_out(
+        received,
+        send_index,
+        tree_part.reshape(tokens, width),
+        cache_share.reshape(tokens, local_heads),
+        tree_share.reshape(tokens, local_heads),
+        w_out,
+    )
     feature = model_width // lax.axis_size("head")
     offset = lax.axis_index("head") * feature
 
     def columns(values):
         return lax.dynamic_slice_in_dim(values, offset, feature, values.ndim - 1)
 
-    attention_sum = lax.psum(attention_term.astype(jnp.bfloat16), "head")
+    attention_sum = lax.psum(attention_term, "head")
     first_normed, down_part = feed_forward(
         attention_sum, hidden, b_out, first_gain, first_shift, w_up, b_up, w_down
     )

time: 258 us -> 262 us (1.016)
  waiting for transfers between devices: 158 us -> 150 us
  local copies, waits for them, and re-layouts: 15.3 us -> 21.6 us
  Pallas kernels: 22 us -> 27.5 us
    all_to_all x1, waiting for transfers between devices: 17.9 us -> 10.6 us  [local(): lax.all_to_all(back, 'dp', split_axis=0, concat_axis=0, tiled=True)]
    pallas_call x0 -> x1, Pallas kernels: none -> 5.47 us  [blend_out(): pl.pallas_call(blend_block, grid_spec=grid_spec, out_shape=jax.ShapeDtype...]
  transfers between devices with their start and end apart: 6 -> 6, of which waited for: 6 -> 6; matrix products, arithmetic and copies ran while one was open for 8% -> 11% of each run, Pallas kernels for 0% -> 0%
where the time goes in v10:
time: 262 us; the launch traced here: 261 us
  waiting for transfers between devices  150 us (57%)
  Pallas kernels  27.5 us (10%)
  starting transfers between devices  26.9 us (10%)
  local copies, waits for them, and re-layouts  21.6 us (8%)
  between operations  14.4 us (5%)
  matrix products  13.9 us (5%)
  other arithmetic  6.98 us (3%)
    psum x1, waiting for transfers between devices, local(): attention_sum = lax.psum(attention_term, 'head')  83.3 us
    all_to_all x1, waiting for transfers between devices, local(): lax.all_to_all(placed_queries, 'dp', split_axis=0, concat_axis=0, tiled=T...  22.3 us
    reduce_scatter x1, waiting for transfers between devices, local(): lax.psum_scatter(down_part, 'head', scatter_dimension=1, tiled=True)  14 us
    all_to_all x1, waiting for transfers between devices, local(): lax.all_to_all(spread(jnp.concatenate([kept_keys, kept_values], axis=1),...  12.1 us
    all_to_all x1, waiting for transfers between devices, local(): lax.all_to_all(back, 'dp', split_axis=0, concat_axis=0, tiled=True)  10.6 us
    pallas_call x1, Pallas kernels, attend(): pl.pallas_call(attend_block, grid_spec=grid_spec, out_shape=jax.ShapeDtyp...  9.28 us
    pallas_call x1, Pallas kernels, feed_forward(): pl.pallas_call(ffn_block, grid=(tokens // block,), in_specs=[pl.BlockSpec...  8.01 us
    all_to_all x1, starting transfers between devices, local(): lax.all_to_all(placed_queries, 'dp', split_axis=0, concat_axis=0, tiled=T...  7.76 us
  transfers between devices with their start and end apart: 6, of which 6 were waited for; matrix products, arithmetic and copies ran while one was open for 11% of the time, Pallas kernels for 0%

profile of v10, /device:TPU:2, one launch (start us, length us, event | category | flops | bytes accessed | tf_op | source)
XLA Modules:
  0.0 260.9 jit_solution(5629321451308985620)
XLA Ops:
  9.5 4.7 %shard_map.238 = (bf16[512,256]{1,0:T(8,128)(2,1)}, bf16[64,64,256]{2,1,0:T(8,128)(2,1)}) custom-call(s32[8]{0:T(128)} %get-tuple-element.14.where_ref, bf16[512,2048]{1,0:T(8,128)(2,1)} %hid_ref.1, bf16[2048,256]{1,0:T(8,128)(2,1)} %weight_ref.2, f32[1,256]{1,0:T(1,128)} %bitcast.96), custom_call_target="tpu_custom_call" | custom-call | tf_op jit(solution)/shard_map/pallas_call | solution.py:152
  14.2 7.8 %all-to-all-start = ((bf16[64,64,256]{2,1,0:T(8,128)(2,1)}), bf16[64,64,256]{2,1,0:T(8,128)(2,1)S(1)}, u32[]{:S(2)}, u32[]{:S(2)}) async-start(bf16[64,64,256]{2,1,0:T(8,128)(2,1)} %get-tuple-element.7), calls=%async_computation | async-start | bytes 4194304 | tf_op jit(solution)/shard_map/all_to_all | solution.py:303
  25.6 22.3 %all-to-all-done.query_ref = bf16[64,64,256]{2,1,0:T(8,128)(2,1)S(1)} async-done(((bf16[64,64,256]{2,1,0:T(8,128)(2,1)}), bf16[64,64,256]{2,1,0:T(8,128)(2,1)S(1)}, u32[]{:S(2)}, u32[]{:S(2)}) %all-to-all-start) | async-done | bytes 2097184 | tf_op jit(solution)/shard_map/all_to_all | solution.py:303
  49.2 9.3 %shard_map.239 = bf16[64,66,256]{2,1,0:T(8,128)(2,1)} custom-call(s32[8]{0:T(128)} %multiply_add_fusion.where_ref, s32[8]{0:T(128)} %length_ref.1, bf16[64,64,256]{2,1,0:T(8,128)(2,1)} %copy-done.2, bf16[8,512,256]{2,1,0:T(8,128)(2,1)} %key_ref.1, bf16[8,512,256]{2,1,0:T(8,128)(2,1)} %value_ref.1), custom_call_target="tpu_custom_call" | custom-call | tf_op jit(solution)/shard_map/pallas_call | solution.py:118
  58.5 7.0 %all-to-all-start.1 = ((bf16[64,66,256]{2,1,0:T(8,128)(2,1)}), bf16[64,66,256]{2,1,0:T(8,128)(2,1)S(1)}, u32[]{:S(2)}, u32[]{:S(2)}) async-start(bf16[64,66,256]{2,1,0:T(8,128)(2,1)} %shard_map.239), calls=%async_computation.1 | async-start | bytes 4718592 | tf_op jit(solution)/shard_map/all_to_all | solution.py:314
  65.5 1.4 convolution_minimum_fusion.3
  68.3 3.0 %convolution_convert_fusion.1 = bf16[512,256]{1,0:T(8,128)(2,1)} fusion(bf16[512,2048]{1,0:T(8,128)(2,1)} %hid_ref.1, bf16[2048,256]{1,0:T(8,128)(2,1)S(1)} %copy-done), kind=kOutput, calls=%fused_computation.12 | convolution fusion | flops 537001984 | bytes 3407872 | tf_op jit(solution)/shard_map/dot_general | solution.py:269
  71.4 1.7 reshape.232
  73.1 3.3 %fusion.2 = bf16[512,256]{1,0:T(8,128)(2,1)} fusion(bf16[512,2048]{1,0:T(8,128)(2,1)} %hid_ref.1, bf16[2048,256]{1,0:T(8,128)(2,1)} %param.34, f32[256]{0:T(256)S(1)} %copy-done.9), kind=kOutput, calls=%fused_computation.11 | convolution fusion | flops 537133056 | bytes 3408896 | tf_op jit(solution)/shard_map/dot_general | solution.py:270
  76.4 1.7 reshape.230
  78.1 1.7 reshape.231
  79.8 1.3 fusion.33
  83.8 10.6 %all-to-all-done.1.received_ref = bf16[64,66,256]{2,1,0:T(8,128)(2,1)S(1)} async-done(((bf16[64,66,256]{2,1,0:T(8,128)(2,1)}), bf16[64,66,256]{2,1,0:T(8,128)(2,1)S(1)}, u32[]{:S(2)}, u32[]{:S(2)}) %all-to-all-start.1) | async-done | bytes 2162720 | tf_op jit(solution)/shard_map/all_to_all | solution.py:314
  94.3 2.0 copy.76
  96.4 1.3 gather_fusion.1
  99.5 5.5 %shard_map.240 = bf16[512,2048]{1,0:T(8,128)(2,1)} custom-call(s32[8]{0:T(128)} %get-tuple-element.14.where_ref, bf16[64,66,256]{2,1,0:T(8,128)(2,1)} %copy-done.1, f32[512,256]{1,0:T(8,128)} %bitcast.80, f32[512,2]{1,0:T(8,128)} %bitcast.82, f32[512,2]{1,0:T(8,128)} %bitcast.81, bf16[256,2048]{1,0:T(8,128)(2,1)} %weight_ref.3), custom_call_target="tpu_custom_call" | custom-call | tf_op jit(solution)/shard_map/pallas_call | solution.py:202
  105.3 83.3 %all-reduce.3.cloned.1.call-done.attn_ref = bf16[512,2048]{1,0:T(8,128)(2,1)} async-done(((bf16[512,2048]{1,0:T(8,128)(2,1)}), bf16[512,2048]{1,0:T(8,128)(2,1)}) %all-reduce.3.cloned.1.call-update) | async-done | bytes 2097168 | tf_op jit(solution)/shard_map/psum | solution.py:337
  188.5 8.0 %shard_map.241 = (bf16[512,2048]{1,0:T(8,128)(2,1)}, bf16[512,2048]{1,0:T(8,128)(2,1)}) custom-call(bf16[512,2048]{1,0:T(8,128)(2,1)} %all-reduce.3.cloned.1.call-done.attn_ref, bf16[512,2048]{1,0:T(8,128)(2,1)} %hid_ref.1, f32[1,2048]{1,0:T(1,128)} %bitcast.92, f32[1,2048]{1,0:T(1,128)} %bitcast.93, f32[1,2048]{1,0:T(1,128)} %bitcast.94, ...), custom_call_target="tpu_custom_call" | custom-call | flops 2147483648 | bytes 12582912 | tf_op jit(solution)/shard_map/pallas_call | solution.py:54
  201.2 7.4 %all-to-all-start.3 = ((bf16[64,32,256]{2,1,0:T(8,128)(2,1)}), bf16[64,32,256]{2,1,0:T(8,128)(2,1)S(1)}, u32[]{:S(2)}, u32[]{:S(2)}) async-start(bf16[64,32,256]{2,1,0:T(8,128)(2,1)} %bitcast.31), calls=%async_computation.4 | async-start | bytes 2097152 | tf_op jit(solution)/shard_map/all_to_all | solution.py:304
  210.9 12.1 %all-to-all-done.3 = bf16[64,32,256]{2,1,0:T(8,128)(2,1)S(1)} async-done(((bf16[64,32,256]{2,1,0:T(8,128)(2,1)}), bf16[64,32,256]{2,1,0:T(8,128)(2,1)S(1)}, u32[]{:S(2)}, u32[]{:S(2)}) %all-to-all-start.3) | async-done | bytes 1048608 | tf_op jit(solution)/shard_map/all_to_all | solution.py:304
  223.6 14.0 %reduce-scatter.2.cloned.1.call-done = bf16[512,256]{1,0:T(8,128)(2,1)} async-done(((bf16[512,2048]{1,0:T(8,128)(2,1)}), bf16[512,256]{1,0:T(8,128)(2,1)}) %reduce-scatter.2.cloned.1.call-update) | async-done | bytes 262160 | tf_op jit(solution)/shard_map/reduce_scatter | solution.py:341
  239.5 4.5 %all-to-all-start.2 = ((f32[8,2,512]{2,1,0:T(2,128)}), f32[8,2,512]{2,1,0:T(2,128)S(1)}, u32[]{:S(2)}, u32[]{:S(2)}) async-start(f32[8,2,512]{2,1,0:T(2,128)} %broadcast_in_dim.54), calls=%async_computation.3 | async-start | bytes 65536 | tf_op jit(solution)/shard_map/all_to_all | solution.py:350
  244.6 7.4 %all-to-all-done.2 = f32[8,2,512]{2,1,0:T(2,128)S(1)} async-done(((f32[8,2,512]{2,1,0:T(2,128)}), f32[8,2,512]{2,1,0:T(2,128)S(1)}, u32[]{:S(2)}, u32[]{:S(2)}) %all-to-all-start.2) | async-done | bytes 32800 | tf_op jit(solution)/shard_map/all_to_all | solution.py:350
  252.1 1.9 add_convert_fusion
  (79 shorter events, 23.3 us)
Async XLA Ops:
  7.2 61.2 %copy-start = (bf16[2048,256]{1,0:T(8,128)(2,1)S(1)}, bf16[2048,256]{1,0:T(8,128)(2,1)}, u32[]{:S(2)}) copy-start(bf16[2048,256]{1,0:T(8,128)(2,1)} %param.33) | copy-start | bytes 3145732
  14.2 7.8 %copy-start.6 = (s32[256]{0:T(256)S(1)}, s32[256]{0:T(256)}, u32[]{:S(2)}) copy-start(s32[256]{0:T(256)} %param.25) | copy-start | bytes 3076
  14.2 9.4 %copy-start.7 = (s32[8,64]{1,0:T(8,128)S(1)}, s32[8,64]{1,0:T(8,128)}, u32[]{:S(2)}) copy-start(s32[8,64]{1,0:T(8,128)} %param.24) | copy-start | bytes 6148
  14.2 33.7 %all-to-all-start = ((bf16[64,64,256]{2,1,0:T(8,128)(2,1)}), bf16[64,64,256]{2,1,0:T(8,128)(2,1)S(1)}, u32[]{:S(2)}, u32[]{:S(2)}) async-start(bf16[64,64,256]{2,1,0:T(8,128)(2,1)} %get-tuple-element.7), calls=%async_computation | async-start | bytes 4194304 | tf_op jit(solution)/shard_map/all_to_all | solution.py:303
  47.9 1.3 copy-start.2
  58.5 35.8 %all-to-all-start.1 = ((bf16[64,66,256]{2,1,0:T(8,128)(2,1)}), bf16[64,66,256]{2,1,0:T(8,128)(2,1)S(1)}, u32[]{:S(2)}, u32[]{:S(2)}) async-start(bf16[64,66,256]{2,1,0:T(8,128)(2,1)} %shard_map.239), calls=%async_computation.1 | async-start | bytes 4718592 | tf_op jit(solution)/shard_map/all_to_all | solution.py:314
  65.5 123.1 %all-reduce.3.cloned.1.call-start = ((), (), s32[]{:S(2)}) async-start(), calls=%async_computation.5 | async-start | bytes 4194304 | tf_op jit(solution)/shard_map/psum | solution.py:337
  68.3 4.8 %copy-start.9 = (f32[256]{0:T(256)S(1)}, f32[256]{0:T(256)}, u32[]{:S(2)}) copy-start(f32[256]{0:T(256)} %param.35) | copy-start | bytes 3076
  94.3 2.0 copy-start.1
  105.0 132.6 %reduce-scatter.2.cloned.1.call-start = ((), (), s32[]{:S(2)}) async-start(), calls=%async_computation.6 | async-start | bytes 2359296 | tf_op jit(solution)/shard_map/reduce_scatter | solution.py:341
  196.6 0.7 copy-start.8
  196.6 1.0 copy-start.3
  196.6 1.8 copy-start.4
  196.6 2.7 %copy-start.10 = (s32[8]{0:T(128)S(1)}, s32[8]{0:T(128)}, u32[]{:S(2)}) copy-start(s32[8]{0:T(128)} %param.28) | copy-start | bytes 100
  196.6 2.9 %copy-start.5 = (s32[8]{0:T(128)S(1)}, s32[8]{0:T(128)}, u32[]{:S(2)}) copy-start(s32[8]{0:T(128)} %get-tuple-element.14.where_ref) | copy-start | bytes 100
  201.2 21.9 %all-to-all-start.3 = ((bf16[64,32,256]{2,1,0:T(8,128)(2,1)}), bf16[64,32,256]{2,1,0:T(8,128)(2,1)S(1)}, u32[]{:S(2)}, u32[]{:S(2)}) async-start(bf16[64,32,256]{2,1,0:T(8,128)(2,1)} %bitcast.31), calls=%async_computation.4 | async-start | bytes 2097152 | tf_op jit(solution)/shard_map/all_to_all | solution.py:304
  239.5 12.5 %all-to-all-start.2 = ((f32[8,2,512]{2,1,0:T(2,128)}), f32[8,2,512]{2,1,0:T(2,128)S(1)}, u32[]{:S(2)}, u32[]{:S(2)}) async-start(f32[8,2,512]{2,1,0:T(2,128)} %broadcast_in_dim.54), calls=%async_computation.3 | async-start | bytes 65536 | tf_op jit(solution)/shard_map/all_to_all | solution.py:350
Sparse Core Ops, SparseCore 0:
  105.2 83.3 all-reduce.2
  196.7 40.8 reduce-scatter.1

commit v11 on v9

--- a/solution.py
+++ b/solution.py
@@ -36,23 +36,38 @@
     return (mixed - center) * lax.rsqrt(square - center * center + EPSILON) * gain + shift
 
 
-def ffn_block(attn_ref, hid_ref, bout_ref, gain_ref, shift_ref, wup_ref, bup_ref, wdown_ref, normed_ref, down_ref):
+def ffn_block(
+    column_ref, attn_ref, hid_ref, bout_ref, gain_ref, shift_ref, wup_ref, bup_ref, wdown_ref,
+    normed_ref, down_ref,
+):
     mixed = attn_ref[...].astype(jnp.float32) + bout_ref[...] + hid_ref[...].astype(jnp.float32)
     center = jnp.mean(mixed, axis=-1, keepdims=True)
     square = jnp.mean(mixed * mixed, axis=-1, keepdims=True)
-    normed = ((mixed - center) * lax.rsqrt(square - center * center + EPSILON) * gain_ref[...] + shift_ref[...]).astype(jnp.bfloat16)
-    normed_ref[...] = normed
+    scale = lax.rsqrt(square - center * center + EPSILON)
+    normed = ((mixed - center) * scale * gain_ref[...] + shift_ref[...]).astype(jnp.bfloat16)
+    feature = normed_ref.shape[1]
+    start = pl.multiple_of(column_ref[0] * feature, feature)
+    cols = pl.ds(start, feature)
+    own = (
+        attn_ref[:, cols].astype(jnp.float32) + bout_ref[:, cols] + hid_ref[:, cols].astype(jnp.float32)
+    )
+    normed_ref[...] = ((own - center) * scale * gain_ref[:, cols] + shift_ref[:, cols]).astype(
+        normed_ref.dtype
+    )
     raised = jnp.dot(normed, wup_ref[...], preferred_element_type=jnp.float32) + bup_ref[...]
     inner = jax.nn.gelu(raised, approximate=True).astype(jnp.bfloat16)
-    down_ref[...] = jnp.dot(inner, wdown_ref[...], preferred_element_type=jnp.float32).astype(jnp.bfloat16)
-
-def feed_forward(attn, hidden, b_out, gain, shift, w_up, b_up, w_down, block=256):
+    down_ref[...] = jnp.dot(inner, wdown_ref[...], preferred_element_type=jnp.float32).astype(
+        jnp.bfloat16
+    )
+
+
+def feed_forward(attn, hidden, b_out, gain, shift, w_up, b_up, w_down, column, feature, block=256):
     tokens, model = hidden.shape
     units = w_up.shape[1]
-    row = lambda i: (i, 0)
-    fixed = lambda i: (0, 0)
-    return pl.pallas_call(
-        ffn_block,
+    row = lambda i, c: (i, 0)
+    fixed = lambda i, c: (0, 0)
+    grid_spec = pltpu.PrefetchScalarGridSpec(
+        num_scalar_prefetch=1,
         grid=(tokens // block,),
         in_specs=[
             pl.BlockSpec((block, model), row),
@@ -64,10 +79,29 @@
             pl.BlockSpec((1, units), fixed),
             pl.BlockSpec((units, model), fixed),
         ],
-        out_specs=[pl.BlockSpec((block, model), row), pl.BlockSpec((block, model), row)],
-        out_shape=[jax.ShapeDtypeStruct((tokens, model), jnp.bfloat16)] * 2,
-        cost_estimate=pl.CostEstimate(flops=4 * tokens * model * units, transcendentals=tokens * units, bytes_accessed=2 * (4 * tokens * model + 2 * model * units)),
-    )(attn, hidden, b_out.reshape(1, -1), gain.reshape(1, -1), shift.reshape(1, -1), w_up, b_up.reshape(1, -1), w_down)
+        out_specs=[
+            pl.BlockSpec((block, feature), lambda i, c: (i, 0)),
+            pl.BlockSpec((block, model), row),
+        ],
+    )
+    return pl.pallas_call(
+        ffn_block,
+        grid_spec=grid_spec,
+        out_shape=[
+            jax.ShapeDtypeStruct((tokens, feature), jnp.bfloat16),
+            jax.ShapeDtypeStruct((tokens, model), jnp.bfloat16),
+        ],
+    )(
+        column,
+        attn,
+        hidden,
+        b_out.reshape(1, -1),
+        gain.reshape(1, -1),
+        shift.reshape(1, -1),
+        w_up,
+        b_up.reshape(1, -1),
+        w_down,
+    )
 
 
 def attend_block(where_ref, length_ref, query_ref, key_ref, value_ref, back_ref):
@@ -287,13 +321,22 @@
         return lax.dynamic_slice_in_dim(values, offset, feature, values.ndim - 1)
 
     attention_sum = lax.psum(attention_term.astype(jnp.bfloat16), "head")
-    first_normed, down_part = feed_forward(
-        attention_sum, hidden, b_out, first_gain, first_shift, w_up, b_up, w_down
+    own_normed, down_part = feed_forward(
+        attention_sum,
+        hidden,
+        b_out,
+        first_gain,
+        first_shift,
+        w_up,
+        b_up,
+        w_down,
+        lax.axis_index("head").reshape(1).astype(jnp.int32),
+        feature,
     )
     down_share = lax.psum_scatter(
         down_part, "head", scatter_dimension=1, tiled=True
     ).astype(jnp.float32)
-    second_mixed = down_share + columns(b_down) + columns(first_normed).astype(jnp.float32)
+    second_mixed = down_share + columns(b_down) + own_normed.astype(jnp.float32)
     heads_along = lax.axis_size("head")
     own_sums = jnp.stack(
         [jnp.sum(second_mixed, axis=1), jnp.sum(second_mixed * second_mixed, axis=1)]

time: 258 us -> 258 us (level)
  waiting for transfers between devices: 158 us -> 155 us
  transfers between devices with their start and end apart: 6 -> 6, of which waited for: 6 -> 6; matrix products, arithmetic and copies ran while one was open for 8% -> 9% of each run, Pallas kernels for 0% -> 0%
where the time goes in v11:
time: 258 us; the launch traced here: 257 us
  waiting for transfers between devices  155 us (60%)
  starting transfers between devices  27.6 us (11%)
  Pallas kernels  22 us (9%)
  matrix products  15.2 us (6%)
  local copies, waits for them, and re-layouts  15.1 us (6%)
  between operations  14.4 us (6%)
  other arithmetic  6.84 us (3%)
    psum x1, waiting for transfers between devices, local(): attention_sum = lax.psum(attention_term.astype(jnp.bfloat16), 'head')  83.4 us
    all_to_all x1, waiting for transfers between devices, local(): lax.all_to_all(placed_queries, 'dp', split_axis=0, concat_axis=0, tiled=T...  20.5 us
    all_to_all x1, waiting for transfers between devices, local(): lax.all_to_all(back, 'dp', split_axis=0, concat_axis=0, tiled=True)  17.9 us
    reduce_scatter x1, waiting for transfers between devices, local(): lax.psum_scatter(down_part, 'head', scatter_dimension=1, tiled=True)  14.1 us
    all_to_all x1, waiting for transfers between devices, local(): lax.all_to_all(spread(jnp.concatenate([kept_keys, kept_values], axis=1),...  12.1 us
    pallas_call x1, Pallas kernels, attend(): pl.pallas_call(attend_block, grid_spec=grid_spec, out_shape=jax.ShapeDtyp...  9.28 us
    pallas_call x1, Pallas kernels, feed_forward(): pl.pallas_call(ffn_block, grid_spec=grid_spec, out_shape=[jax.ShapeDtypeS...  7.96 us
    all_to_all x1, starting transfers between devices, local(): lax.all_to_all(back, 'dp', split_axis=0, concat_axis=0, tiled=True)  7.78 us
  transfers between devices with their start and end apart: 6, of which 6 were waited for; matrix products, arithmetic and copies ran while one was open for 9% of the time, Pallas kernels for 0%

profile of v11, /device:TPU:2, one launch (start us, length us, event | category | flops | bytes accessed | tf_op | source)
XLA Modules:
  0.0 256.5 jit_solution(12802831611278996955)
XLA Ops:
  8.2 1.3 compare_select_fusion.2
  9.5 4.7 %shard_map.238 = (bf16[512,256]{1,0:T(8,128)(2,1)}, bf16[64,64,256]{2,1,0:T(8,128)(2,1)}) custom-call(s32[8]{0:T(128)} %get-tuple-element.17.where_ref, bf16[512,2048]{1,0:T(8,128)(2,1)} %hid_ref.1, bf16[2048,256]{1,0:T(8,128)(2,1)} %weight_ref.1, f32[1,256]{1,0:T(1,128)} %bitcast.112), custom_call_target="tpu_custom_call" | custom-call | tf_op jit(solution)/shard_map/pallas_call | solution.py:186
  14.2 7.8 %all-to-all-start = ((bf16[64,64,256]{2,1,0:T(8,128)(2,1)}), bf16[64,64,256]{2,1,0:T(8,128)(2,1)S(1)}, u32[]{:S(2)}, u32[]{:S(2)}) async-start(bf16[64,64,256]{2,1,0:T(8,128)(2,1)} %get-tuple-element.7), calls=%async_computation | async-start | bytes 4194304 | tf_op jit(solution)/shard_map/all_to_all | solution.py:290
  23.6 1.2 convolution_minimum_fusion.6
  24.9 2.6 convolution_convert_fusion.2
  27.4 20.5 %all-to-all-done.query_ref = bf16[64,64,256]{2,1,0:T(8,128)(2,1)S(1)} async-done(((bf16[64,64,256]{2,1,0:T(8,128)(2,1)}), bf16[64,64,256]{2,1,0:T(8,128)(2,1)S(1)}, u32[]{:S(2)}, u32[]{:S(2)}) %all-to-all-start) | async-done | bytes 2097184 | tf_op jit(solution)/shard_map/all_to_all | solution.py:290
  47.9 1.3 copy-done.1
  49.2 9.3 %shard_map.239 = bf16[64,66,256]{2,1,0:T(8,128)(2,1)} custom-call(s32[8]{0:T(128)} %multiply_add_fusion.1.where_ref, s32[8]{0:T(128)} %length_ref.1, bf16[64,64,256]{2,1,0:T(8,128)(2,1)} %copy-done.1, bf16[8,512,256]{2,1,0:T(8,128)(2,1)} %key_ref.1, bf16[8,512,256]{2,1,0:T(8,128)(2,1)} %value_ref.1), custom_call_target="tpu_custom_call" | custom-call | tf_op jit(solution)/shard_map/pallas_call | solution.py:152
  58.5 7.8 %all-to-all-start.1 = ((bf16[64,66,256]{2,1,0:T(8,128)(2,1)}), bf16[64,66,256]{2,1,0:T(8,128)(2,1)}, u32[]{:S(2)}, u32[]{:S(2)}) async-start(bf16[64,66,256]{2,1,0:T(8,128)(2,1)} %shard_map.239), calls=%async_computation.1 | async-start | bytes 4718592 | tf_op jit(solution)/shard_map/all_to_all | solution.py:301
  69.0 1.4 convolution_minimum_fusion.4
  72.2 2.7 %fusion.5 = bf16[512,256]{1,0:T(8,128)(2,1)} fusion(bf16[512,2048]{1,0:T(8,128)(2,1)S(1)} %copy-done.2, bf16[2048,256]{1,0:T(8,128)(2,1)} %param.34, f32[256]{0:T(256)S(1)} %copy-done.11), kind=kOutput, calls=%fused_computation.15 | convolution fusion | flops 537133056 | bytes 3408896 | tf_op jit(solution)/shard_map/dot_general | solution.py:257
  75.9 1.3 fusion.39
  77.4 17.9 %all-to-all-done.1 = bf16[64,66,256]{2,1,0:T(8,128)(2,1)} async-done(((bf16[64,66,256]{2,1,0:T(8,128)(2,1)}), bf16[64,66,256]{2,1,0:T(8,128)(2,1)}, u32[]{:S(2)}, u32[]{:S(2)}) %all-to-all-start.1) | async-done | bytes 2162720 | tf_op jit(solution)/shard_map/all_to_all | solution.py:301
  95.3 2.2 gather_fusion.1
  98.8 2.1 convolution_convert_fusion.1
  100.9 83.4 %all-reduce.2.cloned.1.call-done.attn_ref = bf16[512,2048]{1,0:T(8,128)(2,1)} async-done(((bf16[512,2048]{1,0:T(8,128)(2,1)}), bf16[512,2048]{1,0:T(8,128)(2,1)}) %all-reduce.2.cloned.1.call-update) | async-done | bytes 2097168 | tf_op jit(solution)/shard_map/psum | solution.py:323
  184.3 8.0 %shard_map.240 = (bf16[512,256]{1,0:T(8,128)(2,1)}, bf16[512,2048]{1,0:T(8,128)(2,1)}) custom-call(s32[1]{0:T(128)} %bitcast.column_ref, bf16[512,2048]{1,0:T(8,128)(2,1)} %all-reduce.2.cloned.1.call-done.attn_ref, bf16[512,2048]{1,0:T(8,128)(2,1)} %hid_ref.1, f32[1,2048]{1,0:T(1,128)} %bitcast.108, f32[1,2048]{1,0:T(1,128)} %bitcast.109, ...), custom_call_target="tpu_custom_call" | custom-call | tf_op jit(solution)/shard_map/pallas_call | solution.py:87
  195.5 1.3 copy.61
  196.8 7.4 %all-to-all-start.3 = ((bf16[64,32,256]{2,1,0:T(8,128)(2,1)}), bf16[64,32,256]{2,1,0:T(8,128)(2,1)S(1)}, u32[]{:S(2)}, u32[]{:S(2)}) async-start(bf16[64,32,256]{2,1,0:T(8,128)(2,1)} %bitcast.32), calls=%async_computation.4 | async-start | bytes 2097152 | tf_op jit(solution)/shard_map/all_to_all | solution.py:291
  206.5 12.1 %all-to-all-done.3 = bf16[64,32,256]{2,1,0:T(8,128)(2,1)S(1)} async-done(((bf16[64,32,256]{2,1,0:T(8,128)(2,1)}), bf16[64,32,256]{2,1,0:T(8,128)(2,1)S(1)}, u32[]{:S(2)}, u32[]{:S(2)}) %all-to-all-start.3) | async-done | bytes 1048608 | tf_op jit(solution)/shard_map/all_to_all | solution.py:291
  219.2 14.1 %reduce-scatter.2.cloned.1.call-done = bf16[512,256]{1,0:T(8,128)(2,1)} async-done(((bf16[512,2048]{1,0:T(8,128)(2,1)}), bf16[512,256]{1,0:T(8,128)(2,1)}) %reduce-scatter.2.cloned.1.call-update) | async-done | bytes 262160 | tf_op jit(solution)/shard_map/reduce_scatter | solution.py:336
  235.2 4.6 %all-to-all-start.2 = ((f32[8,2,512]{2,1,0:T(2,128)}), f32[8,2,512]{2,1,0:T(2,128)S(1)}, u32[]{:S(2)}, u32[]{:S(2)}) async-start(f32[8,2,512]{2,1,0:T(2,128)} %broadcast_in_dim.54), calls=%async_computation.3 | async-start | bytes 65536 | tf_op jit(solution)/shard_map/all_to_all | solution.py:345
  240.4 7.4 %all-to-all-done.2 = f32[8,2,512]{2,1,0:T(2,128)S(1)} async-done(((f32[8,2,512]{2,1,0:T(2,128)}), f32[8,2,512]{2,1,0:T(2,128)S(1)}, u32[]{:S(2)}, u32[]{:S(2)}) %all-to-all-start.2) | async-done | bytes 32800 | tf_op jit(solution)/shard_map/all_to_all | solution.py:345
  247.8 1.9 add_convert_fusion
  (80 shorter events, 18.1 us)
Async XLA Ops:
  7.2 91.6 %copy-start = (bf16[256,2048]{1,0:T(8,128)(2,1)S(1)}, bf16[256,2048]{1,0:T(8,128)(2,1)}, u32[]{:S(2)}) copy-start(bf16[256,2048]{1,0:T(8,128)(2,1)} %param.36) | copy-start | bytes 3145732
  14.2 7.8 %copy-start.7 = (s32[256]{0:T(256)S(1)}, s32[256]{0:T(256)}, u32[]{:S(2)}) copy-start(s32[256]{0:T(256)} %param.25) | copy-start | bytes 3076
  14.2 9.4 %copy-start.9 = (s32[8,64]{1,0:T(8,128)S(1)}, s32[8,64]{1,0:T(8,128)}, u32[]{:S(2)}) copy-start(s32[8,64]{1,0:T(8,128)} %param.24) | copy-start | bytes 6148
  14.2 33.7 %all-to-all-start = ((bf16[64,64,256]{2,1,0:T(8,128)(2,1)}), bf16[64,64,256]{2,1,0:T(8,128)(2,1)S(1)}, u32[]{:S(2)}, u32[]{:S(2)}) async-start(bf16[64,64,256]{2,1,0:T(8,128)(2,1)} %get-tuple-element.7), calls=%async_computation | async-start | bytes 4194304 | tf_op jit(solution)/shard_map/all_to_all | solution.py:290
  47.9 1.3 copy-start.1
  58.5 7.8 %copy-start.4 = (f32[8,64,64]{2,1,0:T(8,128)S(1)}, f32[8,64,64]{2,1,0:T(8,128)}, u32[]{:S(2)}) copy-start(f32[8,64,64]{2,1,0:T(8,128)} %convolution_minimum_fusion.6) | copy-start | bytes 393220
  58.5 9.0 %copy-start.6 = (bf16[512,256]{1,0:T(8,128)(2,1)S(1)}, bf16[512,256]{1,0:T(8,128)(2,1)}, u32[]{:S(2)}) copy-start(bf16[512,256]{1,0:T(8,128)(2,1)} %get-tuple-element.8) | copy-start | bytes 786436
  58.5 36.7 %all-to-all-start.1 = ((bf16[64,66,256]{2,1,0:T(8,128)(2,1)}), bf16[64,66,256]{2,1,0:T(8,128)(2,1)}, u32[]{:S(2)}, u32[]{:S(2)}) async-start(bf16[64,66,256]{2,1,0:T(8,128)(2,1)} %shard_map.239), calls=%async_computation.1 | async-start | bytes 4718592 | tf_op jit(solution)/shard_map/all_to_all | solution.py:301
  66.3 118.0 %all-reduce.2.cloned.1.call-start = ((), (), s32[]{:S(2)}) async-start(), calls=%async_computation.5 | async-start | bytes 4194304 | tf_op jit(solution)/shard_map/psum | solution.py:323
  68.3 3.9 %copy-start.2 = (bf16[512,2048]{1,0:T(8,128)(2,1)S(1)}, bf16[512,2048]{1,0:T(8,128)(2,1)}, u32[]{:S(2)}) copy-start(bf16[512,2048]{1,0:T(8,128)(2,1)} %hid_ref.1) | copy-start | bytes 6291460
  68.3 4.0 %copy-start.11 = (f32[256]{0:T(256)S(1)}, f32[256]{0:T(256)}, u32[]{:S(2)}) copy-start(f32[256]{0:T(256)} %param.35) | copy-start | bytes 3076
  100.9 132.4 %reduce-scatter.2.cloned.1.call-start = ((), (), s32[]{:S(2)}) async-start(), calls=%async_computation.6 | async-start | bytes 2359296 | tf_op jit(solution)/shard_map/reduce_scatter | solution.py:336
  192.2 0.7 copy-start.10
  192.2 1.7 copy-start.3
  192.3 2.6 copy-start.12
  192.3 2.8 %copy-start.8 = (s32[8]{0:T(128)S(1)}, s32[8]{0:T(128)}, u32[]{:S(2)}) copy-start(s32[8]{0:T(128)} %get-tuple-element.17.where_ref) | copy-start | bytes 100
  195.5 37.8 %copy-start.5 = (bf16[512,256]{1,0:T(8,128)(2,1)S(1)}, bf16[512,256]{1,0:T(8,128)(2,1)}, u32[]{:S(2)}) copy-start(bf16[512,256]{1,0:T(8,128)(2,1)} %get-tuple-element.10) | copy-start | bytes 786436
  196.8 21.9 %all-to-all-start.3 = ((bf16[64,32,256]{2,1,0:T(8,128)(2,1)}), bf16[64,32,256]{2,1,0:T(8,128)(2,1)S(1)}, u32[]{:S(2)}, u32[]{:S(2)}) async-start(bf16[64,32,256]{2,1,0:T(8,128)(2,1)} %bitcast.32), calls=%async_computation.4 | async-start | bytes 2097152 | tf_op jit(solution)/shard_map/all_to_all | solution.py:291
  235.2 12.6 %all-to-all-start.2 = ((f32[8,2,512]{2,1,0:T(2,128)}), f32[8,2,512]{2,1,0:T(2,128)S(1)}, u32[]{:S(2)}, u32[]{:S(2)}) async-start(f32[8,2,512]{2,1,0:T(2,128)} %broadcast_in_dim.54), calls=%async_computation.3 | async-start | bytes 65536 | tf_op jit(solution)/shard_map/all_to_all | solution.py:345
Sparse Core Ops, SparseCore 0:
  101.0 83.2 all-reduce.1
  192.4 40.8 reduce-scatter.1

commit v12 on v11

--- a/solution.py
+++ b/solution.py
@@ -61,7 +61,7 @@
     )
 
 
-def feed_forward(attn, hidden, b_out, gain, shift, w_up, b_up, w_down, column, feature, block=256):
+def feed_forward(attn, hidden, b_out, gain, shift, w_up, b_up, w_down, column, feature, block=512):
     tokens, model = hidden.shape
     units = w_up.shape[1]
     row = lambda i, c: (i, 0)

time: 258 us -> 258 us (level)
  no operation moved by 1% of the time
where the time goes in v12:
time: 258 us; the launch traced here: 257 us
  waiting for transfers between devices  155 us (60%)
  starting transfers between devices  27.9 us (11%)
  Pallas kernels  22.6 us (9%)
  matrix products  15.2 us (6%)
  local copies, waits for them, and re-layouts  15.1 us (6%)
  between operations  14.4 us (6%)
  other arithmetic  6.84 us (3%)
    psum x1, waiting for transfers between devices, local(): attention_sum = lax.psum(attention_term.astype(jnp.bfloat16), 'head')  83.2 us
    all_to_all x1, waiting for transfers between devices, local(): lax.all_to_all(placed_queries, 'dp', split_axis=0, concat_axis=0, tiled=T...  20.5 us
    all_to_all x1, waiting for transfers between devices, local(): lax.all_to_all(back, 'dp', split_axis=0, concat_axis=0, tiled=True)  17.9 us
    reduce_scatter x1, waiting for transfers between devices, local(): lax.psum_scatter(down_part, 'head', scatter_dimension=1, tiled=True)  14.1 us
    all_to_all x1, waiting for transfers between devices, local(): lax.all_to_all(spread(jnp.concatenate([kept_keys, kept_values], axis=1),...  12.1 us
    pallas_call x1, Pallas kernels, attend(): pl.pallas_call(attend_block, grid_spec=grid_spec, out_shape=jax.ShapeDtyp...  9.28 us
    pallas_call x1, Pallas kernels, feed_forward(): pl.pallas_call(ffn_block, grid_spec=grid_spec, out_shape=[jax.ShapeDtypeS...  8.55 us
    all_to_all x1, starting transfers between devices, local(): lax.all_to_all(back, 'dp', split_axis=0, concat_axis=0, tiled=True)  7.78 us
  transfers between devices with their start and end apart: 6, of which 6 were waited for; matrix products, arithmetic and copies ran while one was open for 9% of the time, Pallas kernels for 0%

profile of v12, /device:TPU:2, one launch (start us, length us, event | category | flops | bytes accessed | tf_op | source)
XLA Modules:
  0.0 257.2 jit_solution(7291082768773042192)
XLA Ops:
  8.2 1.3 compare_select_fusion.2
  9.5 4.7 %shard_map.238 = (bf16[512,256]{1,0:T(8,128)(2,1)}, bf16[64,64,256]{2,1,0:T(8,128)(2,1)}) custom-call(s32[8]{0:T(128)} %get-tuple-element.17.where_ref, bf16[512,2048]{1,0:T(8,128)(2,1)} %hid_ref.1, bf16[2048,256]{1,0:T(8,128)(2,1)} %weight_ref.1, f32[1,256]{1,0:T(1,128)} %bitcast.112), custom_call_target="tpu_custom_call" | custom-call | tf_op jit(solution)/shard_map/pallas_call | solution.py:186
  14.2 7.8 %all-to-all-start = ((bf16[64,64,256]{2,1,0:T(8,128)(2,1)}), bf16[64,64,256]{2,1,0:T(8,128)(2,1)S(1)}, u32[]{:S(2)}, u32[]{:S(2)}) async-start(bf16[64,64,256]{2,1,0:T(8,128)(2,1)} %get-tuple-element.7), calls=%async_computation | async-start | bytes 4194304 | tf_op jit(solution)/shard_map/all_to_all | solution.py:290
  23.6 1.2 convolution_minimum_fusion.6
  24.9 2.6 convolution_convert_fusion.2
  27.4 20.5 %all-to-all-done.query_ref = bf16[64,64,256]{2,1,0:T(8,128)(2,1)S(1)} async-done(((bf16[64,64,256]{2,1,0:T(8,128)(2,1)}), bf16[64,64,256]{2,1,0:T(8,128)(2,1)S(1)}, u32[]{:S(2)}, u32[]{:S(2)}) %all-to-all-start) | async-done | bytes 2097184 | tf_op jit(solution)/shard_map/all_to_all | solution.py:290
  47.9 1.3 copy-done.1
  49.2 9.3 %shard_map.239 = bf16[64,66,256]{2,1,0:T(8,128)(2,1)} custom-call(s32[8]{0:T(128)} %multiply_add_fusion.1.where_ref, s32[8]{0:T(128)} %length_ref.1, bf16[64,64,256]{2,1,0:T(8,128)(2,1)} %copy-done.1, bf16[8,512,256]{2,1,0:T(8,128)(2,1)} %key_ref.1, bf16[8,512,256]{2,1,0:T(8,128)(2,1)} %value_ref.1), custom_call_target="tpu_custom_call" | custom-call | tf_op jit(solution)/shard_map/pallas_call | solution.py:152
  58.5 7.8 %all-to-all-start.1 = ((bf16[64,66,256]{2,1,0:T(8,128)(2,1)}), bf16[64,66,256]{2,1,0:T(8,128)(2,1)}, u32[]{:S(2)}, u32[]{:S(2)}) async-start(bf16[64,66,256]{2,1,0:T(8,128)(2,1)} %shard_map.239), calls=%async_computation.1 | async-start | bytes 4718592 | tf_op jit(solution)/shard_map/all_to_all | solution.py:301
  69.0 1.4 convolution_minimum_fusion.4
  72.2 2.7 %fusion.5 = bf16[512,256]{1,0:T(8,128)(2,1)} fusion(bf16[512,2048]{1,0:T(8,128)(2,1)S(1)} %copy-done.2, bf16[2048,256]{1,0:T(8,128)(2,1)} %param.34, f32[256]{0:T(256)S(1)} %copy-done.11), kind=kOutput, calls=%fused_computation.15 | convolution fusion | flops 537133056 | bytes 3408896 | tf_op jit(solution)/shard_map/dot_general | solution.py:257
  75.9 1.3 fusion.39
  77.4 17.9 %all-to-all-done.1 = bf16[64,66,256]{2,1,0:T(8,128)(2,1)} async-done(((bf16[64,66,256]{2,1,0:T(8,128)(2,1)}), bf16[64,66,256]{2,1,0:T(8,128)(2,1)}, u32[]{:S(2)}, u32[]{:S(2)}) %all-to-all-start.1) | async-done | bytes 2162720 | tf_op jit(solution)/shard_map/all_to_all | solution.py:301
  95.3 2.2 gather_fusion.1
  98.8 2.1 convolution_convert_fusion.1
  101.1 83.2 %all-reduce.2.cloned.1.call-done.attn_ref = bf16[512,2048]{1,0:T(8,128)(2,1)} async-done(((bf16[512,2048]{1,0:T(8,128)(2,1)}), bf16[512,2048]{1,0:T(8,128)(2,1)}) %all-reduce.2.cloned.1.call-update) | async-done | bytes 2097168 | tf_op jit(solution)/shard_map/psum | solution.py:323
  184.4 8.5 %shard_map.240 = (bf16[512,256]{1,0:T(8,128)(2,1)}, bf16[512,2048]{1,0:T(8,128)(2,1)}) custom-call(s32[1]{0:T(128)} %bitcast.column_ref, bf16[512,2048]{1,0:T(8,128)(2,1)} %all-reduce.2.cloned.1.call-done.attn_ref, bf16[512,2048]{1,0:T(8,128)(2,1)} %hid_ref.1, f32[1,2048]{1,0:T(1,128)} %bitcast.108, f32[1,2048]{1,0:T(1,128)} %bitcast.109, ...), custom_call_target="tpu_custom_call" | custom-call | tf_op jit(solution)/shard_map/pallas_call | solution.py:87
  196.2 1.3 copy.61
  197.5 7.4 %all-to-all-start.3 = ((bf16[64,32,256]{2,1,0:T(8,128)(2,1)}), bf16[64,32,256]{2,1,0:T(8,128)(2,1)S(1)}, u32[]{:S(2)}, u32[]{:S(2)}) async-start(bf16[64,32,256]{2,1,0:T(8,128)(2,1)} %bitcast.32), calls=%async_computation.4 | async-start | bytes 2097152 | tf_op jit(solution)/shard_map/all_to_all | solution.py:291
  207.2 12.1 %all-to-all-done.3 = bf16[64,32,256]{2,1,0:T(8,128)(2,1)S(1)} async-done(((bf16[64,32,256]{2,1,0:T(8,128)(2,1)}), bf16[64,32,256]{2,1,0:T(8,128)(2,1)S(1)}, u32[]{:S(2)}, u32[]{:S(2)}) %all-to-all-start.3) | async-done | bytes 1048608 | tf_op jit(solution)/shard_map/all_to_all | solution.py:291
  219.9 14.1 %reduce-scatter.2.cloned.1.call-done = bf16[512,256]{1,0:T(8,128)(2,1)} async-done(((bf16[512,2048]{1,0:T(8,128)(2,1)}), bf16[512,256]{1,0:T(8,128)(2,1)}) %reduce-scatter.2.cloned.1.call-update) | async-done | bytes 262160 | tf_op jit(solution)/shard_map/reduce_scatter | solution.py:336
  235.8 4.7 %all-to-all-start.2 = ((f32[8,2,512]{2,1,0:T(2,128)}), f32[8,2,512]{2,1,0:T(2,128)S(1)}, u32[]{:S(2)}, u32[]{:S(2)}) async-start(f32[8,2,512]{2,1,0:T(2,128)} %broadcast_in_dim.54), calls=%async_computation.3 | async-start | bytes 65536 | tf_op jit(solution)/shard_map/all_to_all | solution.py:345
  241.1 7.4 %all-to-all-done.2 = f32[8,2,512]{2,1,0:T(2,128)S(1)} async-done(((f32[8,2,512]{2,1,0:T(2,128)}), f32[8,2,512]{2,1,0:T(2,128)S(1)}, u32[]{:S(2)}, u32[]{:S(2)}) %all-to-all-start.2) | async-done | bytes 32800 | tf_op jit(solution)/shard_map/all_to_all | solution.py:345
  248.5 1.9 add_convert_fusion
  (80 shorter events, 18.2 us)
Async XLA Ops:
  7.2 91.6 %copy-start = (bf16[256,2048]{1,0:T(8,128)(2,1)S(1)}, bf16[256,2048]{1,0:T(8,128)(2,1)}, u32[]{:S(2)}) copy-start(bf16[256,2048]{1,0:T(8,128)(2,1)} %param.36) | copy-start | bytes 3145732
  14.2 7.8 %copy-start.7 = (s32[256]{0:T(256)S(1)}, s32[256]{0:T(256)}, u32[]{:S(2)}) copy-start(s32[256]{0:T(256)} %param.25) | copy-start | bytes 3076
  14.2 9.4 %copy-start.9 = (s32[8,64]{1,0:T(8,128)S(1)}, s32[8,64]{1,0:T(8,128)}, u32[]{:S(2)}) copy-start(s32[8,64]{1,0:T(8,128)} %param.24) | copy-start | bytes 6148
  14.2 33.7 %all-to-all-start = ((bf16[64,64,256]{2,1,0:T(8,128)(2,1)}), bf16[64,64,256]{2,1,0:T(8,128)(2,1)S(1)}, u32[]{:S(2)}, u32[]{:S(2)}) async-start(bf16[64,64,256]{2,1,0:T(8,128)(2,1)} %get-tuple-element.7), calls=%async_computation | async-start | bytes 4194304 | tf_op jit(solution)/shard_map/all_to_all | solution.py:290
  47.9 1.3 copy-start.1
  58.5 7.8 %copy-start.4 = (f32[8,64,64]{2,1,0:T(8,128)S(1)}, f32[8,64,64]{2,1,0:T(8,128)}, u32[]{:S(2)}) copy-start(f32[8,64,64]{2,1,0:T(8,128)} %convolution_minimum_fusion.6) | copy-start | bytes 393220
  58.5 9.0 %copy-start.6 = (bf16[512,256]{1,0:T(8,128)(2,1)S(1)}, bf16[512,256]{1,0:T(8,128)(2,1)}, u32[]{:S(2)}) copy-start(bf16[512,256]{1,0:T(8,128)(2,1)} %get-tuple-element.8) | copy-start | bytes 786436
  58.5 36.7 %all-to-all-start.1 = ((bf16[64,66,256]{2,1,0:T(8,128)(2,1)}), bf16[64,66,256]{2,1,0:T(8,128)(2,1)}, u32[]{:S(2)}, u32[]{:S(2)}) async-start(bf16[64,66,256]{2,1,0:T(8,128)(2,1)} %shard_map.239), calls=%async_computation.1 | async-start | bytes 4718592 | tf_op jit(solution)/shard_map/all_to_all | solution.py:301
  66.3 118.0 %all-reduce.2.cloned.1.call-start = ((), (), s32[]{:S(2)}) async-start(), calls=%async_computation.5 | async-start | bytes 4194304 | tf_op jit(solution)/shard_map/psum | solution.py:323
  68.3 3.9 %copy-start.2 = (bf16[512,2048]{1,0:T(8,128)(2,1)S(1)}, bf16[512,2048]{1,0:T(8,128)(2,1)}, u32[]{:S(2)}) copy-start(bf16[512,2048]{1,0:T(8,128)(2,1)} %hid_ref.1) | copy-start | bytes 6291460
  68.3 4.0 %copy-start.11 = (f32[256]{0:T(256)S(1)}, f32[256]{0:T(256)}, u32[]{:S(2)}) copy-start(f32[256]{0:T(256)} %param.35) | copy-start | bytes 3076
  100.9 133.1 %reduce-scatter.2.cloned.1.call-start = ((), (), s32[]{:S(2)}) async-start(), calls=%async_computation.6 | async-start | bytes 2359296 | tf_op jit(solution)/shard_map/reduce_scatter | solution.py:336
  192.9 0.7 copy-start.10
  192.9 1.7 copy-start.3
  192.9 2.6 copy-start.12
  192.9 2.8 %copy-start.8 = (s32[8]{0:T(128)S(1)}, s32[8]{0:T(128)}, u32[]{:S(2)}) copy-start(s32[8]{0:T(128)} %get-tuple-element.17.where_ref) | copy-start | bytes 100
  196.2 37.8 %copy-start.5 = (bf16[512,256]{1,0:T(8,128)(2,1)S(1)}, bf16[512,256]{1,0:T(8,128)(2,1)}, u32[]{:S(2)}) copy-start(bf16[512,256]{1,0:T(8,128)(2,1)} %get-tuple-element.10) | copy-start | bytes 786436
  197.5 21.9 %all-to-all-start.3 = ((bf16[64,32,256]{2,1,0:T(8,128)(2,1)}), bf16[64,32,256]{2,1,0:T(8,128)(2,1)S(1)}, u32[]{:S(2)}, u32[]{:S(2)}) async-start(bf16[64,32,256]{2,1,0:T(8,128)(2,1)} %bitcast.32), calls=%async_computation.4 | async-start | bytes 2097152 | tf_op jit(solution)/shard_map/all_to_all | solution.py:291
  235.8 12.7 %all-to-all-start.2 = ((f32[8,2,512]{2,1,0:T(2,128)}), f32[8,2,512]{2,1,0:T(2,128)S(1)}, u32[]{:S(2)}, u32[]{:S(2)}) async-start(f32[8,2,512]{2,1,0:T(2,128)} %broadcast_in_dim.54), calls=%async_computation.3 | async-start | bytes 65536 | tf_op jit(solution)/shard_map/all_to_all | solution.py:345
Sparse Core Ops, SparseCore 0:
  101.0 83.3 all-reduce.1
  193.1 40.8 reduce-scatter.1

commit v13 on v12

--- a/solution.py
+++ b/solution.py
@@ -61,7 +61,7 @@
     )
 
 
-def feed_forward(attn, hidden, b_out, gain, shift, w_up, b_up, w_down, column, feature, block=512):
+def feed_forward(attn, hidden, b_out, gain, shift, w_up, b_up, w_down, column, feature, block=128):
     tokens, model = hidden.shape
     units = w_up.shape[1]
     row = lambda i, c: (i, 0)

time: 258 us -> 258 us (level)
  no operation moved by 1% of the time
where the time goes in v13:
time: 258 us; the launch traced here: 257 us
  waiting for transfers between devices  155 us (60%)
  starting transfers between devices  27.7 us (11%)
  Pallas kernels  22.5 us (9%)
  matrix products  15.2 us (6%)
  local copies, waits for them, and re-layouts  15.1 us (6%)
  between operations  14.4 us (6%)
  other arithmetic  6.84 us (3%)
    psum x1, waiting for transfers between devices, local(): attention_sum = lax.psum(attention_term.astype(jnp.bfloat16), 'head')  83.4 us
    all_to_all x1, waiting for transfers between devices, local(): lax.all_to_all(placed_queries, 'dp', split_axis=0, concat_axis=0, tiled=T...  20.5 us
    all_to_all x1, waiting for transfers between devices, local(): lax.all_to_all(back, 'dp', split_axis=0, concat_axis=0, tiled=True)  17.9 us
    reduce_scatter x1, waiting for transfers between devices, local(): lax.psum_scatter(down_part, 'head', scatter_dimension=1, tiled=True)  14 us
    all_to_all x1, waiting for transfers between devices, local(): lax.all_to_all(spread(jnp.concatenate([kept_keys, kept_values], axis=1),...  12.1 us
    pallas_call x1, Pallas kernels, attend(): pl.pallas_call(attend_block, grid_spec=grid_spec, out_shape=jax.ShapeDtyp...  9.28 us
    pallas_call x1, Pallas kernels, feed_forward(): pl.pallas_call(ffn_block, grid_spec=grid_spec, out_shape=[jax.ShapeDtypeS...  8.47 us
    all_to_all x1, starting transfers between devices, local(): lax.all_to_all(back, 'dp', split_axis=0, concat_axis=0, tiled=True)  7.76 us
  transfers between devices with their start and end apart: 6, of which 6 were waited for; matrix products, arithmetic and copies ran while one was open for 9% of the time, Pallas kernels for 0%

profile of v13, /device:TPU:2, one launch (start us, length us, event | category | flops | bytes accessed | tf_op | source)
XLA Modules:
  0.0 257.1 jit_solution(16326204665733352673)
XLA Ops:
  8.2 1.3 compare_select_fusion.2
  9.5 4.7 %shard_map.238 = (bf16[512,256]{1,0:T(8,128)(2,1)}, bf16[64,64,256]{2,1,0:T(8,128)(2,1)}) custom-call(s32[8]{0:T(128)} %get-tuple-element.17.where_ref, bf16[512,2048]{1,0:T(8,128)(2,1)} %hid_ref.1, bf16[2048,256]{1,0:T(8,128)(2,1)} %weight_ref.1, f32[1,256]{1,0:T(1,128)} %bitcast.112), custom_call_target="tpu_custom_call" | custom-call | tf_op jit(solution)/shard_map/pallas_call | solution.py:186
  14.2 7.8 %all-to-all-start = ((bf16[64,64,256]{2,1,0:T(8,128)(2,1)}), bf16[64,64,256]{2,1,0:T(8,128)(2,1)S(1)}, u32[]{:S(2)}, u32[]{:S(2)}) async-start(bf16[64,64,256]{2,1,0:T(8,128)(2,1)} %get-tuple-element.7), calls=%async_computation | async-start | bytes 4194304 | tf_op jit(solution)/shard_map/all_to_all | solution.py:290
  23.6 1.2 convolution_minimum_fusion.6
  24.9 2.6 convolution_convert_fusion.2
  27.4 20.5 %all-to-all-done.query_ref = bf16[64,64,256]{2,1,0:T(8,128)(2,1)S(1)} async-done(((bf16[64,64,256]{2,1,0:T(8,128)(2,1)}), bf16[64,64,256]{2,1,0:T(8,128)(2,1)S(1)}, u32[]{:S(2)}, u32[]{:S(2)}) %all-to-all-start) | async-done | bytes 2097184 | tf_op jit(solution)/shard_map/all_to_all | solution.py:290
  47.9 1.3 copy-done.1
  49.2 9.3 %shard_map.239 = bf16[64,66,256]{2,1,0:T(8,128)(2,1)} custom-call(s32[8]{0:T(128)} %multiply_add_fusion.1.where_ref, s32[8]{0:T(128)} %length_ref.1, bf16[64,64,256]{2,1,0:T(8,128)(2,1)} %copy-done.1, bf16[8,512,256]{2,1,0:T(8,128)(2,1)} %key_ref.1, bf16[8,512,256]{2,1,0:T(8,128)(2,1)} %value_ref.1), custom_call_target="tpu_custom_call" | custom-call | tf_op jit(solution)/shard_map/pallas_call | solution.py:152
  58.5 7.8 %all-to-all-start.1 = ((bf16[64,66,256]{2,1,0:T(8,128)(2,1)}), bf16[64,66,256]{2,1,0:T(8,128)(2,1)}, u32[]{:S(2)}, u32[]{:S(2)}) async-start(bf16[64,66,256]{2,1,0:T(8,128)(2,1)} %shard_map.239), calls=%async_computation.1 | async-start | bytes 4718592 | tf_op jit(solution)/shard_map/all_to_all | solution.py:301
  69.0 1.4 convolution_minimum_fusion.4
  72.2 2.7 %fusion.5 = bf16[512,256]{1,0:T(8,128)(2,1)} fusion(bf16[512,2048]{1,0:T(8,128)(2,1)S(1)} %copy-done.2, bf16[2048,256]{1,0:T(8,128)(2,1)} %param.34, f32[256]{0:T(256)S(1)} %copy-done.11), kind=kOutput, calls=%fused_computation.15 | convolution fusion | flops 537133056 | bytes 3408896 | tf_op jit(solution)/shard_map/dot_general | solution.py:257
  75.9 1.3 fusion.39
  77.4 17.9 %all-to-all-done.1 = bf16[64,66,256]{2,1,0:T(8,128)(2,1)} async-done(((bf16[64,66,256]{2,1,0:T(8,128)(2,1)}), bf16[64,66,256]{2,1,0:T(8,128)(2,1)}, u32[]{:S(2)}, u32[]{:S(2)}) %all-to-all-start.1) | async-done | bytes 2162720 | tf_op jit(solution)/shard_map/all_to_all | solution.py:301
  95.2 2.2 gather_fusion.1
  98.8 2.1 convolution_convert_fusion.1
  100.9 83.4 %all-reduce.2.cloned.1.call-done.attn_ref = bf16[512,2048]{1,0:T(8,128)(2,1)} async-done(((bf16[512,2048]{1,0:T(8,128)(2,1)}), bf16[512,2048]{1,0:T(8,128)(2,1)}) %all-reduce.2.cloned.1.call-update) | async-done | bytes 2097168 | tf_op jit(solution)/shard_map/psum | solution.py:323
  184.3 8.5 %shard_map.240 = (bf16[512,256]{1,0:T(8,128)(2,1)}, bf16[512,2048]{1,0:T(8,128)(2,1)}) custom-call(s32[1]{0:T(128)} %bitcast.column_ref, bf16[512,2048]{1,0:T(8,128)(2,1)} %all-reduce.2.cloned.1.call-done.attn_ref, bf16[512,2048]{1,0:T(8,128)(2,1)} %hid_ref.1, f32[1,2048]{1,0:T(1,128)} %bitcast.108, f32[1,2048]{1,0:T(1,128)} %bitcast.109, ...), custom_call_target="tpu_custom_call" | custom-call | tf_op jit(solution)/shard_map/pallas_call | solution.py:87
  196.1 1.3 copy.61
  197.3 7.4 %all-to-all-start.3 = ((bf16[64,32,256]{2,1,0:T(8,128)(2,1)}), bf16[64,32,256]{2,1,0:T(8,128)(2,1)S(1)}, u32[]{:S(2)}, u32[]{:S(2)}) async-start(bf16[64,32,256]{2,1,0:T(8,128)(2,1)} %bitcast.32), calls=%async_computation.4 | async-start | bytes 2097152 | tf_op jit(solution)/shard_map/all_to_all | solution.py:291
  207.1 12.1 %all-to-all-done.3 = bf16[64,32,256]{2,1,0:T(8,128)(2,1)S(1)} async-done(((bf16[64,32,256]{2,1,0:T(8,128)(2,1)}), bf16[64,32,256]{2,1,0:T(8,128)(2,1)S(1)}, u32[]{:S(2)}, u32[]{:S(2)}) %all-to-all-start.3) | async-done | bytes 1048608 | tf_op jit(solution)/shard_map/all_to_all | solution.py:291
  219.7 14.0 %reduce-scatter.2.cloned.1.call-done = bf16[512,256]{1,0:T(8,128)(2,1)} async-done(((bf16[512,2048]{1,0:T(8,128)(2,1)}), bf16[512,256]{1,0:T(8,128)(2,1)}) %reduce-scatter.2.cloned.1.call-update) | async-done | bytes 262160 | tf_op jit(solution)/shard_map/reduce_scatter | solution.py:336
  235.6 4.7 %all-to-all-start.2 = ((f32[8,2,512]{2,1,0:T(2,128)}), f32[8,2,512]{2,1,0:T(2,128)S(1)}, u32[]{:S(2)}, u32[]{:S(2)}) async-start(f32[8,2,512]{2,1,0:T(2,128)} %broadcast_in_dim.54), calls=%async_computation.3 | async-start | bytes 65536 | tf_op jit(solution)/shard_map/all_to_all | solution.py:345
  240.9 7.4 %all-to-all-done.2 = f32[8,2,512]{2,1,0:T(2,128)S(1)} async-done(((f32[8,2,512]{2,1,0:T(2,128)}), f32[8,2,512]{2,1,0:T(2,128)S(1)}, u32[]{:S(2)}, u32[]{:S(2)}) %all-to-all-start.2) | async-done | bytes 32800 | tf_op jit(solution)/shard_map/all_to_all | solution.py:345
  248.4 1.9 add_convert_fusion
  (80 shorter events, 18.1 us)
Async XLA Ops:
  7.2 91.6 %copy-start = (bf16[256,2048]{1,0:T(8,128)(2,1)S(1)}, bf16[256,2048]{1,0:T(8,128)(2,1)}, u32[]{:S(2)}) copy-start(bf16[256,2048]{1,0:T(8,128)(2,1)} %param.36) | copy-start | bytes 3145732
  14.2 7.8 %copy-start.7 = (s32[256]{0:T(256)S(1)}, s32[256]{0:T(256)}, u32[]{:S(2)}) copy-start(s32[256]{0:T(256)} %param.25) | copy-start | bytes 3076
  14.2 9.4 %copy-start.9 = (s32[8,64]{1,0:T(8,128)S(1)}, s32[8,64]{1,0:T(8,128)}, u32[]{:S(2)}) copy-start(s32[8,64]{1,0:T(8,128)} %param.24) | copy-start | bytes 6148
  14.2 33.7 %all-to-all-start = ((bf16[64,64,256]{2,1,0:T(8,128)(2,1)}), bf16[64,64,256]{2,1,0:T(8,128)(2,1)S(1)}, u32[]{:S(2)}, u32[]{:S(2)}) async-start(bf16[64,64,256]{2,1,0:T(8,128)(2,1)} %get-tuple-element.7), calls=%async_computation | async-start | bytes 4194304 | tf_op jit(solution)/shard_map/all_to_all | solution.py:290
  47.9 1.3 copy-start.1
  58.5 7.8 %copy-start.4 = (f32[8,64,64]{2,1,0:T(8,128)S(1)}, f32[8,64,64]{2,1,0:T(8,128)}, u32[]{:S(2)}) copy-start(f32[8,64,64]{2,1,0:T(8,128)} %convolution_minimum_fusion.6) | copy-start | bytes 393220
  58.5 8.9 %copy-start.6 = (bf16[512,256]{1,0:T(8,128)(2,1)S(1)}, bf16[512,256]{1,0:T(8,128)(2,1)}, u32[]{:S(2)}) copy-start(bf16[512,256]{1,0:T(8,128)(2,1)} %get-tuple-element.8) | copy-start | bytes 786436
  58.5 36.7 %all-to-all-start.1 = ((bf16[64,66,256]{2,1,0:T(8,128)(2,1)}), bf16[64,66,256]{2,1,0:T(8,128)(2,1)}, u32[]{:S(2)}, u32[]{:S(2)}) async-start(bf16[64,66,256]{2,1,0:T(8,128)(2,1)} %shard_map.239), calls=%async_computation.1 | async-start | bytes 4718592 | tf_op jit(solution)/shard_map/all_to_all | solution.py:301
  66.3 118.0 %all-reduce.2.cloned.1.call-start = ((), (), s32[]{:S(2)}) async-start(), calls=%async_computation.5 | async-start | bytes 4194304 | tf_op jit(solution)/shard_map/psum | solution.py:323
  68.3 3.9 %copy-start.2 = (bf16[512,2048]{1,0:T(8,128)(2,1)S(1)}, bf16[512,2048]{1,0:T(8,128)(2,1)}, u32[]{:S(2)}) copy-start(bf16[512,2048]{1,0:T(8,128)(2,1)} %hid_ref.1) | copy-start | bytes 6291460
  68.3 4.0 %copy-start.11 = (f32[256]{0:T(256)S(1)}, f32[256]{0:T(256)}, u32[]{:S(2)}) copy-start(f32[256]{0:T(256)} %param.35) | copy-start | bytes 3076
  100.9 132.9 %reduce-scatter.2.cloned.1.call-start = ((), (), s32[]{:S(2)}) async-start(), calls=%async_computation.6 | async-start | bytes 2359296 | tf_op jit(solution)/shard_map/reduce_scatter | solution.py:336
  192.8 0.7 copy-start.10
  192.8 1.7 copy-start.3
  192.8 2.6 copy-start.12
  192.8 2.8 %copy-start.8 = (s32[8]{0:T(128)S(1)}, s32[8]{0:T(128)}, u32[]{:S(2)}) copy-start(s32[8]{0:T(128)} %get-tuple-element.17.where_ref) | copy-start | bytes 100
  196.0 37.7 %copy-start.5 = (bf16[512,256]{1,0:T(8,128)(2,1)S(1)}, bf16[512,256]{1,0:T(8,128)(2,1)}, u32[]{:S(2)}) copy-start(bf16[512,256]{1,0:T(8,128)(2,1)} %get-tuple-element.10) | copy-start | bytes 786436
  197.3 21.9 %all-to-all-start.3 = ((bf16[64,32,256]{2,1,0:T(8,128)(2,1)}), bf16[64,32,256]{2,1,0:T(8,128)(2,1)S(1)}, u32[]{:S(2)}, u32[]{:S(2)}) async-start(bf16[64,32,256]{2,1,0:T(8,128)(2,1)} %bitcast.32), calls=%async_computation.4 | async-start | bytes 2097152 | tf_op jit(solution)/shard_map/all_to_all | solution.py:291
  235.6 12.7 %all-to-all-start.2 = ((f32[8,2,512]{2,1,0:T(2,128)}), f32[8,2,512]{2,1,0:T(2,128)S(1)}, u32[]{:S(2)}, u32[]{:S(2)}) async-start(f32[8,2,512]{2,1,0:T(2,128)} %broadcast_in_dim.54), calls=%async_computation.3 | async-start | bytes 65536 | tf_op jit(solution)/shard_map/all_to_all | solution.py:345
Sparse Core Ops, SparseCore 0:
  101.0 83.2 all-reduce.1
  193.0 40.7 reduce-scatter.1
